TPU v7x, 32 devices: a whole 2x2x4 slice. The times are simulated.
32 devices in a mesh: grp: 2 (over y), ctx: 8 (over z, x), head: 2 (over core).
Axes of the slice: x: 2, y: 2, z: 4, core: 2. Of those that a mesh axis runs over, the one named last changes fastest.
Arguments:
- queries: bfloat16 [2, 1024, 4096], P('grp', ('ctx', 'head')), parts along dimension 0, may hold values from -5.5 to 5.5
- key_states: bfloat16 [2, 1024, 1024], P('grp', ('ctx', 'head')), parts along dimension 0, may hold values from -5.5 to 5.5
- value_states: bfloat16 [2, 1024, 1024], P('grp', ('ctx', 'head')), parts along dimension 0, may hold values from -6 to 6
Outputs:
- attended: bfloat16 [2, 1024, 4096], P('grp', ('ctx', 'head')), parts along dimension 0
There are 2 independent parts, one for each index of `grp`. A program takes and returns all parts, laid end to end along the dimension named above; each array names one. Nothing has to cross between parts.
All inputs are finite; a program needn't handle non-finite values.
Results may differ from a plain program's by a relative error of at most 0.004.
The roundings to bfloat16 on the way count: a program that leaves them out, or rounds other values in their place, can miss the bound.
Values may be sent and summed in bfloat16 or wider, within the bound.
No kernel may reach another device: no remote copies, remote signals or barrier semaphores. Data moves between devices by JAX's collectives and lax.ppermute only.
A program may use at most 64 MiB of HBM per device.

v0:
```python
import math

import jax
import jax.numpy as jnp
from jax import lax
from jax.sharding import PartitionSpec as P

DH = 128


def right_step(query_rows, key_heads, value_heads):
    seq_count, place_count, feature_width = query_rows.shape
    heads_kv = key_heads.shape[2]
    shaped = query_rows.reshape(seq_count, place_count, heads_kv, -1, DH)
    logits = jnp.einsum(
        "scjgd,sijd->sjgci", shaped, key_heads, preferred_element_type=jnp.float32
    ) / math.sqrt(DH)
    weights = jax.nn.softmax(logits, axis=-1)
    entropy = jax.nn.logsumexp(logits, axis=-1) - jnp.sum(weights * logits, axis=-1)
    rounded = weights.astype(jnp.bfloat16)
    key_mix = jnp.einsum(
        "sjgci,sijd->scjgd", rounded, key_heads, preferred_element_type=jnp.float32
    ).astype(jnp.bfloat16)
    entropy = jnp.transpose(entropy, (0, 3, 1, 2))
    value_mix = None
    if value_heads is not None:
        value_mix = jnp.einsum(
            "sjgci,sijd->scjgd", rounded, value_heads, preferred_element_type=jnp.float32
        ).astype(jnp.bfloat16)
        value_mix = value_mix.reshape(seq_count, place_count, feature_width)
    return key_mix.reshape(seq_count, place_count, feature_width), entropy, value_mix


def to_places(stacked, entropy, ctx):
    seq_count, place_count, kinds, feature_width = stacked.shape
    pairs = place_count * feature_width // DH
    chunk = pairs // ctx
    rows = jnp.moveaxis(stacked, 2, 1).reshape(seq_count, kinds, ctx, chunk, DH)
    rows = lax.all_to_all(rows, "ctx", split_axis=2, concat_axis=2, tiled=True)
    ent = entropy.reshape(seq_count, ctx, chunk)
    ent = lax.all_to_all(ent, "ctx", split_axis=1, concat_axis=1, tiled=True)
    return rows, ent


def to_blocks(grid, place_count, feature_width):
    seq_count = grid.shape[0]
    back = lax.all_to_all(grid, "ctx", split_axis=1, concat_axis=1, tiled=True)
    return back.reshape(seq_count, place_count, feature_width)


def left_step(query_grid, key_grid, entropy_grid):
    logits = jnp.einsum(
        "sapd,slpd->spal", query_grid, key_grid, preferred_element_type=jnp.float32
    ) / math.sqrt(DH)
    logits = logits + jnp.transpose(entropy_grid, (0, 2, 1))[:, :, None, :]
    weights = jax.nn.softmax(logits, axis=-1)
    return weights, weights.astype(jnp.bfloat16)


def make_local(ctx):
    def local(queries, key_states, value_states):
        seq_count, place_count, feature_width = queries.shape
        keys = lax.all_gather(key_states, "head", axis=1, tiled=True)
        values = lax.all_gather(value_states, "head", axis=1, tiled=True)
        block_len = keys.shape[1]
        heads_kv = keys.shape[2] // DH
        key_heads = keys.reshape(seq_count, block_len, heads_kv, DH)
        value_heads = values.reshape(seq_count, block_len, heads_kv, DH)

        key_mix, entropy, _ = right_step(queries, key_heads, None)
        stacked = jnp.stack([queries, key_mix], axis=2)
        rows, entropy_grid = to_places(stacked, entropy, ctx)
        query_grid, key_grid = rows[:, 0], rows[:, 1]

        weights, left_rounded = left_step(query_grid, key_grid, entropy_grid)
        column_mass = jnp.transpose(jnp.sum(weights, axis=2), (0, 2, 1))
        mixed = jnp.einsum(
            "spal,sapd->slpd", left_rounded, query_grid, preferred_element_type=jnp.float32
        )
        query_mix = (mixed / jnp.maximum(column_mass, 1.0)[..., None]).astype(jnp.bfloat16)
        returned = to_blocks(query_mix, place_count, feature_width)

        key_mix, entropy, value_mix = right_step(returned, key_heads, value_heads)
        stacked = jnp.stack([key_mix, value_mix], axis=2)
        rows, entropy_grid = to_places(stacked, entropy, ctx)
        key_grid, value_grid = rows[:, 0], rows[:, 1]

        _, final_left = left_step(query_grid, key_grid, entropy_grid)
        attended = jnp.einsum(
            "spal,slpd->sapd", final_left, value_grid, preferred_element_type=jnp.float32
        ).astype(jnp.bfloat16)
        return to_blocks(attended, place_count, feature_width)

    return local


def solution(mesh):
    placed = P("grp", ("ctx", "head"), None)
    return jax.shard_map(
        make_local(mesh.shape["ctx"]),
        mesh=mesh,
        in_specs=(placed, placed, placed),
        out_specs=placed,
        check_vma=False,
    )
```

profile of v0, /device:TPU:0, one launch (start us, length us, event | category | flops | bytes accessed | tf_op | source)
XLA Modules:
  0.0 138.6 jit_solution(735056587213074437)
XLA Ops:
  0.0 2.4 %all_gather.6 = bf16[1,128,1024]{2,1,0:T(8,128)(2,1)S(1)} all-gather(bf16[1,64,1024]{2,1,0:T(8,128)(2,1)} %param.4), channel_id=1, replica_groups=mesh['grp'=2,'ctx'=8,'head'=2] {'head'}, dimensions={1}, use_global_device_ids=true | all-gather | bytes 393216 | tf_op jit(solution)/shard_map/all_gather | solution.py:63
  2.4 0.2 copy.29
  2.6 0.4 reshape.249
  3.0 0.5 fusion.39
  3.5 0.7 fusion.15
  4.2 1.6 %exponential_reduce_fusion.1 = (f32[8,4,64]{2,1,0:T(4,128)S(1)}, f32[8,4,64]{2,1,0:T(4,128)S(1)}) fusion(f32[1,8,4,64,128]{4,3,2,1,0:T(8,128)S(1)} %get-tuple-element.14, f32[8,4,64]{2,1,0:T(4,128)S(1)} %is-finite_select_fusion.3, f32[8,4,64]{2,1,0:T(4,128)S(1)} %fusion.15, f32[8,4,64]{2,1,0:T(4,128)S(1)} %get-tuple-element.13), kind=kLoop, calls=%fused_computation.31 | loop fusion | flops 1568768 | bytes 1089536 | tf_op jit(solution)/shard_map/reduce_sum | solution.py:19
  5.8 0.2 copy.37
  6.0 0.8 reshape.268
  6.7 7.2 %all-to-all-start.1 = ((f32[1,8,256]{2,0,1:T(1,128)}), f32[1,8,256]{2,0,1:T(1,128)S(1)}, u32[]{:S(2)}, u32[]{:S(2)}) async-start(f32[1,8,256]{2,0,1:T(1,128)} %reshape.268), calls=%async_computation.1 | async-start | bytes 16384 | tf_op jit(solution)/shard_map/all_to_all | solution.py:41
  13.9 0.9 fusion.10
  14.8 0.4 copy.33
  15.3 0.4 stack_reshape.9
  15.8 0.5 reshape.251
  16.3 1.1 copy.34
  17.4 3.1 %all-to-all-done.1 = f32[1,8,256]{2,0,1:T(1,128)S(1)} async-done(((f32[1,8,256]{2,0,1:T(1,128)}), f32[1,8,256]{2,0,1:T(1,128)S(1)}, u32[]{:S(2)}, u32[]{:S(2)}) %all-to-all-start.1) | async-done | bytes 8224 | tf_op jit(solution)/shard_map/all_to_all | solution.py:41
  20.4 3.6 %all-to-all-start = ((bf16[1,2,8,256,128]{4,3,1,0,2:T(8,128)(2,1)}), bf16[1,2,8,256,128]{4,3,1,0,2:T(8,128)(2,1)S(1)}, u32[]{:S(2)}, u32[]{:S(2)}) async-start(bf16[1,2,8,256,128]{4,3,1,0,2:T(8,128)(2,1)} %copy.34), calls=%async_computation | async-start | bytes 2097152 | tf_op jit(solution)/shard_map/all_to_all | solution.py:39
  24.0 0.1 copy.66
  24.1 25.0 %all-to-all-done = bf16[1,2,8,256,128]{4,3,1,0,2:T(8,128)(2,1)S(1)} async-done(((bf16[1,2,8,256,128]{4,3,1,0,2:T(8,128)(2,1)}), bf16[1,2,8,256,128]{4,3,1,0,2:T(8,128)(2,1)S(1)}, u32[]{:S(2)}, u32[]{:S(2)}) %all-to-all-start) | async-done | bytes 1048608 | tf_op jit(solution)/shard_map/all_to_all | solution.py:39
  49.2 2.7 %fusion.40 = (f32[256,8]{1,0:T(8,128)S(1)}, f32[256,8,8]{1,2,0:T(8,128)S(1)}) fusion(bf16[1,1,8,256,128]{4,3,1,0,2:T(8,128)(2,1)S(1)} %get-tuple-element.12, f32[256,8]{1,0:T(8,128)S(1)} %bitcast.137, bf16[1,1,8,256,128]{4,3,1,0,2:T(8,128)(2,1)S(1)} %get-tuple-element.11), kind=kOutput, calls=%fused_computation.66 | convolution fusion | flops 4259847 | bytes 1130496 | tf_op jit(solution)/shard_map/sub | solution.py:56
  51.9 0.4 fusion.28
  52.3 0.6 divide_convert_fusion.1
  52.9 0.9 copy.40
  53.8 3.6 %all-to-all-start.2 = ((bf16[1,8,256,128]{3,2,0,1:T(8,128)(2,1)}), bf16[1,8,256,128]{3,2,0,1:T(8,128)(2,1)S(1)}, u32[]{:S(2)}, u32[]{:S(2)}) async-start(bf16[1,8,256,128]{3,2,0,1:T(8,128)(2,1)} %copy.40), calls=%async_computation.2 | async-start | bytes 1048576 | tf_op jit(solution)/shard_map/all_to_all | solution.py:47
  57.5 2.0 %all_gather.7 = bf16[1,128,1024]{2,1,0:T(8,128)(2,1)S(1)} all-gather(bf16[1,64,1024]{2,1,0:T(8,128)(2,1)S(1)} %copy-done.1), channel_id=1, replica_groups=mesh['grp'=2,'ctx'=8,'head'=2] {'head'}, dimensions={1}, use_global_device_ids=true | all-gather | bytes 393216 | tf_op jit(solution)/shard_map/all_gather | solution.py:64
  59.5 0.2 copy.45
  59.6 12.4 %all-to-all-done.2 = bf16[1,8,256,128]{3,2,0,1:T(8,128)(2,1)S(1)} async-done(((bf16[1,8,256,128]{3,2,0,1:T(8,128)(2,1)}), bf16[1,8,256,128]{3,2,0,1:T(8,128)(2,1)S(1)}, u32[]{:S(2)}, u32[]{:S(2)}) %all-to-all-start.2) | async-done | bytes 524320 | tf_op jit(solution)/shard_map/all_to_all | solution.py:47
  72.0 0.5 fusion.41
  72.5 0.7 fusion.17
  73.2 0.9 fusion.11
  74.1 1.6 %exponential_reduce_fusion = (f32[8,4,64]{2,1,0:T(4,128)S(1)}, f32[8,4,64]{2,1,0:T(4,128)S(1)}) fusion(f32[1,8,4,64,128]{4,3,2,1,0:T(8,128)S(1)} %get-tuple-element.18, f32[8,4,64]{2,1,0:T(4,128)S(1)} %is-finite_select_fusion.1, f32[8,4,64]{2,1,0:T(4,128)S(1)} %fusion.17, f32[8,4,64]{2,1,0:T(4,128)S(1)} %get-tuple-element.17), kind=kLoop, calls=%fused_computation.27 | loop fusion | flops 1568768 | bytes 1089536 | tf_op jit(solution)/shard_map/reduce_sum | solution.py:19
  75.8 0.2 copy.51
  75.9 0.8 reshape.269
  76.7 3.6 %all-to-all-start.4 = ((f32[1,8,256]{2,0,1:T(1,128)}), f32[1,8,256]{2,0,1:T(1,128)S(1)}, u32[]{:S(2)}, u32[]{:S(2)}) async-start(f32[1,8,256]{2,0,1:T(1,128)} %reshape.269), calls=%async_computation.4 | async-start | bytes 16384 | tf_op jit(solution)/shard_map/all_to_all | solution.py:41
  80.4 0.9 fusion.12
  81.3 0.4 copy.44
  81.7 0.4 stack_reshape.10
  82.1 0.4 copy.47
  82.5 0.4 stack_reshape.11
  83.0 0.5 reshape.258
  83.6 1.1 copy.48
  84.6 2.3 %all-to-all-done.4 = f32[1,8,256]{2,0,1:T(1,128)S(1)} async-done(((f32[1,8,256]{2,0,1:T(1,128)}), f32[1,8,256]{2,0,1:T(1,128)S(1)}, u32[]{:S(2)}, u32[]{:S(2)}) %all-to-all-start.4) | async-done | bytes 8224 | tf_op jit(solution)/shard_map/all_to_all | solution.py:41
  86.9 3.7 %all-to-all-start.3 = ((bf16[1,2,8,256,128]{4,3,1,0,2:T(8,128)(2,1)}), bf16[1,2,8,256,128]{4,3,1,0,2:T(8,128)(2,1)S(1)}, u32[]{:S(2)}, u32[]{:S(2)}) async-start(bf16[1,2,8,256,128]{4,3,1,0,2:T(8,128)(2,1)} %copy.48), calls=%async_computation.3 | async-start | bytes 2097152 | tf_op jit(solution)/shard_map/all_to_all | solution.py:39
  90.6 0.1 copy.73
  90.8 25.5 %all-to-all-done.3 = bf16[1,2,8,256,128]{4,3,1,0,2:T(8,128)(2,1)S(1)} async-done(((bf16[1,2,8,256,128]{4,3,1,0,2:T(8,128)(2,1)}), bf16[1,2,8,256,128]{4,3,1,0,2:T(8,128)(2,1)S(1)}, u32[]{:S(2)}, u32[]{:S(2)}) %all-to-all-start.3) | async-done | bytes 1048608 | tf_op jit(solution)/shard_map/all_to_all | solution.py:39
  116.3 2.7 %fusion.42 = (f32[256,8]{1,0:T(8,128)S(1)}, f32[256,8,8]{1,2,0:T(8,128)S(1)}) fusion(bf16[1,1,8,256,128]{4,3,1,0,2:T(8,128)(2,1)S(1)} %get-tuple-element.10, f32[256,8]{1,0:T(8,128)S(1)} %bitcast.138, bf16[1,1,8,256,128]{4,3,1,0,2:T(8,128)(2,1)S(1)} %get-tuple-element.11), kind=kOutput, calls=%fused_computation.68 | convolution fusion | flops 4259847 | bytes 1130496 | tf_op jit(solution)/shard_map/sub | solution.py:56
  119.0 0.6 fusion.13
  119.7 17.9 %all_to_all.30 = bf16[1,8,256,128]{3,2,0,1:T(8,128)(2,1)S(1)} all-to-all(bf16[1,8,256,128]{3,2,0,1:T(8,128)(2,1)S(1)} %copy.55), channel_id=1, replica_groups=mesh['grp'=2,'ctx'=8,'head'=2] {'ctx'}, dimensions={1} | all-to-all | bytes 1048576 | tf_op jit(solution)/shard_map/all_to_all | solution.py:47
  137.5 1.0 reshape.262
  (14 shorter events, 0.5 us)
Async XLA Ops:
  0.0 2.6 %copy-start = (bf16[1,64,4096]{2,1,0:T(8,128)(2,1)S(1)}, bf16[1,64,4096]{2,1,0:T(8,128)(2,1)}, u32[]{:S(2)}) copy-start(bf16[1,64,4096]{2,1,0:T(8,128)(2,1)} %param.3) | copy-start | bytes 1572868
  6.7 13.7 %all-to-all-start.1 = ((f32[1,8,256]{2,0,1:T(1,128)}), f32[1,8,256]{2,0,1:T(1,128)S(1)}, u32[]{:S(2)}, u32[]{:S(2)}) async-start(f32[1,8,256]{2,0,1:T(1,128)} %reshape.268), calls=%async_computation.1 | async-start | bytes 16384 | tf_op jit(solution)/shard_map/all_to_all | solution.py:41
  20.4 28.7 %all-to-all-start = ((bf16[1,2,8,256,128]{4,3,1,0,2:T(8,128)(2,1)}), bf16[1,2,8,256,128]{4,3,1,0,2:T(8,128)(2,1)S(1)}, u32[]{:S(2)}, u32[]{:S(2)}) async-start(bf16[1,2,8,256,128]{4,3,1,0,2:T(8,128)(2,1)} %copy.34), calls=%async_computation | async-start | bytes 2097152 | tf_op jit(solution)/shard_map/all_to_all | solution.py:39
  53.8 3.6 %copy-start.1 = (bf16[1,64,1024]{2,1,0:T(8,128)(2,1)S(1)}, bf16[1,64,1024]{2,1,0:T(8,128)(2,1)}, u32[]{:S(2)}) copy-start(bf16[1,64,1024]{2,1,0:T(8,128)(2,1)} %param.5) | copy-start | bytes 393220
  53.8 18.2 %all-to-all-start.2 = ((bf16[1,8,256,128]{3,2,0,1:T(8,128)(2,1)}), bf16[1,8,256,128]{3,2,0,1:T(8,128)(2,1)S(1)}, u32[]{:S(2)}, u32[]{:S(2)}) async-start(bf16[1,8,256,128]{3,2,0,1:T(8,128)(2,1)} %copy.40), calls=%async_computation.2 | async-start | bytes 1048576 | tf_op jit(solution)/shard_map/all_to_all | solution.py:47
  76.7 10.2 %all-to-all-start.4 = ((f32[1,8,256]{2,0,1:T(1,128)}), f32[1,8,256]{2,0,1:T(1,128)S(1)}, u32[]{:S(2)}, u32[]{:S(2)}) async-start(f32[1,8,256]{2,0,1:T(1,128)} %reshape.269), calls=%async_computation.4 | async-start | bytes 16384 | tf_op jit(solution)/shard_map/all_to_all | solution.py:41
  86.9 29.3 %all-to-all-start.3 = ((bf16[1,2,8,256,128]{4,3,1,0,2:T(8,128)(2,1)}), bf16[1,2,8,256,128]{4,3,1,0,2:T(8,128)(2,1)S(1)}, u32[]{:S(2)}, u32[]{:S(2)}) async-start(bf16[1,2,8,256,128]{4,3,1,0,2:T(8,128)(2,1)} %copy.48), calls=%async_computation.3 | async-start | bytes 2097152 | tf_op jit(solution)/shard_map/all_to_all | solution.py:39
where the time goes:
time: 139 us
  waiting for transfers between devices  68.1 us (49%)
  blocking collectives  22.3 us (16%)
  starting transfers between devices  21.7 us (16%)
  local copies, waits for them, and re-layouts  10.6 us (8%)
  matrix products  10.5 us (8%)
  other arithmetic  5.13 us (4%)
    all_to_all x2, waiting for transfers between devices, to_places(): rows = lax.all_to_all(rows, 'ctx', split_axis=2, concat_axis=2, tiled=True)  50.4 us
    all_to_all x1, blocking collectives, to_blocks(): back = lax.all_to_all(grid, 'ctx', split_axis=1, concat_axis=1, tiled=True)  17.9 us
    all_to_all x1, waiting for transfers between devices, to_blocks(): back = lax.all_to_all(grid, 'ctx', split_axis=1, concat_axis=1, tiled=True)  12.4 us
    all_to_all x2, starting transfers between devices, to_places(): ent = lax.all_to_all(ent, 'ctx', split_axis=1, concat_axis=1, tiled=True)  10.8 us
    all_to_all x2, starting transfers between devices, to_places(): rows = lax.all_to_all(rows, 'ctx', split_axis=2, concat_axis=2, tiled=True)  7.31 us
    sub x2, matrix products, left_step(): weights = jax.nn.softmax(logits, axis=-1)  5.46 us
    all_to_all x2, waiting for transfers between devices, to_places(): ent = lax.all_to_all(ent, 'ctx', split_axis=1, concat_axis=1, tiled=True)  5.31 us
    all_to_all x1, starting transfers between devices, to_blocks(): back = lax.all_to_all(grid, 'ctx', split_axis=1, concat_axis=1, tiled=True)  3.63 us
  transfers between devices with their start and end apart: 5, of which 5 were waited for; matrix products, arithmetic and copies ran while one was open for 6% of the time, Pallas kernels for 0%

commit v1 on v0

--- a/solution.py
+++ b/solution.py
@@ -31,21 +31,38 @@
     return key_mix.reshape(seq_count, place_count, feature_width), entropy, value_mix
 
 
-def to_places(stacked, entropy, ctx):
-    seq_count, place_count, kinds, feature_width = stacked.shape
-    pairs = place_count * feature_width // DH
-    chunk = pairs // ctx
-    rows = jnp.moveaxis(stacked, 2, 1).reshape(seq_count, kinds, ctx, chunk, DH)
-    rows = lax.all_to_all(rows, "ctx", split_axis=2, concat_axis=2, tiled=True)
-    ent = entropy.reshape(seq_count, ctx, chunk)
-    ent = lax.all_to_all(ent, "ctx", split_axis=1, concat_axis=1, tiled=True)
-    return rows, ent
+def entropy_rows(entropy, ctx):
+    seq_count = entropy.shape[0]
+    flat = entropy.reshape(seq_count, ctx, -1)
+    chunk = flat.shape[2]
+    high = lax.optimization_barrier(flat.astype(jnp.bfloat16))
+    rest = flat - high.astype(jnp.float32)
+    middle = lax.optimization_barrier(rest.astype(jnp.bfloat16))
+    low = (rest - middle.astype(jnp.float32)).astype(jnp.bfloat16)
+    terms = jnp.concatenate([high, middle, low], axis=2)
+    row_count = -(-3 * chunk // DH)
+    terms = jnp.pad(terms, ((0, 0), (0, 0), (0, row_count * DH - 3 * chunk)))
+    return terms.reshape(seq_count, ctx, row_count, DH)
+
+
+def entropy_from_rows(rows, chunk):
+    seq_count, ctx = rows.shape[:2]
+    terms = rows.reshape(seq_count, ctx, -1)[:, :, : 3 * chunk].astype(jnp.float32)
+    return (terms[:, :, :chunk] + terms[:, :, chunk : 2 * chunk]) + terms[:, :, 2 * chunk :]
+
+
+def pair_rows(rows, ctx):
+    seq_count = rows.shape[0]
+    return rows.reshape(seq_count, ctx, -1, DH)
+
+
+def exchange(grid):
+    return lax.all_to_all(grid, "ctx", split_axis=1, concat_axis=1, tiled=True)
 
 
 def to_blocks(grid, place_count, feature_width):
     seq_count = grid.shape[0]
-    back = lax.all_to_all(grid, "ctx", split_axis=1, concat_axis=1, tiled=True)
-    return back.reshape(seq_count, place_count, feature_width)
+    return exchange(grid).reshape(seq_count, place_count, feature_width)
 
 
 def left_step(query_grid, key_grid, entropy_grid):
@@ -68,9 +85,15 @@
         value_heads = values.reshape(seq_count, block_len, heads_kv, DH)
 
         key_mix, entropy, _ = right_step(queries, key_heads, None)
-        stacked = jnp.stack([queries, key_mix], axis=2)
-        rows, entropy_grid = to_places(stacked, entropy, ctx)
-        query_grid, key_grid = rows[:, 0], rows[:, 1]
+        query_rows = pair_rows(queries, ctx)
+        chunk = query_rows.shape[2]
+        rows = exchange(
+            jnp.concatenate(
+                [query_rows, pair_rows(key_mix, ctx), entropy_rows(entropy, ctx)], axis=2
+            )
+        )
+        query_grid, key_grid = rows[:, :, :chunk], rows[:, :, chunk : 2 * chunk]
+        entropy_grid = entropy_from_rows(rows[:, :, 2 * chunk :], chunk)
 
         weights, left_rounded = left_step(query_grid, key_grid, entropy_grid)
         column_mass = jnp.transpose(jnp.sum(weights, axis=2), (0, 2, 1))
@@ -81,9 +104,14 @@
         returned = to_blocks(query_mix, place_count, feature_width)
 
         key_mix, entropy, value_mix = right_step(returned, key_heads, value_heads)
-        stacked = jnp.stack([key_mix, value_mix], axis=2)
-        rows, entropy_grid = to_places(stacked, entropy, ctx)
-        key_grid, value_grid = rows[:, 0], rows[:, 1]
+        rows = exchange(
+            jnp.concatenate(
+                [pair_rows(key_mix, ctx), pair_rows(value_mix, ctx), entropy_rows(entropy, ctx)],
+                axis=2,
+            )
+        )
+        key_grid, value_grid = rows[:, :, :chunk], rows[:, :, chunk : 2 * chunk]
+        entropy_grid = entropy_from_rows(rows[:, :, 2 * chunk :], chunk)
 
         _, final_left = left_step(query_grid, key_grid, entropy_grid)
         attended = jnp.einsum(

time: 139 us -> 123 us (0.88)
  blocking collectives: 22.3 us -> 84.8 us
  waiting for transfers between devices: 68.1 us -> 11.6 us
  starting transfers between devices: 21.7 us -> 3.49 us
  local copies, waits for them, and re-layouts: 10.6 us -> 6.4 us
    all_to_all x1 -> x3, blocking collectives: 17.9 us -> 80.7 us  [exchange(): return lax.all_to_all(grid, 'ctx', split_axis=1, concat_axis=1, tiled=True)]
    all_to_all x5 -> x1, waiting for transfers between devices: 68.1 us -> 11.6 us  [exchange(): return lax.all_to_all(grid, 'ctx', split_axis=1, concat_axis=1, tiled=True)]
    all_to_all x5 -> x1, starting transfers between devices: 21.7 us -> 3.49 us  [exchange(): return lax.all_to_all(grid, 'ctx', split_axis=1, concat_axis=1, tiled=True)]
    reshape x7 -> x6, local copies, waits for them, and re-layouts: 5.75 us -> 1.6 us  [the longest x1 1.02 us: to_blocks(): return exchange(grid).reshape(seq_count, place_count, feature_width)]
  transfers between devices with their start and end apart: 5 -> 1, of which waited for: 5 -> 1; matrix products, arithmetic and copies ran while one was open for 6% -> 0% of each run, Pallas kernels for 0% -> 0%
where the time goes in v1:
time: 123 us; the launch traced here: 122 us
  blocking collectives  84.8 us (69%)
  waiting for transfers between devices  11.6 us (9%)
  matrix products  10.5 us (9%)
  local copies, waits for them, and re-layouts  6.4 us (5%)
  other arithmetic  5.17 us (4%)
  starting transfers between devices  3.49 us (3%)
    all_to_all x3, blocking collectives, exchange(): return lax.all_to_all(grid, 'ctx', split_axis=1, concat_axis=1, tiled=True)  80.7 us
    all_to_all x1, waiting for transfers between devices, exchange(): return lax.all_to_all(grid, 'ctx', split_axis=1, concat_axis=1, tiled=True)  11.6 us
    sub x2, matrix products, left_step(): weights = jax.nn.softmax(logits, axis=-1)  5.46 us
    all_to_all x1, starting transfers between devices, exchange(): return lax.all_to_all(grid, 'ctx', split_axis=1, concat_axis=1, tiled=True)  3.49 us
    reduce_sum x2, other arithmetic, right_step(): jax.nn.logsumexp(logits, axis=-1) - jnp.sum(weights * logits, axis=-1)  3.2 us
  transfers between devices with their start and end apart: 1, of which 1 were waited for; matrix products, arithmetic and copies ran while one was open for 0% of the time, Pallas kernels for 0%

profile of v1, /device:TPU:0, one launch (start us, length us, event | category | flops | bytes accessed | tf_op | source)
XLA Modules:
  0.0 122.3 jit_solution(6142364145627886975)
XLA Ops:
  0.0 0.0 copy-start
  0.0 0.0 copy-start.1
  0.0 1.5 %reshape.301 = bf16[64,8,4,128]{3,2,1,0:T(4,128)(2,1)S(1)} reshape(bf16[1,64,4096]{2,1,0:T(8,128)(2,1)} %param.3) | data formatting | bytes 1048576 | tf_op jit(solution)/shard_map/reshape.1
  1.5 0.0 copy-done
  1.5 0.2 reshape.299
  1.7 0.0 copy-done.1
  1.8 2.1 %all_gather.6 = bf16[1,128,1024]{2,1,0:T(8,128)(2,1)S(1)} all-gather(bf16[1,64,1024]{2,1,0:T(8,128)(2,1)S(1)} %copy-done.1), channel_id=1, replica_groups=mesh['grp'=2,'ctx'=8,'head'=2] {'head'}, dimensions={1}, use_global_device_ids=true | all-gather | bytes 393216 | tf_op jit(solution)/shard_map/all_gather | solution.py:80
  3.8 0.2 copy.58
  4.0 0.5 fusion.45
  4.5 0.7 fusion.15
  5.2 0.9 fusion.10
  6.2 1.6 %exponential_reduce_fusion.1 = (f32[8,4,64]{2,1,0:T(4,128)S(1)}, f32[8,4,64]{2,1,0:T(4,128)S(1)}) fusion(f32[1,8,4,64,128]{4,3,2,1,0:T(8,128)S(1)} %get-tuple-element.14, f32[8,4,64]{2,1,0:T(4,128)S(1)} %is-finite_select_fusion.3, f32[8,4,64]{2,1,0:T(4,128)S(1)} %fusion.15, f32[8,4,64]{2,1,0:T(4,128)S(1)} %get-tuple-element.13), kind=kLoop, calls=%fused_computation.31 | loop fusion | flops 1568768 | bytes 1089536 | tf_op jit(solution)/shard_map/reduce_sum | solution.py:19
  7.8 0.4 copy.62
  8.2 0.2 copy.63
  8.4 0.2 reshape.303
  8.6 0.1 maximum_bitcast_fusion
  8.7 34.2 %all_to_all.20 = bf16[1,8,518,128]{3,2,0,1:T(8,128)(2,1)S(1)} all-to-all(bf16[1,8,518,128]{3,2,0,1:T(8,128)(2,1)S(1)} %maximum_bitcast_fusion), channel_id=1, replica_groups=mesh['grp'=2,'ctx'=8,'head'=2] {'ctx'}, dimensions={1} | all-to-all | bytes 2121728 | tf_op jit(solution)/shard_map/all_to_all | solution.py:60
  42.9 0.1 copy.69
  43.0 0.1 fusion.44
  43.2 2.7 %fusion.46 = (f32[256,8]{1,0:T(8,128)S(1)}, f32[256,8,8]{1,2,0:T(8,128)S(1)}) fusion(bf16[1,8,256,128]{3,2,0,1:T(8,128)(2,1)S(1)} %get-tuple-element.12, f32[256,8]{1,0:T(8,128)S(1)} %copy.69, bf16[1,8,256,128]{3,2,0,1:T(8,128)(2,1)S(1)} %get-tuple-element.11), kind=kOutput, calls=%fused_computation.84 | convolution fusion | flops 4259847 | bytes 1130496 | tf_op jit(solution)/shard_map/sub | solution.py:73
  45.9 0.4 fusion.28
  46.3 0.6 divide_convert_fusion.1
  46.9 0.0 copy-start.2
  46.9 0.9 copy.70
  47.8 3.5 %all-to-all-start.1 = ((bf16[1,8,256,128]{3,2,0,1:T(8,128)(2,1)}), bf16[1,8,256,128]{3,2,0,1:T(8,128)(2,1)S(1)}, u32[]{:S(2)}, u32[]{:S(2)}) async-start(bf16[1,8,256,128]{3,2,0,1:T(8,128)(2,1)} %copy.70), calls=%async_computation.1 | async-start | bytes 1048576 | tf_op jit(solution)/shard_map/all_to_all | solution.py:60
  51.3 0.0 copy-done.2
  51.3 2.0 %all_gather.7 = bf16[1,128,1024]{2,1,0:T(8,128)(2,1)S(1)} all-gather(bf16[1,64,1024]{2,1,0:T(8,128)(2,1)S(1)} %copy-done.2), channel_id=1, replica_groups=mesh['grp'=2,'ctx'=8,'head'=2] {'head'}, dimensions={1}, use_global_device_ids=true | all-gather | bytes 393216 | tf_op jit(solution)/shard_map/all_gather | solution.py:81
  53.3 0.2 copy.75
  53.5 11.6 %all-to-all-done.1 = bf16[1,8,256,128]{3,2,0,1:T(8,128)(2,1)S(1)} async-done(((bf16[1,8,256,128]{3,2,0,1:T(8,128)(2,1)}), bf16[1,8,256,128]{3,2,0,1:T(8,128)(2,1)S(1)}, u32[]{:S(2)}, u32[]{:S(2)}) %all-to-all-start.1) | async-done | bytes 524320 | tf_op jit(solution)/shard_map/all_to_all | solution.py:60
  65.1 0.5 fusion.47
  65.6 0.7 fusion.17
  66.3 0.9 fusion.11
  67.2 1.6 %exponential_reduce_fusion = (f32[8,4,64]{2,1,0:T(4,128)S(1)}, f32[8,4,64]{2,1,0:T(4,128)S(1)}) fusion(f32[1,8,4,64,128]{4,3,2,1,0:T(8,128)S(1)} %get-tuple-element.18, f32[8,4,64]{2,1,0:T(4,128)S(1)} %is-finite_select_fusion.1, f32[8,4,64]{2,1,0:T(4,128)S(1)} %fusion.17, f32[8,4,64]{2,1,0:T(4,128)S(1)} %get-tuple-element.17), kind=kLoop, calls=%fused_computation.27 | loop fusion | flops 1568768 | bytes 1089536 | tf_op jit(solution)/shard_map/reduce_sum | solution.py:19
  68.9 0.2 copy.78
  69.0 0.2 reshape.310
  69.3 1.0 fusion.12
  70.2 0.4 copy.74
  70.6 0.4 copy.77
  71.1 0.1 maximum_bitcast_fusion.1
  71.1 29.9 %all_to_all.21 = bf16[1,8,518,128]{3,2,0,1:T(8,128)(2,1)S(1)} all-to-all(bf16[1,8,518,128]{3,2,0,1:T(8,128)(2,1)S(1)} %maximum_bitcast_fusion.1), channel_id=1, replica_groups=mesh['grp'=2,'ctx'=8,'head'=2] {'ctx'}, dimensions={1} | all-to-all | bytes 2121728 | tf_op jit(solution)/shard_map/all_to_all | solution.py:60
  101.1 0.1 copy.84
  101.2 0.1 fusion.43
  101.4 2.7 %fusion.48 = (f32[256,8]{1,0:T(8,128)S(1)}, f32[256,8,8]{1,2,0:T(8,128)S(1)}) fusion(bf16[1,8,256,128]{3,2,0,1:T(8,128)(2,1)S(1)} %get-tuple-element.10, f32[256,8]{1,0:T(8,128)S(1)} %copy.84, bf16[1,8,256,128]{3,2,0,1:T(8,128)(2,1)S(1)} %get-tuple-element.11), kind=kOutput, calls=%fused_computation.86 | convolution fusion | flops 4259847 | bytes 1130496 | tf_op jit(solution)/shard_map/sub | solution.py:73
  104.1 0.6 fusion.13
  104.7 0.1 copy.86
  104.7 16.6 %all_to_all.22 = bf16[1,8,256,128]{3,2,0,1:T(8,128)(2,1)S(1)} all-to-all(bf16[1,8,256,128]{3,2,0,1:T(8,128)(2,1)S(1)} %copy.86), channel_id=1, replica_groups=mesh['grp'=2,'ctx'=8,'head'=2] {'ctx'}, dimensions={1} | all-to-all | bytes 1048576 | tf_op jit(solution)/shard_map/all_to_all | solution.py:60
  121.3 1.0 reshape.314
  (21 shorter events, 0.1 us)
Async XLA Ops:
  0.0 1.5 %copy-start = (bf16[1,64,4096]{2,1,0:T(8,128)(2,1)S(1)}, bf16[1,64,4096]{2,1,0:T(8,128)(2,1)}, u32[]{:S(2)}) copy-start(bf16[1,64,4096]{2,1,0:T(8,128)(2,1)} %param.3) | copy-start | bytes 1572868
  0.0 1.7 %copy-start.1 = (bf16[1,64,1024]{2,1,0:T(8,128)(2,1)S(1)}, bf16[1,64,1024]{2,1,0:T(8,128)(2,1)}, u32[]{:S(2)}) copy-start(bf16[1,64,1024]{2,1,0:T(8,128)(2,1)} %param.4) | copy-start | bytes 393220
  46.9 4.4 %copy-start.2 = (bf16[1,64,1024]{2,1,0:T(8,128)(2,1)S(1)}, bf16[1,64,1024]{2,1,0:T(8,128)(2,1)}, u32[]{:S(2)}) copy-start(bf16[1,64,1024]{2,1,0:T(8,128)(2,1)} %param.5) | copy-start | bytes 393220
  47.8 17.3 %all-to-all-start.1 = ((bf16[1,8,256,128]{3,2,0,1:T(8,128)(2,1)}), bf16[1,8,256,128]{3,2,0,1:T(8,128)(2,1)S(1)}, u32[]{:S(2)}, u32[]{:S(2)}) async-start(bf16[1,8,256,128]{3,2,0,1:T(8,128)(2,1)} %copy.70), calls=%async_computation.1 | async-start | bytes 1048576 | tf_op jit(solution)/shard_map/all_to_all | solution.py:60

commit v2 on v1

--- a/solution.py
+++ b/solution.py
@@ -74,58 +74,66 @@
     return weights, weights.astype(jnp.bfloat16)
 
 
-def make_local(ctx):
+def make_local(ctx, streams):
     def local(queries, key_states, value_states):
-        seq_count, place_count, feature_width = queries.shape
+        seq_count = queries.shape[0]
         keys = lax.all_gather(key_states, "head", axis=1, tiled=True)
         values = lax.all_gather(value_states, "head", axis=1, tiled=True)
         block_len = keys.shape[1]
         heads_kv = keys.shape[2] // DH
         key_heads = keys.reshape(seq_count, block_len, heads_kv, DH)
         value_heads = values.reshape(seq_count, block_len, heads_kv, DH)
-
-        key_mix, entropy, _ = right_step(queries, key_heads, None)
-        query_rows = pair_rows(queries, ctx)
-        chunk = query_rows.shape[2]
-        rows = exchange(
-            jnp.concatenate(
-                [query_rows, pair_rows(key_mix, ctx), entropy_rows(entropy, ctx)], axis=2
-            )
+        parts = jnp.split(queries, streams, axis=1)
+        return jnp.concatenate(
+            [pipeline(part, key_heads, value_heads, ctx) for part in parts], axis=1
         )
-        query_grid, key_grid = rows[:, :, :chunk], rows[:, :, chunk : 2 * chunk]
-        entropy_grid = entropy_from_rows(rows[:, :, 2 * chunk :], chunk)
-
-        weights, left_rounded = left_step(query_grid, key_grid, entropy_grid)
-        column_mass = jnp.transpose(jnp.sum(weights, axis=2), (0, 2, 1))
-        mixed = jnp.einsum(
-            "spal,sapd->slpd", left_rounded, query_grid, preferred_element_type=jnp.float32
-        )
-        query_mix = (mixed / jnp.maximum(column_mass, 1.0)[..., None]).astype(jnp.bfloat16)
-        returned = to_blocks(query_mix, place_count, feature_width)
-
-        key_mix, entropy, value_mix = right_step(returned, key_heads, value_heads)
-        rows = exchange(
-            jnp.concatenate(
-                [pair_rows(key_mix, ctx), pair_rows(value_mix, ctx), entropy_rows(entropy, ctx)],
-                axis=2,
-            )
-        )
-        key_grid, value_grid = rows[:, :, :chunk], rows[:, :, chunk : 2 * chunk]
-        entropy_grid = entropy_from_rows(rows[:, :, 2 * chunk :], chunk)
-
-        _, final_left = left_step(query_grid, key_grid, entropy_grid)
-        attended = jnp.einsum(
-            "spal,slpd->sapd", final_left, value_grid, preferred_element_type=jnp.float32
-        ).astype(jnp.bfloat16)
-        return to_blocks(attended, place_count, feature_width)
 
     return local
+
+
+def pipeline(queries, key_heads, value_heads, ctx):
+    seq_count, place_count, feature_width = queries.shape
+
+    key_mix, entropy, _ = right_step(queries, key_heads, None)
+    query_rows = pair_rows(queries, ctx)
+    chunk = query_rows.shape[2]
+    rows = exchange(
+        jnp.concatenate(
+            [query_rows, pair_rows(key_mix, ctx), entropy_rows(entropy, ctx)], axis=2
+        )
+    )
+    query_grid, key_grid = rows[:, :, :chunk], rows[:, :, chunk : 2 * chunk]
+    entropy_grid = entropy_from_rows(rows[:, :, 2 * chunk :], chunk)
+
+    weights, left_rounded = left_step(query_grid, key_grid, entropy_grid)
+    column_mass = jnp.transpose(jnp.sum(weights, axis=2), (0, 2, 1))
+    mixed = jnp.einsum(
+        "spal,sapd->slpd", left_rounded, query_grid, preferred_element_type=jnp.float32
+    )
+    query_mix = (mixed / jnp.maximum(column_mass, 1.0)[..., None]).astype(jnp.bfloat16)
+    returned = to_blocks(query_mix, place_count, feature_width)
+
+    key_mix, entropy, value_mix = right_step(returned, key_heads, value_heads)
+    rows = exchange(
+        jnp.concatenate(
+            [pair_rows(key_mix, ctx), pair_rows(value_mix, ctx), entropy_rows(entropy, ctx)],
+            axis=2,
+        )
+    )
+    key_grid, value_grid = rows[:, :, :chunk], rows[:, :, chunk : 2 * chunk]
+    entropy_grid = entropy_from_rows(rows[:, :, 2 * chunk :], chunk)
+
+    _, final_left = left_step(query_grid, key_grid, entropy_grid)
+    attended = jnp.einsum(
+        "spal,slpd->sapd", final_left, value_grid, preferred_element_type=jnp.float32
+    ).astype(jnp.bfloat16)
+    return to_blocks(attended, place_count, feature_width)
 
 
 def solution(mesh):
     placed = P("grp", ("ctx", "head"), None)
     return jax.shard_map(
-        make_local(mesh.shape["ctx"]),
+        make_local(mesh.shape["ctx"], 2),
         mesh=mesh,
         in_specs=(placed, placed, placed),
         out_specs=placed,

time: 123 us -> 136 us (1.11)
  blocking collectives: 84.8 us -> 4.07 us
  waiting for transfers between devices: 11.6 us -> 72.1 us
  starting transfers between devices: 3.49 us -> 32.6 us
  other arithmetic: 5.17 us -> 9.77 us
  matrix products: 10.5 us -> 8.15 us
  local copies, waits for them, and re-layouts: 6.4 us -> 8.29 us
    all_to_all x3 -> x0, blocking collectives: 80.7 us -> none  [exchange(): return lax.all_to_all(grid, 'ctx', split_axis=1, concat_axis=1, tiled=True)]
    all_to_all x1 -> x8, waiting for transfers between devices: 11.6 us -> 72.1 us  [exchange(): return lax.all_to_all(grid, 'ctx', split_axis=1, concat_axis=1, tiled=True)]
    all_to_all x1 -> x8, starting transfers between devices: 3.49 us -> 32.6 us  [exchange(): return lax.all_to_all(grid, 'ctx', split_axis=1, concat_axis=1, tiled=True)]
    concatenate x2 -> x5, other arithmetic: 0.15 us -> 4.18 us  [the longest x2 1.68 us: pipeline(): jnp.concatenate([query_rows, pair_rows(key_mix, ctx), entropy_rows(entrop...]
    sub x2 -> x4, matrix products: 5.46 us -> 2.55 us  [left_step(): weights = jax.nn.softmax(logits, axis=-1)]
    convert_element_type x2 -> x4, local copies, waits for them, and re-layouts: 0.95 us -> 2.97 us  [the longest x2 1.48 us: pipeline(): (mixed / jnp.maximum(column_mass, 1.0)[..., None]).astype(jnp.bfloat16)]
    reduce_sum x2 -> x4, other arithmetic: 3.2 us -> 3.28 us  [right_step(): jax.nn.logsumexp(logits, axis=-1) - jnp.sum(weights * logits, axis=-1)]
  transfers between devices with their start and end apart: 1 -> 8, of which waited for: 1 -> 8; matrix products, arithmetic and copies ran while one was open for 0% -> 15% of each run, Pallas kernels for 0% -> 0%
where the time goes in v2:
time: 136 us
  waiting for transfers between devices  72.1 us (53%)
  starting transfers between devices  32.6 us (24%)
  other arithmetic  9.77 us (7%)
  local copies, waits for them, and re-layouts  8.29 us (6%)
  matrix products  8.15 us (6%)
  blocking collectives  4.07 us (3%)
    all_to_all x8, waiting for transfers between devices, exchange(): return lax.all_to_all(grid, 'ctx', split_axis=1, concat_axis=1, tiled=True)  72.1 us
    all_to_all x8, starting transfers between devices, exchange(): return lax.all_to_all(grid, 'ctx', split_axis=1, concat_axis=1, tiled=True)  32.6 us
    reduce_sum x4, other arithmetic, right_step(): jax.nn.logsumexp(logits, axis=-1) - jnp.sum(weights * logits, axis=-1)  3.28 us
  transfers between devices with their start and end apart: 8, of which 8 were waited for; matrix products, arithmetic and copies ran while one was open for 15% of the time, Pallas kernels for 0%

profile of v2, /device:TPU:0, one launch (start us, length us, event | category | flops | bytes accessed | tf_op | source)
XLA Modules:
  0.0 135.5 jit_solution(7358728105405410628)
XLA Ops:
  0.0 1.1 fusion.96
  1.4 0.6 copy-done
  2.0 2.1 %all_gather.6 = bf16[1,128,1024]{2,1,0:T(8,128)(2,1)S(1)} all-gather(bf16[1,64,1024]{2,1,0:T(8,128)(2,1)S(1)} %copy-done), channel_id=1, replica_groups=mesh['grp'=2,'ctx'=8,'head'=2] {'head'}, dimensions={1}, use_global_device_ids=true | all-gather | bytes 393216 | tf_op jit(solution)/shard_map/all_gather | solution.py:80
  4.2 0.4 fusion.100
  4.6 0.4 fusion.37
  5.0 0.5 fusion.24
  5.5 0.8 exponential_reduce_fusion.1
  6.8 0.8 maximum_bitcast_fusion.2
  7.6 7.2 %all-to-all-start.4 = ((bf16[1,8,259,128]{3,2,0,1:T(8,128)(2,1)}), bf16[1,8,259,128]{3,2,0,1:T(8,128)(2,1)S(1)}, u32[]{:S(2)}, u32[]{:S(2)}) async-start(bf16[1,8,259,128]{3,2,0,1:T(8,128)(2,1)} %maximum_bitcast_fusion.2), calls=%async_computation.4 | async-start | bytes 1081344 | tf_op jit(solution)/shard_map/all_to_all | solution.py:60
  15.5 0.4 fusion.33
  15.9 0.8 exponential_reduce_fusion.3
  16.8 2.0 %all_gather.7 = bf16[1,128,1024]{2,1,0:T(8,128)(2,1)S(1)} all-gather(bf16[1,64,1024]{2,1,0:T(8,128)(2,1)S(1)} %copy-done.1), channel_id=1, replica_groups=mesh['grp'=2,'ctx'=8,'head'=2] {'head'}, dimensions={1}, use_global_device_ids=true | all-gather | bytes 393216 | tf_op jit(solution)/shard_map/all_gather | solution.py:81
  19.3 0.5 fusion.20
  19.9 0.8 maximum_bitcast_fusion
  20.7 9.2 %all-to-all-done.4 = bf16[1,8,259,128]{3,2,0,1:T(8,128)(2,1)S(1)} async-done(((bf16[1,8,259,128]{3,2,0,1:T(8,128)(2,1)}), bf16[1,8,259,128]{3,2,0,1:T(8,128)(2,1)S(1)}, u32[]{:S(2)}, u32[]{:S(2)}) %all-to-all-start.4) | async-done | bytes 530464 | tf_op jit(solution)/shard_map/all_to_all | solution.py:60
  29.9 3.6 %all-to-all-start = ((bf16[1,8,259,128]{3,2,0,1:T(8,128)(2,1)}), bf16[1,8,259,128]{3,2,0,1:T(8,128)(2,1)S(1)}, u32[]{:S(2)}, u32[]{:S(2)}) async-start(bf16[1,8,259,128]{3,2,0,1:T(8,128)(2,1)} %maximum_bitcast_fusion), calls=%async_computation | async-start | bytes 1081344 | tf_op jit(solution)/shard_map/all_to_all | solution.py:60
  33.8 0.6 fusion.101
  35.0 0.7 copy.146
  35.8 12.8 %all-to-all-done = bf16[1,8,259,128]{3,2,0,1:T(8,128)(2,1)S(1)} async-done(((bf16[1,8,259,128]{3,2,0,1:T(8,128)(2,1)}), bf16[1,8,259,128]{3,2,0,1:T(8,128)(2,1)S(1)}, u32[]{:S(2)}, u32[]{:S(2)}) %all-to-all-start) | async-done | bytes 530464 | tf_op jit(solution)/shard_map/all_to_all | solution.py:60
  48.6 3.6 %all-to-all-start.5 = ((bf16[1,8,128,128]{3,2,0,1:T(8,128)(2,1)}), bf16[1,8,128,128]{3,2,0,1:T(8,128)(2,1)S(1)}, u32[]{:S(2)}, u32[]{:S(2)}) async-start(bf16[1,8,128,128]{3,2,0,1:T(8,128)(2,1)} %copy.146), calls=%async_computation.5 | async-start | bytes 524288 | tf_op jit(solution)/shard_map/all_to_all | solution.py:60
  52.4 0.6 fusion.98
  53.7 0.7 copy.118
  54.4 6.9 %all-to-all-done.5 = bf16[1,8,128,128]{3,2,0,1:T(8,128)(2,1)S(1)} async-done(((bf16[1,8,128,128]{3,2,0,1:T(8,128)(2,1)}), bf16[1,8,128,128]{3,2,0,1:T(8,128)(2,1)S(1)}, u32[]{:S(2)}, u32[]{:S(2)}) %all-to-all-start.5) | async-done | bytes 262176 | tf_op jit(solution)/shard_map/all_to_all | solution.py:60
  61.3 3.6 %all-to-all-start.1 = ((bf16[1,8,128,128]{3,2,0,1:T(8,128)(2,1)}), bf16[1,8,128,128]{3,2,0,1:T(8,128)(2,1)S(1)}, u32[]{:S(2)}, u32[]{:S(2)}) async-start(bf16[1,8,128,128]{3,2,0,1:T(8,128)(2,1)} %copy.118), calls=%async_computation.1 | async-start | bytes 524288 | tf_op jit(solution)/shard_map/all_to_all | solution.py:60
  65.3 0.4 fusion.39
  65.7 0.8 exponential_reduce_fusion
  66.9 0.5 fusion.26
  67.5 0.5 fusion.25
  68.1 0.8 maximum_bitcast_fusion.3
  68.9 4.6 %all-to-all-done.1 = bf16[1,8,128,128]{3,2,0,1:T(8,128)(2,1)S(1)} async-done(((bf16[1,8,128,128]{3,2,0,1:T(8,128)(2,1)}), bf16[1,8,128,128]{3,2,0,1:T(8,128)(2,1)S(1)}, u32[]{:S(2)}, u32[]{:S(2)}) %all-to-all-start.1) | async-done | bytes 262176 | tf_op jit(solution)/shard_map/all_to_all | solution.py:60
  73.5 3.7 %all-to-all-start.6 = ((bf16[1,8,259,128]{3,2,0,1:T(8,128)(2,1)}), bf16[1,8,259,128]{3,2,0,1:T(8,128)(2,1)S(1)}, u32[]{:S(2)}, u32[]{:S(2)}) async-start(bf16[1,8,259,128]{3,2,0,1:T(8,128)(2,1)} %maximum_bitcast_fusion.3), calls=%async_computation.6 | async-start | bytes 1081344 | tf_op jit(solution)/shard_map/all_to_all | solution.py:60
  77.6 0.4 fusion.35
  78.0 0.8 exponential_reduce_fusion.2
  79.2 0.5 fusion.22
  79.8 0.5 fusion.21
  80.4 0.8 maximum_bitcast_fusion.1
  81.2 10.2 %all-to-all-done.6 = bf16[1,8,259,128]{3,2,0,1:T(8,128)(2,1)S(1)} async-done(((bf16[1,8,259,128]{3,2,0,1:T(8,128)(2,1)}), bf16[1,8,259,128]{3,2,0,1:T(8,128)(2,1)S(1)}, u32[]{:S(2)}, u32[]{:S(2)}) %all-to-all-start.6) | async-done | bytes 530464 | tf_op jit(solution)/shard_map/all_to_all | solution.py:60
  91.5 3.6 %all-to-all-start.2 = ((bf16[1,8,259,128]{3,2,0,1:T(8,128)(2,1)}), bf16[1,8,259,128]{3,2,0,1:T(8,128)(2,1)S(1)}, u32[]{:S(2)}, u32[]{:S(2)}) async-start(bf16[1,8,259,128]{3,2,0,1:T(8,128)(2,1)} %maximum_bitcast_fusion.1), calls=%async_computation.2 | async-start | bytes 1081344 | tf_op jit(solution)/shard_map/all_to_all | solution.py:60
  95.3 0.6 fusion.103
  96.3 0.7 copy.161
  97.1 12.7 %all-to-all-done.2 = bf16[1,8,259,128]{3,2,0,1:T(8,128)(2,1)S(1)} async-done(((bf16[1,8,259,128]{3,2,0,1:T(8,128)(2,1)}), bf16[1,8,259,128]{3,2,0,1:T(8,128)(2,1)S(1)}, u32[]{:S(2)}, u32[]{:S(2)}) %all-to-all-start.2) | async-done | bytes 530464 | tf_op jit(solution)/shard_map/all_to_all | solution.py:60
  109.8 3.6 %all-to-all-start.7 = ((bf16[1,8,128,128]{3,2,0,1:T(8,128)(2,1)}), bf16[1,8,128,128]{3,2,0,1:T(8,128)(2,1)S(1)}, u32[]{:S(2)}, u32[]{:S(2)}) async-start(bf16[1,8,128,128]{3,2,0,1:T(8,128)(2,1)} %copy.161), calls=%async_computation.7 | async-start | bytes 524288 | tf_op jit(solution)/shard_map/all_to_all | solution.py:60
  113.6 0.6 fusion.104
  114.6 0.7 copy.134
  115.3 7.1 %all-to-all-done.7 = bf16[1,8,128,128]{3,2,0,1:T(8,128)(2,1)S(1)} async-done(((bf16[1,8,128,128]{3,2,0,1:T(8,128)(2,1)}), bf16[1,8,128,128]{3,2,0,1:T(8,128)(2,1)S(1)}, u32[]{:S(2)}, u32[]{:S(2)}) %all-to-all-start.7) | async-done | bytes 262176 | tf_op jit(solution)/shard_map/all_to_all | solution.py:60
  122.4 3.6 %all-to-all-start.3 = ((bf16[1,8,128,128]{3,2,0,1:T(8,128)(2,1)}), bf16[1,8,128,128]{3,2,0,1:T(8,128)(2,1)S(1)}, u32[]{:S(2)}, u32[]{:S(2)}) async-start(bf16[1,8,128,128]{3,2,0,1:T(8,128)(2,1)} %copy.134), calls=%async_computation.3 | async-start | bytes 524288 | tf_op jit(solution)/shard_map/all_to_all | solution.py:60
  126.1 8.4 %all-to-all-done.3 = bf16[1,8,128,128]{3,2,0,1:T(8,128)(2,1)S(1)} async-done(((bf16[1,8,128,128]{3,2,0,1:T(8,128)(2,1)}), bf16[1,8,128,128]{3,2,0,1:T(8,128)(2,1)S(1)}, u32[]{:S(2)}, u32[]{:S(2)}) %all-to-all-start.3) | async-done | bytes 262176 | tf_op jit(solution)/shard_map/all_to_all | solution.py:60
  134.7 0.8 pad_maximum_fusion
  (84 shorter events, 6.9 us)
Async XLA Ops:
  1.1 0.9 copy-start
  7.6 22.3 %all-to-all-start.4 = ((bf16[1,8,259,128]{3,2,0,1:T(8,128)(2,1)}), bf16[1,8,259,128]{3,2,0,1:T(8,128)(2,1)S(1)}, u32[]{:S(2)}, u32[]{:S(2)}) async-start(bf16[1,8,259,128]{3,2,0,1:T(8,128)(2,1)} %maximum_bitcast_fusion.2), calls=%async_computation.4 | async-start | bytes 1081344 | tf_op jit(solution)/shard_map/all_to_all | solution.py:60
  15.5 1.3 copy-start.1
  29.9 18.7 %all-to-all-start = ((bf16[1,8,259,128]{3,2,0,1:T(8,128)(2,1)}), bf16[1,8,259,128]{3,2,0,1:T(8,128)(2,1)S(1)}, u32[]{:S(2)}, u32[]{:S(2)}) async-start(bf16[1,8,259,128]{3,2,0,1:T(8,128)(2,1)} %maximum_bitcast_fusion), calls=%async_computation | async-start | bytes 1081344 | tf_op jit(solution)/shard_map/all_to_all | solution.py:60
  48.6 12.7 %all-to-all-start.5 = ((bf16[1,8,128,128]{3,2,0,1:T(8,128)(2,1)}), bf16[1,8,128,128]{3,2,0,1:T(8,128)(2,1)S(1)}, u32[]{:S(2)}, u32[]{:S(2)}) async-start(bf16[1,8,128,128]{3,2,0,1:T(8,128)(2,1)} %copy.146), calls=%async_computation.5 | async-start | bytes 524288 | tf_op jit(solution)/shard_map/all_to_all | solution.py:60
  61.3 12.2 %all-to-all-start.1 = ((bf16[1,8,128,128]{3,2,0,1:T(8,128)(2,1)}), bf16[1,8,128,128]{3,2,0,1:T(8,128)(2,1)S(1)}, u32[]{:S(2)}, u32[]{:S(2)}) async-start(bf16[1,8,128,128]{3,2,0,1:T(8,128)(2,1)} %copy.118), calls=%async_computation.1 | async-start | bytes 524288 | tf_op jit(solution)/shard_map/all_to_all | solution.py:60
  73.5 18.0 %all-to-all-start.6 = ((bf16[1,8,259,128]{3,2,0,1:T(8,128)(2,1)}), bf16[1,8,259,128]{3,2,0,1:T(8,128)(2,1)S(1)}, u32[]{:S(2)}, u32[]{:S(2)}) async-start(bf16[1,8,259,128]{3,2,0,1:T(8,128)(2,1)} %maximum_bitcast_fusion.3), calls=%async_computation.6 | async-start | bytes 1081344 | tf_op jit(solution)/shard_map/all_to_all | solution.py:60
  91.5 18.3 %all-to-all-start.2 = ((bf16[1,8,259,128]{3,2,0,1:T(8,128)(2,1)}), bf16[1,8,259,128]{3,2,0,1:T(8,128)(2,1)S(1)}, u32[]{:S(2)}, u32[]{:S(2)}) async-start(bf16[1,8,259,128]{3,2,0,1:T(8,128)(2,1)} %maximum_bitcast_fusion.1), calls=%async_computation.2 | async-start | bytes 1081344 | tf_op jit(solution)/shard_map/all_to_all | solution.py:60
  109.8 12.6 %all-to-all-start.7 = ((bf16[1,8,128,128]{3,2,0,1:T(8,128)(2,1)}), bf16[1,8,128,128]{3,2,0,1:T(8,128)(2,1)S(1)}, u32[]{:S(2)}, u32[]{:S(2)}) async-start(bf16[1,8,128,128]{3,2,0,1:T(8,128)(2,1)} %copy.161), calls=%async_computation.7 | async-start | bytes 524288 | tf_op jit(solution)/shard_map/all_to_all | solution.py:60
  122.4 12.2 %all-to-all-start.3 = ((bf16[1,8,128,128]{3,2,0,1:T(8,128)(2,1)}), bf16[1,8,128,128]{3,2,0,1:T(8,128)(2,1)S(1)}, u32[]{:S(2)}, u32[]{:S(2)}) async-start(bf16[1,8,128,128]{3,2,0,1:T(8,128)(2,1)} %copy.134), calls=%async_computation.3 | async-start | bytes 524288 | tf_op jit(solution)/shard_map/all_to_all | solution.py:60

commit v3 on v1

--- a/solution.py
+++ b/solution.py
@@ -3,32 +3,68 @@
 import jax
 import jax.numpy as jnp
 from jax import lax
+from jax.experimental import pallas as pl
 from jax.sharding import PartitionSpec as P
 
 DH = 128
 
 
-def right_step(query_rows, key_heads, value_heads):
+def right_kernel(query_ref, key_ref, *refs):
+    with_values = len(refs) == 4
+    if with_values:
+        value_ref, key_mix_ref, entropy_ref, value_mix_ref = refs
+    else:
+        key_mix_ref, entropy_ref = refs
+    heads = query_ref.shape[1] // DH
+    group = heads // (key_ref.shape[1] // DH)
+    for head in range(heads):
+        cols = slice(head * DH, (head + 1) * DH)
+        kv_cols = slice((head // group) * DH, (head // group + 1) * DH)
+        keys = key_ref[:, kv_cols]
+        logits = lax.dot_general(
+            query_ref[:, cols], keys, (((1,), (1,)), ((), ())),
+            preferred_element_type=jnp.float32,
+        ) / math.sqrt(DH)
+        peak = jnp.max(logits, axis=1, keepdims=True)
+        unnormalized = jnp.exp(logits - peak)
+        total = jnp.sum(unnormalized, axis=1, keepdims=True)
+        weights = unnormalized / total
+        entropy = (jnp.log(total) + peak) - jnp.sum(weights * logits, axis=1, keepdims=True)
+        entropy_ref[:, head : head + 1] = entropy
+        rounded = weights.astype(jnp.bfloat16)
+        key_mix_ref[:, cols] = jnp.dot(
+            rounded, keys, preferred_element_type=jnp.float32
+        ).astype(jnp.bfloat16)
+        if with_values:
+            value_mix_ref[:, cols] = jnp.dot(
+                rounded, value_ref[:, kv_cols], preferred_element_type=jnp.float32
+            ).astype(jnp.bfloat16)
+
+
+def right_step(query_rows, keys, values):
     seq_count, place_count, feature_width = query_rows.shape
-    heads_kv = key_heads.shape[2]
-    shaped = query_rows.reshape(seq_count, place_count, heads_kv, -1, DH)
-    logits = jnp.einsum(
-        "scjgd,sijd->sjgci", shaped, key_heads, preferred_element_type=jnp.float32
-    ) / math.sqrt(DH)
-    weights = jax.nn.softmax(logits, axis=-1)
-    entropy = jax.nn.logsumexp(logits, axis=-1) - jnp.sum(weights * logits, axis=-1)
-    rounded = weights.astype(jnp.bfloat16)
-    key_mix = jnp.einsum(
-        "sjgci,sijd->scjgd", rounded, key_heads, preferred_element_type=jnp.float32
-    ).astype(jnp.bfloat16)
-    entropy = jnp.transpose(entropy, (0, 3, 1, 2))
-    value_mix = None
-    if value_heads is not None:
-        value_mix = jnp.einsum(
-            "sjgci,sijd->scjgd", rounded, value_heads, preferred_element_type=jnp.float32
-        ).astype(jnp.bfloat16)
-        value_mix = value_mix.reshape(seq_count, place_count, feature_width)
-    return key_mix.reshape(seq_count, place_count, feature_width), entropy, value_mix
+    heads = feature_width // DH
+    row_spec = pl.BlockSpec((None, place_count, feature_width), lambda s: (s, 0, 0))
+    kv_spec = pl.BlockSpec((None,) + keys.shape[1:], lambda s: (s, 0, 0))
+    entropy_spec = pl.BlockSpec((None, place_count, heads), lambda s: (s, 0, 0))
+    row_shape = jax.ShapeDtypeStruct(query_rows.shape, jnp.bfloat16)
+    entropy_shape = jax.ShapeDtypeStruct((seq_count, place_count, heads), jnp.float32)
+    if values is None:
+        key_mix, entropy = pl.pallas_call(
+            right_kernel,
+            grid=(seq_count,),
+            in_specs=[row_spec, kv_spec],
+            out_specs=[row_spec, entropy_spec],
+            out_shape=[row_shape, entropy_shape],
+        )(query_rows, keys)
+        return key_mix, entropy, None
+    return pl.pallas_call(
+        right_kernel,
+        grid=(seq_count,),
+        in_specs=[row_spec, kv_spec, kv_spec],
+        out_specs=[row_spec, entropy_spec, row_spec],
+        out_shape=[row_shape, entropy_shape, row_shape],
+    )(query_rows, keys, values)
 
 
 def entropy_rows(entropy, ctx):
@@ -79,10 +115,7 @@
         seq_count, place_count, feature_width = queries.shape
         keys = lax.all_gather(key_states, "head", axis=1, tiled=True)
         values = lax.all_gather(value_states, "head", axis=1, tiled=True)
-        block_len = keys.shape[1]
-        heads_kv = keys.shape[2] // DH
-        key_heads = keys.reshape(seq_count, block_len, heads_kv, DH)
-        value_heads = values.reshape(seq_count, block_len, heads_kv, DH)
+        key_heads, value_heads = keys, values
 
         key_mix, entropy, _ = right_step(queries, key_heads, None)
         query_rows = pair_rows(queries, ctx)

time: 123 us -> 134 us (1.089)
  Pallas kernels: 0 us -> 16.5 us
  other arithmetic: 5.17 us -> 0.6 us
  matrix products: 10.5 us -> 6.62 us
  blocking collectives: 84.8 us -> 86.8 us
  local copies, waits for them, and re-layouts: 6.4 us -> 7.77 us
    pallas_call x0 -> x2, Pallas kernels: none -> 16.5 us  [right_step(): pl.pallas_call(right_kernel, grid=(seq_count,), in_specs=[row_spec, kv_sp...]
    reduce_sum x4 -> x0, other arithmetic: 4.53 us -> none  [the longest x2 3.2 us: right_step(): jax.nn.logsumexp(logits, axis=-1) - jnp.sum(weights * logits, axis=-1)]
    reshape x1 -> x4, local copies, waits for them, and re-layouts: 0.24 us -> 4.16 us  [pair_rows(): return rows.reshape(seq_count, ctx, -1, DH)]
    dot_general x5 -> x0, matrix products: 3.89 us -> none  [the longest x2 1.9 us: right_step(): jnp.einsum('sjgci,sijd->scjgd', rounded, key_heads, preferred_element_typ...]
    all_gather x1, blocking collectives: 2.09 us -> 3.83 us  [local(): keys = lax.all_gather(key_states, 'head', axis=1, tiled=True)]
    another operation x1 -> x0, local copies, waits for them, and re-layouts: 1.47 us -> none
where the time goes in v3:
time: 134 us
  blocking collectives  86.8 us (65%)
  Pallas kernels  16.5 us (12%)
  waiting for transfers between devices  11.8 us (9%)
  local copies, waits for them, and re-layouts  7.77 us (6%)
  matrix products  6.62 us (5%)
  starting transfers between devices  3.49 us (3%)
    all_to_all x3, blocking collectives, exchange(): return lax.all_to_all(grid, 'ctx', split_axis=1, concat_axis=1, tiled=True)  80.9 us
    pallas_call x2, Pallas kernels, right_step(): pl.pallas_call(right_kernel, grid=(seq_count,), in_specs=[row_spec, kv_sp...  16.5 us
    all_to_all x1, waiting for transfers between devices, exchange(): return lax.all_to_all(grid, 'ctx', split_axis=1, concat_axis=1, tiled=True)  11.8 us
    sub x2, matrix products, left_step(): weights = jax.nn.softmax(logits, axis=-1)  5.46 us
    reshape x4, local copies, waits for them, and re-layouts, pair_rows(): return rows.reshape(seq_count, ctx, -1, DH)  4.16 us
    all_gather x1, blocking collectives, local(): keys = lax.all_gather(key_states, 'head', axis=1, tiled=True)  3.83 us
    all_to_all x1, starting transfers between devices, exchange(): return lax.all_to_all(grid, 'ctx', split_axis=1, concat_axis=1, tiled=True)  3.49 us
  transfers between devices with their start and end apart: 1, of which 1 were waited for; matrix products, arithmetic and copies ran while one was open for 0% of the time, Pallas kernels for 0%

profile of v3, /device:TPU:0, one launch (start us, length us, event | category | flops | bytes accessed | tf_op | source)
XLA Modules:
  0.0 133.8 jit_solution(680521940312761853)
XLA Ops:
  0.0 3.8 %all_gather.6.key_ref = bf16[1,128,1024]{2,1,0:T(8,128)(2,1)} all-gather(bf16[1,64,1024]{2,1,0:T(8,128)(2,1)} %param.4), channel_id=1, replica_groups=mesh['grp'=2,'ctx'=8,'head'=2] {'head'}, dimensions={1}, use_global_device_ids=true | all-gather | bytes 393216 | tf_op jit(solution)/shard_map/all_gather | solution.py:116
  3.8 1.3 reshape.151
  5.1 12.2 %shard_map.37 = (bf16[1,64,4096]{2,1,0:T(8,128)(2,1)}, f32[1,64,32]{2,1,0:T(8,128)}) custom-call(bf16[1,64,4096]{2,1,0:T(8,128)(2,1)} %query_ref.1, bf16[1,128,1024]{2,1,0:T(8,128)(2,1)} %all_gather.6.key_ref), custom_call_target="tpu_custom_call" | custom-call | tf_op jit(solution)/shard_map/pallas_call | solution.py:53
  17.3 0.0 copy-start.3
  17.3 1.3 reshape.152
  18.6 0.0 copy-done.3
  18.6 0.1 reshape.153
  18.7 0.1 maximum_bitcast_fusion
  18.8 34.2 %all_to_all.20 = bf16[1,8,518,128]{3,2,0,1:T(8,128)(2,1)S(1)} all-to-all(bf16[1,8,518,128]{3,2,0,1:T(8,128)(2,1)S(1)} %maximum_bitcast_fusion), channel_id=1, replica_groups=mesh['grp'=2,'ctx'=8,'head'=2] {'ctx'}, dimensions={1} | all-to-all | bytes 2121728 | tf_op jit(solution)/shard_map/all_to_all | solution.py:96
  53.0 0.1 copy.38
  53.1 0.1 fusion.19
  53.2 2.7 %fusion.20 = (f32[256,8]{1,0:T(8,128)S(1)}, f32[256,8,8]{1,2,0:T(8,128)S(1)}) fusion(bf16[1,8,256,128]{3,2,0,1:T(8,128)(2,1)S(1)} %get-tuple-element.18, f32[256,8]{1,0:T(8,128)S(1)} %copy.38, bf16[1,8,256,128]{3,2,0,1:T(8,128)(2,1)S(1)} %get-tuple-element.17), kind=kOutput, calls=%fused_computation.46 | convolution fusion | flops 4259847 | bytes 1130496 | tf_op jit(solution)/shard_map/sub | solution.py:109
  56.0 0.4 fusion.11
  56.3 0.6 divide_convert_fusion.1
  57.0 0.0 copy-start.1
  57.0 0.9 copy.39
  57.8 3.5 %all-to-all-start.1 = ((bf16[1,8,256,128]{3,2,0,1:T(8,128)(2,1)}), bf16[1,8,256,128]{3,2,0,1:T(8,128)(2,1)S(1)}, u32[]{:S(2)}, u32[]{:S(2)}) async-start(bf16[1,8,256,128]{3,2,0,1:T(8,128)(2,1)} %copy.39), calls=%async_computation.1 | async-start | bytes 1048576 | tf_op jit(solution)/shard_map/all_to_all | solution.py:96
  61.3 0.0 copy-done.1
  61.4 2.1 %all_gather.7.refs_0_ = bf16[1,128,1024]{2,1,0:T(8,128)(2,1)} all-gather(bf16[1,64,1024]{2,1,0:T(8,128)(2,1)S(1)} %copy-done.1), channel_id=1, replica_groups=mesh['grp'=2,'ctx'=8,'head'=2] {'head'}, dimensions={1}, use_global_device_ids=true | all-gather | bytes 393216 | tf_op jit(solution)/shard_map/all_gather | solution.py:117
  63.5 11.8 %all-to-all-done.1 = bf16[1,8,256,128]{3,2,0,1:T(8,128)(2,1)S(1)} async-done(((bf16[1,8,256,128]{3,2,0,1:T(8,128)(2,1)}), bf16[1,8,256,128]{3,2,0,1:T(8,128)(2,1)S(1)}, u32[]{:S(2)}, u32[]{:S(2)}) %all-to-all-start.1) | async-done | bytes 524320 | tf_op jit(solution)/shard_map/all_to_all | solution.py:96
  75.3 1.0 reshape.157.query_ref
  76.3 4.4 %shard_map.38 = (bf16[1,64,4096]{2,1,0:T(8,128)(2,1)}, f32[1,64,32]{2,1,0:T(8,128)}, bf16[1,64,4096]{2,1,0:T(8,128)(2,1)}) custom-call(bf16[1,64,4096]{2,1,0:T(8,128)(2,1)} %reshape.157.query_ref, bf16[1,128,1024]{2,1,0:T(8,128)(2,1)} %all_gather.6.key_ref, bf16[1,128,1024]{2,1,0:T(8,128)(2,1)} %all_gather.7.refs_0_), custom_call_target="tpu_custom_call" | custom-call | tf_op jit(solution)/shard_map/pallas_call | solution.py:61
  80.6 0.0 copy-start.2
  80.6 0.0 copy-start
  80.6 1.3 %reshape.158 = bf16[1,8,256,128]{3,2,1,0:T(8,128)(2,1)S(1)} reshape(bf16[1,64,4096]{2,1,0:T(8,128)(2,1)} %get-tuple-element.12) | data formatting | bytes 1048576 | tf_op jit(solution)/shard_map/reshape | solution.py:92
  82.0 0.0 copy-done.2
  82.0 0.1 reshape.160
  82.1 0.0 copy-done
  82.1 0.2 reshape.159
  82.4 0.1 pad_maximum_fusion
  82.5 30.1 %all_to_all.21 = bf16[1,8,518,128]{3,2,0,1:T(8,128)(2,1)S(1)} all-to-all(bf16[1,8,518,128]{3,2,0,1:T(8,128)(2,1)S(1)} %pad_maximum_fusion), channel_id=1, replica_groups=mesh['grp'=2,'ctx'=8,'head'=2] {'ctx'}, dimensions={1} | all-to-all | bytes 2121728 | tf_op jit(solution)/shard_map/all_to_all | solution.py:96
  112.6 0.1 copy.46
  112.7 0.1 fusion.18
  112.8 2.7 %fusion.21 = (f32[256,8]{1,0:T(8,128)S(1)}, f32[256,8,8]{1,2,0:T(8,128)S(1)}) fusion(bf16[1,8,256,128]{3,2,0,1:T(8,128)(2,1)S(1)} %get-tuple-element.16, f32[256,8]{1,0:T(8,128)S(1)} %copy.46, bf16[1,8,256,128]{3,2,0,1:T(8,128)(2,1)S(1)} %get-tuple-element.17), kind=kOutput, calls=%fused_computation.47 | convolution fusion | flops 4259847 | bytes 1130496 | tf_op jit(solution)/shard_map/sub | solution.py:109
  115.5 0.6 fusion.8
  116.1 0.1 copy.48
  116.2 16.6 %all_to_all.22 = bf16[1,8,256,128]{3,2,0,1:T(8,128)(2,1)S(1)} all-to-all(bf16[1,8,256,128]{3,2,0,1:T(8,128)(2,1)S(1)} %copy.48), channel_id=1, replica_groups=mesh['grp'=2,'ctx'=8,'head'=2] {'ctx'}, dimensions={1} | all-to-all | bytes 1048576 | tf_op jit(solution)/shard_map/all_to_all | solution.py:96
  132.8 1.0 reshape.164
  (17 shorter events, 0.1 us)
Async XLA Ops:
  17.3 1.3 copy-start.3
  57.0 4.4 %copy-start.1 = (bf16[1,64,1024]{2,1,0:T(8,128)(2,1)S(1)}, bf16[1,64,1024]{2,1,0:T(8,128)(2,1)}, u32[]{:S(2)}) copy-start(bf16[1,64,1024]{2,1,0:T(8,128)(2,1)} %param.5) | copy-start | bytes 393220
  57.8 17.4 %all-to-all-start.1 = ((bf16[1,8,256,128]{3,2,0,1:T(8,128)(2,1)}), bf16[1,8,256,128]{3,2,0,1:T(8,128)(2,1)S(1)}, u32[]{:S(2)}, u32[]{:S(2)}) async-start(bf16[1,8,256,128]{3,2,0,1:T(8,128)(2,1)} %copy.39), calls=%async_computation.1 | async-start | bytes 1048576 | tf_op jit(solution)/shard_map/all_to_all | solution.py:96
  80.6 1.4 %copy-start.2 = (f32[1,64,32]{2,1,0:T(8,128)S(1)}, f32[1,64,32]{2,1,0:T(8,128)}, u32[]{:S(2)}) copy-start(f32[1,64,32]{2,1,0:T(8,128)} %get-tuple-element.14) | copy-start | bytes 24580
  80.6 1.5 %copy-start = (bf16[1,64,4096]{2,1,0:T(8,128)(2,1)S(1)}, bf16[1,64,4096]{2,1,0:T(8,128)(2,1)}, u32[]{:S(2)}) copy-start(bf16[1,64,4096]{2,1,0:T(8,128)(2,1)} %get-tuple-element.13) | copy-start | bytes 1572868

commit v4 on v1

--- a/solution.py
+++ b/solution.py
@@ -33,7 +33,7 @@
 
 def entropy_rows(entropy, ctx):
     seq_count = entropy.shape[0]
-    flat = entropy.reshape(seq_count, ctx, -1)
+    flat = pair_entropy(entropy.reshape(seq_count, entropy.shape[1], -1), ctx)
     chunk = flat.shape[2]
     high = lax.optimization_barrier(flat.astype(jnp.bfloat16))
     rest = flat - high.astype(jnp.float32)
@@ -52,8 +52,27 @@
 
 
 def pair_rows(rows, ctx):
-    seq_count = rows.shape[0]
-    return rows.reshape(seq_count, ctx, -1, DH)
+    seq_count, place_count, feature_width = rows.shape
+    if place_count % ctx:
+        return rows.reshape(seq_count, ctx, -1, DH)
+    shaped = rows.reshape(seq_count, ctx, place_count // ctx, feature_width // DH, DH)
+    return jnp.swapaxes(shaped, 2, 3).reshape(seq_count, ctx, -1, DH)
+
+
+def rows_back(grid, place_count, feature_width):
+    seq_count, ctx = grid.shape[:2]
+    if place_count % ctx:
+        return grid.reshape(seq_count, place_count, feature_width)
+    shaped = grid.reshape(seq_count, ctx, feature_width // DH, place_count // ctx, DH)
+    return jnp.swapaxes(shaped, 2, 3).reshape(seq_count, place_count, feature_width)
+
+
+def pair_entropy(entropy, ctx):
+    seq_count, place_count, heads = entropy.shape
+    if place_count % ctx:
+        return entropy.reshape(seq_count, ctx, -1)
+    shaped = entropy.reshape(seq_count, ctx, place_count // ctx, heads)
+    return jnp.swapaxes(shaped, 2, 3).reshape(seq_count, ctx, -1)
 
 
 def exchange(grid):
@@ -61,8 +80,7 @@
 
 
 def to_blocks(grid, place_count, feature_width):
-    seq_count = grid.shape[0]
-    return exchange(grid).reshape(seq_count, place_count, feature_width)
+    return rows_back(exchange(grid), place_count, feature_width)
 
 
 def left_step(query_grid, key_grid, entropy_grid):

time: 123 us -> 120 us (0.976)
  local copies, waits for them, and re-layouts: 6.4 us -> 3.88 us
where the time goes in v4:
time: 120 us
  blocking collectives  85.1 us (71%)
  waiting for transfers between devices  11.6 us (10%)
  matrix products  10.5 us (9%)
  other arithmetic  5.17 us (4%)
  local copies, waits for them, and re-layouts  3.88 us (3%)
  starting transfers between devices  3.49 us (3%)
    all_to_all x3, blocking collectives, exchange(): return lax.all_to_all(grid, 'ctx', split_axis=1, concat_axis=1, tiled=True)  80.7 us
    all_to_all x1, waiting for transfers between devices, exchange(): return lax.all_to_all(grid, 'ctx', split_axis=1, concat_axis=1, tiled=True)  11.6 us
    sub x2, matrix products, left_step(): weights = jax.nn.softmax(logits, axis=-1)  5.46 us
    all_to_all x1, starting transfers between devices, exchange(): return lax.all_to_all(grid, 'ctx', split_axis=1, concat_axis=1, tiled=True)  3.49 us
    reduce_sum x2, other arithmetic, right_step(): jax.nn.logsumexp(logits, axis=-1) - jnp.sum(weights * logits, axis=-1)  3.2 us
    all_gather x1, blocking collectives, local(): keys = lax.all_gather(key_states, 'head', axis=1, tiled=True)  2.42 us
  transfers between devices with their start and end apart: 1, of which 1 were waited for; matrix products, arithmetic and copies ran while one was open for 0% of the time, Pallas kernels for 0%

profile of v4, /device:TPU:0, one launch (start us, length us, event | category | flops | bytes accessed | tf_op | source)
XLA Modules:
  0.0 120.1 jit_solution(13218062482816086877)
XLA Ops:
  0.0 0.0 copy-start
  0.0 2.4 %all_gather.6 = bf16[1,128,1024]{2,1,0:T(8,128)(2,1)S(1)} all-gather(bf16[1,64,1024]{2,1,0:T(8,128)(2,1)} %param.4), channel_id=1, replica_groups=mesh['grp'=2,'ctx'=8,'head'=2] {'head'}, dimensions={1}, use_global_device_ids=true | all-gather | bytes 393216 | tf_op jit(solution)/shard_map/all_gather | solution.py:98
  2.4 0.2 copy.31
  2.6 0.0 copy-done
  2.6 0.4 reshape.320
  3.0 0.5 fusion.41
  3.5 0.7 fusion.12
  4.2 0.9 convolution_convert_fusion.3
  5.1 1.6 %exponential_reduce_fusion.1 = (f32[8,4,64]{2,1,0:T(4,128)S(1)}, f32[8,4,64]{2,1,0:T(4,128)S(1)}) fusion(f32[1,8,4,64,128]{4,3,2,1,0:T(8,128)S(1)} %get-tuple-element.14, f32[8,4,64]{2,1,0:T(4,128)S(1)} %is-finite_select_fusion.3, f32[8,4,64]{2,1,0:T(4,128)S(1)} %fusion.12, f32[8,4,64]{2,1,0:T(4,128)S(1)} %get-tuple-element.13), kind=kLoop, calls=%fused_computation.28 | loop fusion | flops 1568768 | bytes 1089536 | tf_op jit(solution)/shard_map/reduce_sum | solution.py:19
  6.7 0.1 copy.111
  6.9 0.1 reshape_reshape.17
  7.0 0.1 reshape.323
  7.2 0.1 pad_maximum_fusion
  7.3 34.2 %all_to_all.20 = bf16[1,8,518,128]{3,2,0,1:T(8,128)(2,1)S(1)} all-to-all(bf16[1,8,518,128]{3,2,0,1:T(8,128)(2,1)S(1)} %pad_maximum_fusion), channel_id=1, replica_groups=mesh['grp'=2,'ctx'=8,'head'=2] {'ctx'}, dimensions={1} | all-to-all | bytes 2121728 | tf_op jit(solution)/shard_map/all_to_all | solution.py:79
  41.5 0.1 copy.41
  41.6 0.1 fusion.40
  41.7 2.7 %fusion.42 = (f32[256,8]{1,0:T(8,128)S(1)}, f32[256,8,8]{1,2,0:T(8,128)S(1)}) fusion(bf16[1,8,256,128]{3,2,0,1:T(8,128)(2,1)S(1)} %get-tuple-element.12, f32[256,8]{1,0:T(8,128)S(1)} %copy.41, bf16[1,8,256,128]{3,2,0,1:T(8,128)(2,1)S(1)} %get-tuple-element.11), kind=kOutput, calls=%fused_computation.83 | convolution fusion | flops 4259847 | bytes 1130496 | tf_op jit(solution)/shard_map/sub | solution.py:91
  44.5 0.4 fusion.24
  44.8 0.6 divide_convert_fusion.1
  45.4 0.0 copy-start.1
  45.5 0.9 copy.42
  46.3 3.5 %all-to-all-start.1 = ((bf16[1,8,256,128]{3,2,0,1:T(8,128)(2,1)}), bf16[1,8,256,128]{3,2,0,1:T(8,128)(2,1)S(1)}, u32[]{:S(2)}, u32[]{:S(2)}) async-start(bf16[1,8,256,128]{3,2,0,1:T(8,128)(2,1)} %copy.42), calls=%async_computation.1 | async-start | bytes 1048576 | tf_op jit(solution)/shard_map/all_to_all | solution.py:79
  49.8 0.0 copy-done.1
  49.8 2.0 %all_gather.7 = bf16[1,128,1024]{2,1,0:T(8,128)(2,1)S(1)} all-gather(bf16[1,64,1024]{2,1,0:T(8,128)(2,1)S(1)} %copy-done.1), channel_id=1, replica_groups=mesh['grp'=2,'ctx'=8,'head'=2] {'head'}, dimensions={1}, use_global_device_ids=true | all-gather | bytes 393216 | tf_op jit(solution)/shard_map/all_gather | solution.py:99
  51.8 0.2 copy.47
  52.0 11.6 %all-to-all-done.1 = bf16[1,8,256,128]{3,2,0,1:T(8,128)(2,1)S(1)} async-done(((bf16[1,8,256,128]{3,2,0,1:T(8,128)(2,1)}), bf16[1,8,256,128]{3,2,0,1:T(8,128)(2,1)S(1)}, u32[]{:S(2)}, u32[]{:S(2)}) %all-to-all-start.1) | async-done | bytes 524320 | tf_op jit(solution)/shard_map/all_to_all | solution.py:79
  63.6 0.1 copy.43
  63.8 0.5 fusion.43
  64.3 0.7 fusion.14
  65.0 0.9 convolution_convert_fusion.2
  65.9 1.6 %exponential_reduce_fusion = (f32[8,4,64]{2,1,0:T(4,128)S(1)}, f32[8,4,64]{2,1,0:T(4,128)S(1)}) fusion(f32[1,8,4,64,128]{4,3,2,1,0:T(8,128)S(1)} %get-tuple-element.18, f32[8,4,64]{2,1,0:T(4,128)S(1)} %is-finite_select_fusion.1, f32[8,4,64]{2,1,0:T(4,128)S(1)} %fusion.14, f32[8,4,64]{2,1,0:T(4,128)S(1)} %get-tuple-element.17), kind=kLoop, calls=%fused_computation.24 | loop fusion | flops 1568768 | bytes 1089536 | tf_op jit(solution)/shard_map/reduce_sum | solution.py:19
  67.6 0.1 reshape_reshape.20
  67.7 0.1 reshape.333
  67.9 1.0 convolution_convert_fusion.1
  68.8 0.2 copy_bitcast_fusion.7
  69.1 0.1 pad_maximum_fusion.1
  69.2 29.9 %all_to_all.21 = bf16[1,8,518,128]{3,2,0,1:T(8,128)(2,1)S(1)} all-to-all(bf16[1,8,518,128]{3,2,0,1:T(8,128)(2,1)S(1)} %pad_maximum_fusion.1), channel_id=1, replica_groups=mesh['grp'=2,'ctx'=8,'head'=2] {'ctx'}, dimensions={1} | all-to-all | bytes 2121728 | tf_op jit(solution)/shard_map/all_to_all | solution.py:79
  99.1 0.1 copy.55
  99.3 0.1 fusion.39
  99.4 2.7 %fusion.44 = (f32[256,8]{1,0:T(8,128)S(1)}, f32[256,8,8]{1,2,0:T(8,128)S(1)}) fusion(bf16[1,8,256,128]{3,2,0,1:T(8,128)(2,1)S(1)} %get-tuple-element.10, f32[256,8]{1,0:T(8,128)S(1)} %copy.55, bf16[1,8,256,128]{3,2,0,1:T(8,128)(2,1)S(1)} %get-tuple-element.11), kind=kOutput, calls=%fused_computation.85 | convolution fusion | flops 4259847 | bytes 1130496 | tf_op jit(solution)/shard_map/sub | solution.py:91
  102.1 0.6 fusion.10
  102.7 0.1 copy.57
  102.8 16.6 %all_to_all.22 = bf16[1,8,256,128]{3,2,0,1:T(8,128)(2,1)S(1)} all-to-all(bf16[1,8,256,128]{3,2,0,1:T(8,128)(2,1)S(1)} %copy.57), channel_id=1, replica_groups=mesh['grp'=2,'ctx'=8,'head'=2] {'ctx'}, dimensions={1} | all-to-all | bytes 1048576 | tf_op jit(solution)/shard_map/all_to_all | solution.py:79
  119.3 0.8 copy.113
  (23 shorter events, 0.2 us)
Async XLA Ops:
  0.0 2.6 %copy-start = (bf16[1,64,4096]{2,1,0:T(8,128)(2,1)S(1)}, bf16[1,64,4096]{2,1,0:T(8,128)(2,1)}, u32[]{:S(2)}) copy-start(bf16[1,64,4096]{2,1,0:T(8,128)(2,1)} %param.3) | copy-start | bytes 1572868
  45.4 4.4 %copy-start.1 = (bf16[1,64,1024]{2,1,0:T(8,128)(2,1)S(1)}, bf16[1,64,1024]{2,1,0:T(8,128)(2,1)}, u32[]{:S(2)}) copy-start(bf16[1,64,1024]{2,1,0:T(8,128)(2,1)} %param.5) | copy-start | bytes 393220
  46.3 17.3 %all-to-all-start.1 = ((bf16[1,8,256,128]{3,2,0,1:T(8,128)(2,1)}), bf16[1,8,256,128]{3,2,0,1:T(8,128)(2,1)S(1)}, u32[]{:S(2)}, u32[]{:S(2)}) async-start(bf16[1,8,256,128]{3,2,0,1:T(8,128)(2,1)} %copy.42), calls=%async_computation.1 | async-start | bytes 1048576 | tf_op jit(solution)/shard_map/all_to_all | solution.py:79

commit v5 on v0

v5 whole, which is shorter than its diff:
```python
import math

import jax
import jax.numpy as jnp
from jax import lax
from jax.sharding import PartitionSpec as P

DH = 128


def softmax_terms(logits):
    weights = jax.nn.softmax(logits, axis=-1)
    entropy = jax.nn.logsumexp(logits, axis=-1) - jnp.sum(weights * logits, axis=-1)
    return weights, entropy


def entropy_rows(flat):
    ctx, chunk = flat.shape
    high = lax.optimization_barrier(flat.astype(jnp.bfloat16))
    rest = flat - high.astype(jnp.float32)
    middle = lax.optimization_barrier(rest.astype(jnp.bfloat16))
    low = (rest - middle.astype(jnp.float32)).astype(jnp.bfloat16)
    terms = jnp.concatenate([high, middle, low], axis=1)
    row_count = -(-3 * chunk // DH)
    terms = jnp.pad(terms, ((0, 0), (0, row_count * DH - 3 * chunk)))
    return terms.reshape(ctx, row_count, DH)


def entropy_from_rows(rows, chunk):
    ctx = rows.shape[0]
    terms = rows.reshape(ctx, -1)[:, : 3 * chunk].astype(jnp.float32)
    return (terms[:, :chunk] + terms[:, chunk : 2 * chunk]) + terms[:, 2 * chunk :]


def exchange(grid):
    return lax.all_to_all(grid, "ctx", split_axis=0, concat_axis=0, tiled=True)


def left_step(query_grid, key_grid, entropy_grid):
    logits = jnp.einsum(
        "apd,lpd->pal", query_grid, key_grid, preferred_element_type=jnp.float32
    ) / math.sqrt(DH)
    logits = logits + jnp.transpose(entropy_grid, (1, 0))[:, None, :]
    weights = jax.nn.softmax(logits, axis=-1)
    return weights, weights.astype(jnp.bfloat16)


def to_dest(rows, ctx, heads_kv):
    place_count, group = rows.shape[0], rows.shape[2]
    repeat = ctx // heads_kv
    shaped = rows.reshape((repeat, place_count // repeat) + rows.shape[1:])
    shaped = jnp.moveaxis(shaped, 2, 0)
    return shaped.reshape((ctx, place_count // repeat * group) + rows.shape[3:])


def from_dest(grid, place_count, heads_kv):
    ctx = grid.shape[0]
    repeat = ctx // heads_kv
    shaped = grid.reshape(heads_kv, repeat, place_count // repeat, -1, DH)
    shaped = jnp.moveaxis(shaped, 0, 2)
    return shaped.reshape(place_count, -1)


def one_sequence(queries, keys, values, ctx):
    place_count, feature_width = queries.shape
    block_len = keys.shape[0]
    heads_kv = keys.shape[1] // DH
    repeat = ctx // heads_kv
    query_heads = queries.reshape(place_count, heads_kv, -1, DH)
    key_heads = keys.reshape(block_len, heads_kv, DH)
    value_heads = values.reshape(block_len, heads_kv, DH)

    logits = jnp.einsum(
        "cjgd,ijd->cjgi", query_heads, key_heads, preferred_element_type=jnp.float32
    ) / math.sqrt(DH)
    weights, entropy = softmax_terms(logits)
    rounded = weights.astype(jnp.bfloat16)
    key_mix = jnp.einsum(
        "cjgi,ijd->cjgd", rounded, key_heads, preferred_element_type=jnp.float32
    ).astype(jnp.bfloat16)

    query_rows = to_dest(query_heads, ctx, heads_kv)
    chunk = query_rows.shape[1]
    key_rows = jnp.repeat(jnp.swapaxes(key_heads, 0, 1), repeat, axis=0)
    value_rows = jnp.repeat(jnp.swapaxes(value_heads, 0, 1), repeat, axis=0)
    payload = jnp.concatenate(
        [
            query_rows,
            to_dest(key_mix, ctx, heads_kv),
            key_rows,
            value_rows,
            entropy_rows(to_dest(entropy, ctx, heads_kv)),
        ],
        axis=1,
    )
    rows = exchange(payload)
    query_grid = rows[:, :chunk]
    key_grid = rows[:, chunk : 2 * chunk]
    block_keys = rows[:, 2 * chunk : 2 * chunk + block_len]
    block_values = rows[:, 2 * chunk + block_len : 2 * chunk + 2 * block_len]
    entropy_grid = entropy_from_rows(rows[:, 2 * chunk + 2 * block_len :], chunk)

    weights, left_rounded = left_step(query_grid, key_grid, entropy_grid)
    column_mass = jnp.transpose(jnp.sum(weights, axis=1), (1, 0))
    mixed = jnp.einsum(
        "pal,apd->lpd", left_rounded, query_grid, preferred_element_type=jnp.float32
    )
    query_mix = (mixed / jnp.maximum(column_mass, 1.0)[..., None]).astype(jnp.bfloat16)

    logits = jnp.einsum(
        "lpd,lid->lpi", query_mix, block_keys, preferred_element_type=jnp.float32
    ) / math.sqrt(DH)
    weights, entropy = softmax_terms(logits)
    rounded = weights.astype(jnp.bfloat16)
    key_mix = jnp.einsum(
        "lpi,lid->lpd", rounded, block_keys, preferred_element_type=jnp.float32
    ).astype(jnp.bfloat16)
    value_mix = jnp.einsum(
        "lpi,lid->lpd", rounded, block_values, preferred_element_type=jnp.float32
    ).astype(jnp.bfloat16)

    _, final_left = left_step(query_grid, key_mix, entropy)
    attended = jnp.einsum(
        "pal,lpd->apd", final_left, value_mix, preferred_element_type=jnp.float32
    ).astype(jnp.bfloat16)
    return from_dest(exchange(attended), place_count, heads_kv)


def make_local(ctx):
    def local(queries, key_states, value_states):
        keys = lax.all_gather(key_states, "head", axis=1, tiled=True)
        values = lax.all_gather(value_states, "head", axis=1, tiled=True)
        return jnp.stack(
            [
                one_sequence(queries[s], keys[s], values[s], ctx)
                for s in range(queries.shape[0])
            ]
        )

    return local


def solution(mesh):
    placed = P("grp", ("ctx", "head"), None)
    return jax.shard_map(
        make_local(mesh.shape["ctx"]),
        mesh=mesh,
        in_specs=(placed, placed, placed),
        out_specs=placed,
        check_vma=False,
    )
```

time: 139 us -> 88.1 us (0.63)
  waiting for transfers between devices: 68.1 us -> 0 us
  blocking collectives: 22.3 us -> 66.5 us
  starting transfers between devices: 21.7 us -> 0 us
  local copies, waits for them, and re-layouts: 10.6 us -> 7.68 us
  other arithmetic: 5.13 us -> 3.26 us
    all_to_all x5 -> x0, waiting for transfers between devices: 68.1 us -> none  [the longest x2 50.4 us: to_places(): rows = lax.all_to_all(rows, 'ctx', split_axis=2, concat_axis=2, tiled=True)]
    all_to_all x1 -> x2, blocking collectives: 17.9 us -> 62.5 us  [exchange(): return lax.all_to_all(grid, 'ctx', split_axis=0, concat_axis=0, tiled=True)]
    all_to_all x5 -> x0, starting transfers between devices: 21.7 us -> none  [the longest x2 10.8 us: to_places(): ent = lax.all_to_all(ent, 'ctx', split_axis=1, concat_axis=1, tiled=True)]
    reshape x7 -> x1, local copies, waits for them, and re-layouts: 5.75 us -> 0.06 us  [to_dest(): return shaped.reshape((ctx, place_count // repeat * group) + rows.shape[3:])]
    another operation x4, local copies, waits for them, and re-layouts: 1.54 us -> 4.11 us  [the longest x2 1.48 us: to_dest(): shaped = rows.reshape((repeat, place_count // repeat) + rows.shape[1:])]
    convert_element_type x5 -> x1, local copies, waits for them, and re-layouts: 2.17 us -> 0.07 us  [one_sequence(): attended = jnp.einsum('pal,lpd->apd', final_left, value_mix, preferred_el...]
    reduce_sum x5, other arithmetic: 4.87 us -> 3.16 us  [the longest x2 1.98 us: softmax_terms(): jax.nn.logsumexp(logits, axis=-1) - jnp.sum(weights * logits, axis=-1)]
  transfers between devices with their start and end apart: 5 -> 0, of which waited for: 5 -> 0; matrix products, arithmetic and copies ran while one was open for 6% -> 0% of each run, Pallas kernels for 0% -> 0%
where the time goes in v5:
time: 88.1 us; the launch traced here: 87.7 us
  blocking collectives  66.5 us (75%)
  matrix products  9.94 us (11%)
  local copies, waits for them, and re-layouts  7.68 us (9%)
  other arithmetic  3.26 us (4%)
    all_to_all x2, blocking collectives, exchange(): return lax.all_to_all(grid, 'ctx', split_axis=0, concat_axis=0, tiled=True)  62.5 us
    sub x2, matrix products, left_step(): weights = jax.nn.softmax(logits, axis=-1)  5.41 us
    all_gather x1, blocking collectives, local(): keys = lax.all_gather(key_states, 'head', axis=1, tiled=True)  2.09 us
    all_gather x1, blocking collectives, local(): values = lax.all_gather(value_states, 'head', axis=1, tiled=True)  1.99 us
    reduce_sum x2, other arithmetic, softmax_terms(): jax.nn.logsumexp(logits, axis=-1) - jnp.sum(weights * logits, axis=-1)  1.98 us

profile of v5, /device:TPU:0, one launch (start us, length us, event | category | flops | bytes accessed | tf_op | source)
XLA Modules:
  0.0 87.7 jit_solution(13777374624694599312)
XLA Ops:
  0.0 0.0 copy-start
  0.0 0.0 copy-start.1
  0.0 1.4 %reshape_squeeze.10 = bf16[64,8,4,128]{3,2,1,0:T(4,128)(2,1)S(1)} reshape(bf16[1,64,4096]{2,1,0:T(8,128)(2,1)} %param.3) | data formatting | bytes 1048576 | tf_op jit(solution)/shard_map/reshape;squeeze | solution.py:69
  1.5 1.4 %reshape_reshape_squeeze.3 = bf16[1,64,8,4,128]{4,3,2,1,0:T(4,128)(2,1)S(1)} reshape(bf16[1,64,4096]{2,1,0:T(8,128)(2,1)} %param.3) | data formatting | bytes 1048576 | tf_op jit(solution)/shard_map/reshape;reshape;squeeze | solution.py:51
  2.9 0.0 copy-done
  2.9 2.1 %all_gather.6 = bf16[1,128,1024]{2,1,0:T(8,128)(2,1)S(1)} all-gather(bf16[1,64,1024]{2,1,0:T(8,128)(2,1)S(1)} %copy-done), channel_id=1, replica_groups=mesh['grp'=2,'ctx'=8,'head'=2] {'head'}, dimensions={1}, use_global_device_ids=true | all-gather | bytes 393216 | tf_op jit(solution)/shard_map/all_gather | solution.py:131
  5.0 0.2 copy.76
  5.1 0.2 copy.84
  5.3 0.0 copy-done.1
  5.3 2.0 %all_gather.7 = bf16[1,128,1024]{2,1,0:T(8,128)(2,1)S(1)} all-gather(bf16[1,64,1024]{2,1,0:T(8,128)(2,1)S(1)} %copy-done.1), channel_id=1, replica_groups=mesh['grp'=2,'ctx'=8,'head'=2] {'head'}, dimensions={1}, use_global_device_ids=true | all-gather | bytes 393216 | tf_op jit(solution)/shard_map/all_gather | solution.py:132
  7.4 0.1 copy.75
  7.5 0.5 fusion.46
  8.0 0.7 fusion.14
  8.7 0.9 %fusion.11 = bf16[8,1,64,4,128]{4,2,3,0,1:T(8,128)(2,1)S(1)} fusion(bf16[128,8,128,1]{0,2,3,1:T(8,128)(2,1)S(1)} %bitcast.68, f32[64,8,4,128]{3,0,2,1:T(8,128)S(1)} %get-tuple-element.12, f32[64,8,4]{0,2,1:T(4,128)S(1)} %fusion.14, f32[64,8,4]{0,2,1:T(4,128)S(1)} %get-tuple-element.11), kind=kOutput, calls=%fused_computation.20 | convolution fusion | flops 68157440 | bytes 1851392 | tf_op jit(solution)/shard_map/cjgi,ijd->cjgd/dot_general | solution.py:78
  9.6 1.6 %exponential_reduce_fusion.1 = (f32[64,8,4]{0,2,1:T(4,128)S(1)}, f32[64,8,4]{0,2,1:T(4,128)S(1)}) fusion(f32[64,8,4,128]{3,0,2,1:T(8,128)S(1)} %get-tuple-element.12, f32[64,8,4]{0,2,1:T(4,128)S(1)} %is-finite_select_fusion.1, f32[64,8,4]{0,2,1:T(4,128)S(1)} %fusion.14, f32[64,8,4]{0,2,1:T(4,128)S(1)} %get-tuple-element.11), kind=kLoop, calls=%fused_computation.27 | loop fusion | flops 1568768 | bytes 1089536 | tf_op jit(solution)/shard_map/reduce_sum | solution.py:13
  11.2 0.3 copy.80
  11.6 0.1 copy.81
  11.7 0.1 copy.82
  11.9 0.1 constant_dynamic-update-slice_fusion.1
  12.1 0.2 copy.85
  12.3 45.4 %all_to_all.10 = bf16[8,774,128]{2,1,0:T(8,128)(2,1)S(1)} all-to-all(bf16[8,774,128]{2,1,0:T(8,128)(2,1)S(1)} %copy.85), channel_id=1, replica_groups=mesh['grp'=2,'ctx'=8,'head'=2] {'ctx'}, dimensions={0} | all-to-all | bytes 3170304 | tf_op jit(solution)/shard_map/all_to_all | solution.py:36
  57.7 0.1 copy.89
  57.8 0.9 %fusion.45 = (bf16[8,256,128]{2,1,0:T(8,128)(2,1)S(1)}, bf16[8,256,128]{2,1,0:T(8,128)(2,1)}) fusion(bf16[8,774,128]{2,1,0:T(8,128)(2,1)S(1)} %all_to_all.10), kind=kLoop, calls=%fused_computation.74 | loop fusion | bytes 2097152 | tf_op jit(solution)/shard_map/slice | solution.py:97
  58.7 2.2 %fusion.47 = (f32[256,8]{1,0:T(8,128)S(1)}, f32[256,8,8]{1,2,0:T(8,128)S(1)}) fusion(bf16[8,256,128]{2,1,0:T(8,128)(2,1)} %get-tuple-element.10, f32[256,8]{1,0:T(8,128)S(1)} %copy.89, bf16[8,256,128]{2,1,0:T(8,128)(2,1)S(1)} %get-tuple-element.9), kind=kOutput, calls=%fused_computation.76 | convolution fusion | flops 4259847 | bytes 1130496 | tf_op jit(solution)/shard_map/sub | solution.py:44
  61.0 0.4 fusion.30
  61.3 0.6 fusion.10
  62.0 0.3 fusion.48
  62.3 0.2 fusion.16
  62.5 0.4 exponential_reduce_fusion
  62.9 0.1 copy.94
  63.0 1.2 %convolution_convert_fusion.1 = bf16[8,256,128]{2,1,0:T(8,128)(2,1)} fusion(bf16[8,774,128]{2,1,0:T(8,128)(2,1)S(1)} %all_to_all.10, f32[8,256,128]{1,2,0:T(8,128)S(1)} %get-tuple-element.16, f32[8,256]{1,0:T(8,128)S(1)} %fusion.16, f32[8,256]{1,0:T(8,128)S(1)} %get-tuple-element.15), kind=kOutput, calls=%fused_computation.16 | convolution fusion | flops 68157440 | bytes 1851392 | tf_op jit(solution)/shard_map/lpi,lid->lpd/dot_general | solution.py:115
  64.2 3.2 %fusion.49 = (f32[256,8]{1,0:T(8,128)S(1)}, f32[256,8,8]{1,2,0:T(8,128)}) fusion(bf16[8,256,128]{2,1,0:T(8,128)(2,1)} %convolution_convert_fusion.1, f32[256,8]{1,0:T(8,128)S(1)} %copy.94, bf16[8,256,128]{2,1,0:T(8,128)(2,1)S(1)} %get-tuple-element.9), kind=kOutput, calls=%fused_computation.78 | convolution fusion | flops 4259847 | bytes 1130496 | tf_op jit(solution)/shard_map/sub | solution.py:44
  67.4 0.0 copy-start.2
  67.4 0.4 convolution_convert_fusion.2
  67.7 0.8 copy-done.2
  68.6 0.6 fusion.12
  69.2 0.1 copy.97
  69.3 17.0 %all_to_all.11 = bf16[8,256,128]{2,1,0:T(8,128)(2,1)S(1)} all-to-all(bf16[8,256,128]{2,1,0:T(8,128)(2,1)S(1)} %copy.97), channel_id=1, replica_groups=mesh['grp'=2,'ctx'=8,'head'=2] {'ctx'}, dimensions={0} | all-to-all | bytes 1048576 | tf_op jit(solution)/shard_map/all_to_all | solution.py:36
  86.3 0.2 copy.98
  86.5 1.2 %stack_reshape.3 = bf16[1,64,4096]{2,1,0:T(8,128)(2,1)} reshape(bf16[1,64,8,4,128]{4,3,2,1,0:T(4,128)(2,1)S(1)} %copy.98) | data formatting | bytes 1048576 | tf_op jit(solution)/shard_map/stack;reshape | solution.py:133
  (16 shorter events, 0.3 us)
Async XLA Ops:
  0.0 2.9 %copy-start = (bf16[1,64,1024]{2,1,0:T(8,128)(2,1)S(1)}, bf16[1,64,1024]{2,1,0:T(8,128)(2,1)}, u32[]{:S(2)}) copy-start(bf16[1,64,1024]{2,1,0:T(8,128)(2,1)} %param.4) | copy-start | bytes 393220
  0.0 5.3 %copy-start.1 = (bf16[1,64,1024]{2,1,0:T(8,128)(2,1)S(1)}, bf16[1,64,1024]{2,1,0:T(8,128)(2,1)}, u32[]{:S(2)}) copy-start(bf16[1,64,1024]{2,1,0:T(8,128)(2,1)} %param.5) | copy-start | bytes 393220
  67.4 1.2 %copy-start.2 = (f32[256,8,8]{1,2,0:T(8,128)S(1)}, f32[256,8,8]{1,2,0:T(8,128)}, u32[]{:S(2)}) copy-start(f32[256,8,8]{1,2,0:T(8,128)} %get-tuple-element.18) | copy-start | bytes 196612

commit v6 on v5

--- a/solution.py
+++ b/solution.py
@@ -70,26 +70,27 @@
     key_heads = keys.reshape(block_len, heads_kv, DH)
     value_heads = values.reshape(block_len, heads_kv, DH)
 
+    query_rows = to_dest(query_heads, ctx, heads_kv)
+    chunk = query_rows.shape[1]
+    by_head = query_rows.reshape(heads_kv, -1, DH)
     logits = jnp.einsum(
-        "cjgd,ijd->cjgi", query_heads, key_heads, preferred_element_type=jnp.float32
+        "jpd,ijd->jpi", by_head, key_heads, preferred_element_type=jnp.float32
     ) / math.sqrt(DH)
     weights, entropy = softmax_terms(logits)
     rounded = weights.astype(jnp.bfloat16)
     key_mix = jnp.einsum(
-        "cjgi,ijd->cjgd", rounded, key_heads, preferred_element_type=jnp.float32
+        "jpi,ijd->jpd", rounded, key_heads, preferred_element_type=jnp.float32
     ).astype(jnp.bfloat16)
 
-    query_rows = to_dest(query_heads, ctx, heads_kv)
-    chunk = query_rows.shape[1]
     key_rows = jnp.repeat(jnp.swapaxes(key_heads, 0, 1), repeat, axis=0)
     value_rows = jnp.repeat(jnp.swapaxes(value_heads, 0, 1), repeat, axis=0)
     payload = jnp.concatenate(
         [
             query_rows,
-            to_dest(key_mix, ctx, heads_kv),
+            key_mix.reshape(ctx, chunk, DH),
             key_rows,
             value_rows,
-            entropy_rows(to_dest(entropy, ctx, heads_kv)),
+            entropy_rows(entropy.reshape(ctx, chunk)),
         ],
         axis=1,
     )
@@ -128,8 +129,11 @@
 
 def make_local(ctx):
     def local(queries, key_states, value_states):
-        keys = lax.all_gather(key_states, "head", axis=1, tiled=True)
-        values = lax.all_gather(value_states, "head", axis=1, tiled=True)
+        both = lax.all_gather(
+            jnp.concatenate([key_states, value_states], axis=2), "head", axis=1, tiled=True
+        )
+        width = key_states.shape[2]
+        keys, values = both[:, :, :width], both[:, :, width:]
         return jnp.stack(
             [
                 one_sequence(queries[s], keys[s], values[s], ctx)

time: 88.1 us -> 85.8 us (0.974)
  blocking collectives: 66.5 us -> 64.9 us
    unnamed x11 -> x10, local copies, waits for them, and re-layouts: 1.08 us -> 3.63 us
    all_gather x2 -> x1, blocking collectives: 4.08 us -> 2.26 us  [local(): lax.all_gather(jnp.concatenate([key_states, value_states], axis=2), 'head...]
    reduce_sum x2, other arithmetic: 1.98 us -> 0.75 us  [softmax_terms(): jax.nn.logsumexp(logits, axis=-1) - jnp.sum(weights * logits, axis=-1)]
    another operation x1 -> x2, local copies, waits for them, and re-layouts: 1.45 us -> 0.36 us  [the longest x1 0.18 us: one_sequence(): value_heads = values.reshape(block_len, heads_kv, DH)]
    concatenate x1, other arithmetic: 0.01 us -> 1.04 us  [local(): jnp.concatenate([key_states, value_states], axis=2)]
    another operation x2, local copies, waits for them, and re-layouts: 1.48 us -> 0.55 us  [to_dest(): shaped = rows.reshape((repeat, place_count // repeat) + rows.shape[1:])]
where the time goes in v6:
time: 85.8 us; the launch traced here: 85.5 us
  blocking collectives  64.9 us (76%)
  matrix products  10 us (12%)
  local copies, waits for them, and re-layouts  7.77 us (9%)
  other arithmetic  2.54 us (3%)
    all_to_all x2, blocking collectives, exchange(): return lax.all_to_all(grid, 'ctx', split_axis=0, concat_axis=0, tiled=True)  62.7 us
    sub x2, matrix products, left_step(): weights = jax.nn.softmax(logits, axis=-1)  5.41 us
    unnamed x10, local copies, waits for them, and re-layouts  3.63 us
    all_gather x1, blocking collectives, local(): lax.all_gather(jnp.concatenate([key_states, value_states], axis=2), 'head...  2.26 us

profile of v6, /device:TPU:0, one launch (start us, length us, event | category | flops | bytes accessed | tf_op | source)
XLA Modules:
  0.0 85.5 jit_solution(44494453286367736)
XLA Ops:
  0.0 0.0 copy-start
  0.0 1.0 %pad_maximum_fusion = bf16[1,64,2048]{2,1,0:T(8,128)(2,1)S(1)} fusion(bf16[1,64,1024]{2,1,0:T(8,128)(2,1)} %param.5, bf16[1,64,1024]{2,1,0:T(8,128)(2,1)} %param.4), kind=kLoop, calls=%fused_computation.49 | loop fusion | flops 524288 | bytes 524288 | tf_op jit(solution)/shard_map/concatenate | solution.py:133
  1.0 2.3 %all_gather.3 = bf16[1,128,2048]{2,1,0:T(8,128)(2,1)S(1)} all-gather(bf16[1,64,2048]{2,1,0:T(8,128)(2,1)S(1)} %pad_maximum_fusion), channel_id=1, replica_groups=mesh['grp'=2,'ctx'=8,'head'=2] {'head'}, dimensions={1}, use_global_device_ids=true | all-gather | bytes 786432 | tf_op jit(solution)/shard_map/all_gather | solution.py:132
  3.4 0.2 copy.58
  3.5 0.0 copy-done
  3.5 0.4 reshape_reshape_squeeze.3
  3.9 0.2 copy.29
  4.1 0.9 %constant_dynamic-update-slice_fusion = bf16[8,774,128]{2,1,0:T(8,128)(2,1)} fusion(bf16[8,256,128]{2,1,0:T(8,128)(2,1)S(1)} %bitcast.42), kind=kLoop, calls=%fused_computation.62 | loop fusion | bytes 1048576
  5.0 0.4 fusion.44
  5.4 0.2 copy.34
  5.6 0.2 fusion.14
  5.7 0.4 exponential_reduce_fusion.1
  6.2 1.2 %fusion.10 = bf16[8,774,128]{2,1,0:T(8,128)(2,1)} fusion(bf16[8,774,128]{2,1,0:T(8,128)(2,1)} %constant_dynamic-update-slice_fusion, bf16[128,8,128]{0,2,1:T(8,128)(2,1)S(1)} %bitcast.46, f32[8,256,128]{1,2,0:T(8,128)S(1)} %get-tuple-element.16, f32[8,256]{1,0:T(8,128)S(1)} %fusion.14, f32[8,256]{1,0:T(8,128)S(1)} %get-tuple-element.15), kind=kOutput, calls=%fused_computation.19 | convolution fusion | flops 68157440 | bytes 1851392 | tf_op jit(solution)/shard_map/jpi,ijd->jpd/dot_general | solution.py:81
  7.4 0.2 copy.59
  7.5 0.2 copy.36
  7.7 0.8 bitcast_dynamic-update-slice_fusion.1
  8.5 0.8 bitcast_dynamic-update-slice_fusion
  9.2 0.6 copy_dynamic-update-slice_fusion
  9.8 45.6 %all_to_all.10 = bf16[8,774,128]{2,1,0:T(8,128)(2,1)S(1)} all-to-all(bf16[8,774,128]{2,1,0:T(8,128)(2,1)} %copy_dynamic-update-slice_fusion), channel_id=1, replica_groups=mesh['grp'=2,'ctx'=8,'head'=2] {'ctx'}, dimensions={0} | all-to-all | bytes 3170304 | tf_op jit(solution)/shard_map/all_to_all | solution.py:36
  55.5 0.1 copy.40
  55.6 0.9 %fusion.42 = (bf16[8,256,128]{2,1,0:T(8,128)(2,1)S(1)}, bf16[8,256,128]{2,1,0:T(8,128)(2,1)}) fusion(bf16[8,774,128]{2,1,0:T(8,128)(2,1)S(1)} %all_to_all.10), kind=kLoop, calls=%fused_computation.73 | loop fusion | bytes 2097152 | tf_op jit(solution)/shard_map/slice | solution.py:98
  56.5 2.2 %fusion.45 = (f32[256,8]{1,0:T(8,128)S(1)}, f32[256,8,8]{1,2,0:T(8,128)S(1)}) fusion(bf16[8,256,128]{2,1,0:T(8,128)(2,1)} %get-tuple-element.12, f32[256,8]{1,0:T(8,128)S(1)} %copy.40, bf16[8,256,128]{2,1,0:T(8,128)(2,1)S(1)} %get-tuple-element.11), kind=kOutput, calls=%fused_computation.76 | convolution fusion | flops 4259847 | bytes 1130496 | tf_op jit(solution)/shard_map/sub | solution.py:44
  58.7 0.4 fusion.31
  59.1 0.6 fusion.11
  59.7 0.3 fusion.46
  60.1 0.2 fusion.16
  60.3 0.4 exponential_reduce_fusion
  60.7 0.1 copy.47
  60.8 1.2 %convolution_convert_fusion.1 = bf16[8,256,128]{2,1,0:T(8,128)(2,1)} fusion(bf16[8,774,128]{2,1,0:T(8,128)(2,1)S(1)} %all_to_all.10, f32[8,256,128]{1,2,0:T(8,128)S(1)} %get-tuple-element.20, f32[8,256]{1,0:T(8,128)S(1)} %fusion.16, f32[8,256]{1,0:T(8,128)S(1)} %get-tuple-element.19), kind=kOutput, calls=%fused_computation.16 | convolution fusion | flops 68157440 | bytes 1851392 | tf_op jit(solution)/shard_map/lpi,lid->lpd/dot_general | solution.py:116
  62.0 3.2 %fusion.47 = (f32[256,8]{1,0:T(8,128)S(1)}, f32[256,8,8]{1,2,0:T(8,128)}) fusion(bf16[8,256,128]{2,1,0:T(8,128)(2,1)} %convolution_convert_fusion.1, f32[256,8]{1,0:T(8,128)S(1)} %copy.47, bf16[8,256,128]{2,1,0:T(8,128)(2,1)S(1)} %get-tuple-element.11), kind=kOutput, calls=%fused_computation.78 | convolution fusion | flops 4259847 | bytes 1130496 | tf_op jit(solution)/shard_map/sub | solution.py:44
  65.2 0.0 copy-start.1
  65.2 0.4 convolution_convert_fusion.2
  65.5 0.8 copy-done.1
  66.4 0.6 fusion.12
  67.0 0.1 copy.50
  67.1 17.0 %all_to_all.11 = bf16[8,256,128]{2,1,0:T(8,128)(2,1)S(1)} all-to-all(bf16[8,256,128]{2,1,0:T(8,128)(2,1)S(1)} %copy.50), channel_id=1, replica_groups=mesh['grp'=2,'ctx'=8,'head'=2] {'ctx'}, dimensions={0} | all-to-all | bytes 1048576 | tf_op jit(solution)/shard_map/all_to_all | solution.py:36
  84.1 0.2 copy.51
  84.3 1.2 %stack_reshape.3 = bf16[1,64,4096]{2,1,0:T(8,128)(2,1)} reshape(bf16[1,64,8,4,128]{4,3,2,1,0:T(4,128)(2,1)S(1)} %copy.51) | data formatting | bytes 1048576 | tf_op jit(solution)/shard_map/stack;reshape | solution.py:137
  (12 shorter events, 0.1 us)
Async XLA Ops:
  0.0 3.5 %copy-start = (bf16[1,64,4096]{2,1,0:T(8,128)(2,1)S(1)}, bf16[1,64,4096]{2,1,0:T(8,128)(2,1)}, u32[]{:S(2)}) copy-start(bf16[1,64,4096]{2,1,0:T(8,128)(2,1)} %param.3) | copy-start | bytes 1572868
  65.2 1.2 %copy-start.1 = (f32[256,8,8]{1,2,0:T(8,128)S(1)}, f32[256,8,8]{1,2,0:T(8,128)}, u32[]{:S(2)}) copy-start(f32[256,8,8]{1,2,0:T(8,128)} %get-tuple-element.22) | copy-start | bytes 196612

commit v7 on v6

--- a/solution.py
+++ b/solution.py
@@ -61,14 +61,13 @@
     return shaped.reshape(place_count, -1)
 
 
-def one_sequence(queries, keys, values, ctx):
+def one_sequence(queries, keys, own_keys, own_values, ctx):
     place_count, feature_width = queries.shape
     block_len = keys.shape[0]
     heads_kv = keys.shape[1] // DH
     repeat = ctx // heads_kv
     query_heads = queries.reshape(place_count, heads_kv, -1, DH)
     key_heads = keys.reshape(block_len, heads_kv, DH)
-    value_heads = values.reshape(block_len, heads_kv, DH)
 
     query_rows = to_dest(query_heads, ctx, heads_kv)
     chunk = query_rows.shape[1]
@@ -82,8 +81,13 @@
         "jpi,ijd->jpd", rounded, key_heads, preferred_element_type=jnp.float32
     ).astype(jnp.bfloat16)
 
-    key_rows = jnp.repeat(jnp.swapaxes(key_heads, 0, 1), repeat, axis=0)
-    value_rows = jnp.repeat(jnp.swapaxes(value_heads, 0, 1), repeat, axis=0)
+    own_len = own_keys.shape[0]
+    key_rows = jnp.repeat(
+        jnp.swapaxes(own_keys.reshape(own_len, heads_kv, DH), 0, 1), repeat, axis=0
+    )
+    value_rows = jnp.repeat(
+        jnp.swapaxes(own_values.reshape(own_len, heads_kv, DH), 0, 1), repeat, axis=0
+    )
     payload = jnp.concatenate(
         [
             query_rows,
@@ -97,9 +101,12 @@
     rows = exchange(payload)
     query_grid = rows[:, :chunk]
     key_grid = rows[:, chunk : 2 * chunk]
-    block_keys = rows[:, 2 * chunk : 2 * chunk + block_len]
-    block_values = rows[:, 2 * chunk + block_len : 2 * chunk + 2 * block_len]
-    entropy_grid = entropy_from_rows(rows[:, 2 * chunk + 2 * block_len :], chunk)
+    halves = rows[:, 2 * chunk : 2 * chunk + 2 * own_len]
+    entropy_grid = entropy_from_rows(rows[:, 2 * chunk + 2 * own_len :], chunk)
+    halves = lax.all_gather(
+        halves.reshape(ctx, 2, own_len, DH), "head", axis=2, tiled=True
+    )
+    block_keys, block_values = halves[:, 0], halves[:, 1]
 
     weights, left_rounded = left_step(query_grid, key_grid, entropy_grid)
     column_mass = jnp.transpose(jnp.sum(weights, axis=1), (1, 0))
@@ -129,14 +136,10 @@
 
 def make_local(ctx):
     def local(queries, key_states, value_states):
-        both = lax.all_gather(
-            jnp.concatenate([key_states, value_states], axis=2), "head", axis=1, tiled=True
-        )
-        width = key_states.shape[2]
-        keys, values = both[:, :, :width], both[:, :, width:]
+        keys = lax.all_gather(key_states, "head", axis=1, tiled=True)
         return jnp.stack(
             [
-                one_sequence(queries[s], keys[s], values[s], ctx)
+                one_sequence(queries[s], keys[s], key_states[s], value_states[s], ctx)
                 for s in range(queries.shape[0])
             ]
         )

time: 85.8 us -> 76.2 us (0.89)
  local copies, waits for them, and re-layouts: 7.77 us -> 4.12 us
  blocking collectives: 64.9 us -> 61.5 us
  matrix products: 10 us -> 8.51 us
  other arithmetic: 2.54 us -> 1.5 us
    all_to_all x2, blocking collectives: 62.7 us -> 57.3 us  [exchange(): return lax.all_to_all(grid, 'ctx', split_axis=0, concat_axis=0, tiled=True)]
    unnamed x10, local copies, waits for them, and re-layouts: 3.63 us -> 0.5 us
    all_gather x1 -> x2, blocking collectives: 2.26 us -> 4.27 us  [the longest x1 2.18 us: one_sequence(): lax.all_gather(halves.reshape(ctx, 2, own_len, DH), 'head', axis=2, tiled...]
    another operation x2, local copies, waits for them, and re-layouts: 0.55 us -> 1.62 us  [to_dest(): shaped = rows.reshape((repeat, place_count // repeat) + rows.shape[1:])]
    concatenate x1 -> x0, other arithmetic: 1.04 us -> none  [local(): jnp.concatenate([key_states, value_states], axis=2)]
where the time goes in v7:
time: 76.2 us; the launch traced here: 75.9 us
  blocking collectives  61.5 us (81%)
  matrix products  8.51 us (11%)
  local copies, waits for them, and re-layouts  4.12 us (5%)
  other arithmetic  1.5 us (2%)
    all_to_all x2, blocking collectives, exchange(): return lax.all_to_all(grid, 'ctx', split_axis=0, concat_axis=0, tiled=True)  57.3 us
    sub x2, matrix products, left_step(): weights = jax.nn.softmax(logits, axis=-1)  5.46 us
    all_gather x1, blocking collectives, one_sequence(): lax.all_gather(halves.reshape(ctx, 2, own_len, DH), 'head', axis=2, tiled...  2.18 us
    all_gather x1, blocking collectives, local(): keys = lax.all_gather(key_states, 'head', axis=1, tiled=True)  2.09 us
    another operation x2, local copies, waits for them, and re-layouts, to_dest(): shaped = rows.reshape((repeat, place_count // repeat) + rows.shape[1:])  1.62 us

profile of v7, /device:TPU:0, one launch (start us, length us, event | category | flops | bytes accessed | tf_op | source)
XLA Modules:
  0.0 75.9 jit_solution(12552882311452885520)
XLA Ops:
  0.0 0.0 copy-start
  0.0 1.4 %reshape_reshape_squeeze.3 = bf16[1,64,8,4,128]{4,3,2,1,0:T(4,128)(2,1)S(1)} reshape(bf16[1,64,4096]{2,1,0:T(8,128)(2,1)} %param.3) | data formatting | bytes 1048576 | tf_op jit(solution)/shard_map/reshape;reshape;squeeze | solution.py:51
  1.4 0.2 copy.30
  1.7 0.0 copy-done
  1.7 2.1 %all_gather.6 = bf16[1,128,1024]{2,1,0:T(8,128)(2,1)S(1)} all-gather(bf16[1,64,1024]{2,1,0:T(8,128)(2,1)S(1)} %copy-done), channel_id=1, replica_groups=mesh['grp'=2,'ctx'=8,'head'=2] {'head'}, dimensions={1}, use_global_device_ids=true | all-gather | bytes 393216 | tf_op jit(solution)/shard_map/all_gather | solution.py:139
  3.8 0.2 copy.31
  3.9 0.0 copy-start.1
  4.0 0.4 fusion.39
  4.3 0.2 fusion.13
  4.5 0.3 copy-done.1
  4.9 0.5 fusion.9
  5.3 0.4 exponential_reduce_fusion.1
  5.9 39.8 %all_to_all.10 = bf16[8,646,128]{2,1,0:T(8,128)(2,1)S(1)} all-to-all(bf16[8,646,128]{2,1,0:T(8,128)(2,1)S(1)} %copy_dynamic-update-slice_fusion), channel_id=1, replica_groups=mesh['grp'=2,'ctx'=8,'head'=2] {'ctx'}, dimensions={0} | all-to-all | bytes 2646016 | tf_op jit(solution)/shard_map/all_to_all | solution.py:36
  45.7 2.2 %all_gather.7 = bf16[8,2,128,128]{3,2,0,1:T(8,128)(2,1)S(1)} all-gather(bf16[8,2,64,128]{3,2,0,1:T(8,128)(2,1)S(1)} %copy.42), channel_id=1, replica_groups=mesh['grp'=2,'ctx'=8,'head'=2] {'head'}, dimensions={2}, use_global_device_ids=true | all-gather | bytes 786432 | tf_op jit(solution)/shard_map/all_gather | solution.py:106
  47.9 0.1 copy.40
  48.1 0.1 fusion.38
  48.2 2.7 %fusion.40 = (f32[256,8]{1,0:T(8,128)S(1)}, f32[256,8,8]{1,2,0:T(8,128)S(1)}) fusion(bf16[8,256,128]{2,1,0:T(8,128)(2,1)S(1)} %get-tuple-element.12, f32[256,8]{1,0:T(8,128)S(1)} %copy.40, bf16[8,256,128]{2,1,0:T(8,128)(2,1)S(1)} %get-tuple-element.11), kind=kOutput, calls=%fused_computation.72 | convolution fusion | flops 4259847 | bytes 1130496 | tf_op jit(solution)/shard_map/sub | solution.py:44
  50.9 0.4 fusion.30
  51.3 0.6 fusion.10
  51.9 0.3 fusion.41
  52.3 0.2 fusion.15
  52.4 0.4 convolution_convert_fusion.1
  52.8 0.4 convolution_convert_fusion.2
  53.2 0.4 exponential_reduce_fusion
  53.6 0.1 copy.48
  53.7 2.7 %fusion.42 = (f32[256,8]{1,0:T(8,128)S(1)}, f32[256,8,8]{1,2,0:T(8,128)S(1)}) fusion(bf16[8,256,128]{2,1,0:T(8,128)(2,1)S(1)} %convolution_convert_fusion.1, f32[256,8]{1,0:T(8,128)S(1)} %copy.48, bf16[8,256,128]{2,1,0:T(8,128)(2,1)S(1)} %get-tuple-element.11), kind=kOutput, calls=%fused_computation.74 | convolution fusion | flops 4259847 | bytes 1130496 | tf_op jit(solution)/shard_map/sub | solution.py:44
  56.4 0.6 fusion.11
  57.0 0.1 copy.51
  57.1 17.5 %all_to_all.11 = bf16[8,256,128]{2,1,0:T(8,128)(2,1)S(1)} all-to-all(bf16[8,256,128]{2,1,0:T(8,128)(2,1)S(1)} %copy.51), channel_id=1, replica_groups=mesh['grp'=2,'ctx'=8,'head'=2] {'ctx'}, dimensions={0} | all-to-all | bytes 1048576 | tf_op jit(solution)/shard_map/all_to_all | solution.py:36
  74.6 0.2 copy.52
  74.7 1.2 %stack_reshape.3 = bf16[1,64,4096]{2,1,0:T(8,128)(2,1)} reshape(bf16[1,64,8,4,128]{4,3,2,1,0:T(4,128)(2,1)S(1)} %copy.52) | data formatting | bytes 1048576 | tf_op jit(solution)/shard_map/stack;reshape | solution.py:140
  (19 shorter events, 0.3 us)
Async XLA Ops:
  0.0 1.7 %copy-start = (bf16[1,64,1024]{2,1,0:T(8,128)(2,1)S(1)}, bf16[1,64,1024]{2,1,0:T(8,128)(2,1)}, u32[]{:S(2)}) copy-start(bf16[1,64,1024]{2,1,0:T(8,128)(2,1)} %param.4) | copy-start | bytes 393220
  3.9 0.9 %copy-start.1 = (bf16[1,64,1024]{2,1,0:T(8,128)(2,1)S(1)}, bf16[1,64,1024]{2,1,0:T(8,128)(2,1)}, u32[]{:S(2)}) copy-start(bf16[1,64,1024]{2,1,0:T(8,128)(2,1)} %param.5) | copy-start | bytes 393220

commit v8 on v7

--- a/solution.py
+++ b/solution.py
@@ -49,15 +49,15 @@
     place_count, group = rows.shape[0], rows.shape[2]
     repeat = ctx // heads_kv
     shaped = rows.reshape((repeat, place_count // repeat) + rows.shape[1:])
-    shaped = jnp.moveaxis(shaped, 2, 0)
+    shaped = jnp.moveaxis(shaped, (2, 0, 3), (0, 1, 2))
     return shaped.reshape((ctx, place_count // repeat * group) + rows.shape[3:])
 
 
 def from_dest(grid, place_count, heads_kv):
     ctx = grid.shape[0]
     repeat = ctx // heads_kv
-    shaped = grid.reshape(heads_kv, repeat, place_count // repeat, -1, DH)
-    shaped = jnp.moveaxis(shaped, 0, 2)
+    shaped = grid.reshape(heads_kv, repeat, -1, place_count // repeat, DH)
+    shaped = jnp.moveaxis(shaped, (0, 1, 2), (2, 0, 3))
     return shaped.reshape(place_count, -1)
 
 
@@ -103,8 +103,11 @@
     key_grid = rows[:, chunk : 2 * chunk]
     halves = rows[:, 2 * chunk : 2 * chunk + 2 * own_len]
     entropy_grid = entropy_from_rows(rows[:, 2 * chunk + 2 * own_len :], chunk)
-    halves = lax.all_gather(
-        halves.reshape(ctx, 2, own_len, DH), "head", axis=2, tiled=True
+    mine = halves.reshape(ctx, 2, own_len, DH)
+    other = lax.ppermute(mine, "head", [(0, 1), (1, 0)])
+    first = lax.axis_index("head") == 0
+    halves = jnp.concatenate(
+        [jnp.where(first, mine, other), jnp.where(first, other, mine)], axis=2
     )
     block_keys, block_values = halves[:, 0], halves[:, 1]
 

time: 76.2 us -> 78.4 us (1.029)
  blocking collectives: 61.5 us -> 20.6 us
  waiting for transfers between devices: 0 us -> 32.1 us
  starting transfers between devices: 0 us -> 7.23 us
  local copies, waits for them, and re-layouts: 4.12 us -> 7.15 us
    all_to_all x2 -> x1, blocking collectives: 57.3 us -> 18.6 us  [exchange(): return lax.all_to_all(grid, 'ctx', split_axis=0, concat_axis=0, tiled=True)]
    all_to_all x0 -> x1, waiting for transfers between devices: none -> 32 us  [exchange(): return lax.all_to_all(grid, 'ctx', split_axis=0, concat_axis=0, tiled=True)]
    all_to_all x0 -> x1, starting transfers between devices: none -> 7.16 us  [exchange(): return lax.all_to_all(grid, 'ctx', split_axis=0, concat_axis=0, tiled=True)]
    unnamed x10, local copies, waits for them, and re-layouts: 0.5 us -> 2.69 us
    all_gather x1 -> x0, blocking collectives: 2.18 us -> none  [one_sequence(): lax.all_gather(halves.reshape(ctx, 2, own_len, DH), 'head', axis=2, tiled...]
  transfers between devices with their start and end apart: 0 -> 2, of which waited for: 0 -> 1; matrix products, arithmetic and copies ran while one was open for 0% -> 5% of each run, Pallas kernels for 0% -> 0%
where the time goes in v8:
time: 78.4 us; the launch traced here: 78.1 us
  waiting for transfers between devices  32.1 us (41%)
  blocking collectives  20.6 us (26%)
  matrix products  9.24 us (12%)
  starting transfers between devices  7.23 us (9%)
  local copies, waits for them, and re-layouts  7.15 us (9%)
  other arithmetic  1.53 us (2%)
    all_to_all x1, waiting for transfers between devices, exchange(): return lax.all_to_all(grid, 'ctx', split_axis=0, concat_axis=0, tiled=True)  32 us
    all_to_all x1, blocking collectives, exchange(): return lax.all_to_all(grid, 'ctx', split_axis=0, concat_axis=0, tiled=True)  18.6 us
    all_to_all x1, starting transfers between devices, exchange(): return lax.all_to_all(grid, 'ctx', split_axis=0, concat_axis=0, tiled=True)  7.16 us
    sub x2, matrix products, left_step(): weights = jax.nn.softmax(logits, axis=-1)  5.46 us
    unnamed x10, local copies, waits for them, and re-layouts  2.69 us
    all_gather x1, blocking collectives, local(): keys = lax.all_gather(key_states, 'head', axis=1, tiled=True)  2.07 us
    another operation x2, local copies, waits for them, and re-layouts, to_dest(): shaped = rows.reshape((repeat, place_count // repeat) + rows.shape[1:])  1.64 us
  transfers between devices with their start and end apart: 2, of which 1 were waited for; matrix products, arithmetic and copies ran while one was open for 5% of the time, Pallas kernels for 0%

profile of v8, /device:TPU:0, one launch (start us, length us, event | category | flops | bytes accessed | tf_op | source)
XLA Modules:
  0.0 78.1 jit_solution(15123921077033722871)
XLA Ops:
  0.0 0.0 copy-start
  0.0 1.4 %reshape_reshape_squeeze.3 = bf16[1,64,8,4,128]{4,3,2,1,0:T(4,128)(2,1)S(1)} reshape(bf16[1,64,4096]{2,1,0:T(8,128)(2,1)} %param.3) | data formatting | bytes 1048576 | tf_op jit(solution)/shard_map/reshape;reshape;squeeze | solution.py:51
  1.4 0.2 copy.34
  1.7 0.9 %constant_dynamic-update-slice_fusion = bf16[8,646,128]{2,1,0:T(8,128)(2,1)} fusion(bf16[8,256,128]{2,1,0:T(8,128)(2,1)S(1)} %bitcast.55), kind=kLoop, calls=%fused_computation.66 | loop fusion | bytes 1048576
  2.6 0.0 copy-done
  2.6 2.1 %all_gather.3 = bf16[1,128,1024]{2,1,0:T(8,128)(2,1)S(1)} all-gather(bf16[1,64,1024]{2,1,0:T(8,128)(2,1)S(1)} %copy-done), channel_id=1, replica_groups=mesh['grp'=2,'ctx'=8,'head'=2] {'head'}, dimensions={1}, use_global_device_ids=true | all-gather | bytes 393216 | tf_op jit(solution)/shard_map/all_gather | solution.py:142
  4.7 0.2 copy.35
  4.8 0.0 copy-start.1
  4.8 0.4 fusion.47
  5.2 0.2 fusion.13
  5.4 0.3 copy-done.1
  5.8 1.2 %fusion.9 = bf16[8,646,128]{2,1,0:T(8,128)(2,1)} fusion(bf16[8,646,128]{2,1,0:T(8,128)(2,1)} %constant_dynamic-update-slice_fusion, bf16[128,8,128]{0,2,1:T(8,128)(2,1)S(1)} %bitcast.61, f32[8,256,128]{1,2,0:T(8,128)S(1)} %get-tuple-element.16, f32[8,256]{1,0:T(8,128)S(1)} %fusion.13, f32[8,256]{1,0:T(8,128)S(1)} %get-tuple-element.15), kind=kOutput, calls=%fused_computation.18 | convolution fusion | flops 68157440 | bytes 1851392 | tf_op jit(solution)/shard_map/jpi,ijd->jpd/dot_general | solution.py:80
  7.0 0.4 exponential_reduce_fusion.1
  7.4 0.7 bitcast_dynamic-update-slice_fusion.1
  8.1 0.7 bitcast_dynamic-update-slice_fusion
  8.8 0.6 copy_dynamic-update-slice_fusion
  9.4 7.2 %all-to-all-start = ((bf16[8,646,128]{2,1,0:T(8,128)(2,1)}), bf16[8,646,128]{2,1,0:T(8,128)(2,1)S(1)}, u32[]{:S(2)}, u32[]{:S(2)}) async-start(bf16[8,646,128]{2,1,0:T(8,128)(2,1)} %copy_dynamic-update-slice_fusion), calls=%async_computation | async-start | bytes 2654208 | tf_op jit(solution)/shard_map/all_to_all | solution.py:36
  16.5 32.0 %all-to-all-done = bf16[8,646,128]{2,1,0:T(8,128)(2,1)S(1)} async-done(((bf16[8,646,128]{2,1,0:T(8,128)(2,1)}), bf16[8,646,128]{2,1,0:T(8,128)(2,1)S(1)}, u32[]{:S(2)}, u32[]{:S(2)}) %all-to-all-start) | async-done | bytes 1323040 | tf_op jit(solution)/shard_map/all_to_all | solution.py:36
  48.6 0.1 collective-permute-start
  48.8 0.1 copy.44
  48.9 0.1 fusion.46
  49.0 2.7 %fusion.48 = (f32[256,8]{1,0:T(8,128)S(1)}, f32[256,8,8]{1,2,0:T(8,128)S(1)}) fusion(bf16[8,256,128]{2,1,0:T(8,128)(2,1)S(1)} %get-tuple-element.12, f32[256,8]{1,0:T(8,128)S(1)} %copy.44, bf16[8,256,128]{2,1,0:T(8,128)(2,1)S(1)} %get-tuple-element.11), kind=kOutput, calls=%fused_computation.80 | convolution fusion | flops 4259847 | bytes 1130496 | tf_op jit(solution)/shard_map/sub | solution.py:44
  51.7 0.4 fusion.30
  52.1 0.6 fusion.10
  52.7 0.0 collective-permute-done
  52.8 0.3 fusion.49
  53.1 0.2 fusion.15
  53.3 0.4 convolution_convert_fusion.1
  53.7 0.4 convolution_convert_fusion.2
  54.0 0.4 exponential_reduce_fusion
  54.4 0.1 copy.54
  54.6 2.7 %fusion.50 = (f32[256,8]{1,0:T(8,128)S(1)}, f32[256,8,8]{1,2,0:T(8,128)S(1)}) fusion(bf16[8,256,128]{2,1,0:T(8,128)(2,1)S(1)} %convolution_convert_fusion.1, f32[256,8]{1,0:T(8,128)S(1)} %copy.54, bf16[8,256,128]{2,1,0:T(8,128)(2,1)S(1)} %get-tuple-element.11), kind=kOutput, calls=%fused_computation.82 | convolution fusion | flops 4259847 | bytes 1130496 | tf_op jit(solution)/shard_map/sub | solution.py:44
  57.3 0.6 fusion.11
  57.9 0.1 copy.57
  58.0 18.6 %all_to_all.10 = bf16[8,256,128]{2,1,0:T(8,128)(2,1)S(1)} all-to-all(bf16[8,256,128]{2,1,0:T(8,128)(2,1)S(1)} %copy.57), channel_id=1, replica_groups=mesh['grp'=2,'ctx'=8,'head'=2] {'ctx'}, dimensions={0} | all-to-all | bytes 1048576 | tf_op jit(solution)/shard_map/all_to_all | solution.py:36
  76.5 0.4 copy.58
  76.9 1.2 %stack_reshape.3 = bf16[1,64,4096]{2,1,0:T(8,128)(2,1)} reshape(bf16[1,64,8,4,128]{4,3,2,1,0:T(4,128)(2,1)S(1)} %copy.58) | data formatting | bytes 1048576 | tf_op jit(solution)/shard_map/stack;reshape | solution.py:143
  (16 shorter events, 0.2 us)
Async XLA Ops:
  0.0 2.6 %copy-start = (bf16[1,64,1024]{2,1,0:T(8,128)(2,1)S(1)}, bf16[1,64,1024]{2,1,0:T(8,128)(2,1)}, u32[]{:S(2)}) copy-start(bf16[1,64,1024]{2,1,0:T(8,128)(2,1)} %param.4) | copy-start | bytes 393220
  4.8 0.9 %copy-start.1 = (bf16[1,64,1024]{2,1,0:T(8,128)(2,1)S(1)}, bf16[1,64,1024]{2,1,0:T(8,128)(2,1)}, u32[]{:S(2)}) copy-start(bf16[1,64,1024]{2,1,0:T(8,128)(2,1)} %param.5) | copy-start | bytes 393220
  9.4 39.2 %all-to-all-start = ((bf16[8,646,128]{2,1,0:T(8,128)(2,1)}), bf16[8,646,128]{2,1,0:T(8,128)(2,1)S(1)}, u32[]{:S(2)}, u32[]{:S(2)}) async-start(bf16[8,646,128]{2,1,0:T(8,128)(2,1)} %copy_dynamic-update-slice_fusion), calls=%async_computation | async-start | bytes 2654208 | tf_op jit(solution)/shard_map/all_to_all | solution.py:36
  48.6 4.1 %collective-permute-start = (bf16[8,2,64,128]{3,2,0,1:T(8,128)(2,1)S(1)}, bf16[8,2,64,128]{3,2,0,1:T(8,128)(2,1)S(1)}, u32[]{:S(2)}, u32[]{:S(2)}) collective-permute-start(bf16[8,2,64,128]{3,2,0,1:T(8,128)(2,1)S(1)} %copy.47), channel_id=1, source_target_pairs={{0,1},{1,0},{2,3},{3,2},{4,5},{5,4},{6,7},{7,6},{8,9},{9,8},{10,11... | collective-permute-start | bytes 786440 | tf_op jit(solution)/shard_map/ppermute | solution.py:107

commit v9 on v8

--- a/solution.py
+++ b/solution.py
@@ -49,15 +49,15 @@
     place_count, group = rows.shape[0], rows.shape[2]
     repeat = ctx // heads_kv
     shaped = rows.reshape((repeat, place_count // repeat) + rows.shape[1:])
-    shaped = jnp.moveaxis(shaped, (2, 0, 3), (0, 1, 2))
+    shaped = jnp.moveaxis(shaped, 2, 0)
     return shaped.reshape((ctx, place_count // repeat * group) + rows.shape[3:])
 
 
 def from_dest(grid, place_count, heads_kv):
     ctx = grid.shape[0]
     repeat = ctx // heads_kv
-    shaped = grid.reshape(heads_kv, repeat, -1, place_count // repeat, DH)
-    shaped = jnp.moveaxis(shaped, (0, 1, 2), (2, 0, 3))
+    shaped = grid.reshape(heads_kv, repeat, place_count // repeat, -1, DH)
+    shaped = jnp.moveaxis(shaped, 0, 2)
     return shaped.reshape(place_count, -1)
 
 

time: 78.4 us -> 78.1 us (level)
  no operation moved by 1% of the time
where the time goes in v9:
time: 78.1 us; the launch traced here: 77.9 us
  waiting for transfers between devices  32.1 us (41%)
  blocking collectives  20.6 us (26%)
  matrix products  9.24 us (12%)
  starting transfers between devices  7.23 us (9%)
  local copies, waits for them, and re-layouts  6.9 us (9%)
  other arithmetic  1.53 us (2%)
    all_to_all x1, waiting for transfers between devices, exchange(): return lax.all_to_all(grid, 'ctx', split_axis=0, concat_axis=0, tiled=True)  32 us
    all_to_all x1, blocking collectives, exchange(): return lax.all_to_all(grid, 'ctx', split_axis=0, concat_axis=0, tiled=True)  18.6 us
    all_to_all x1, starting transfers between devices, exchange(): return lax.all_to_all(grid, 'ctx', split_axis=0, concat_axis=0, tiled=True)  7.16 us
    sub x2, matrix products, left_step(): weights = jax.nn.softmax(logits, axis=-1)  5.46 us
    unnamed x10, local copies, waits for them, and re-layouts  2.69 us
    all_gather x1, blocking collectives, local(): keys = lax.all_gather(key_states, 'head', axis=1, tiled=True)  2.07 us
    another operation x2, local copies, waits for them, and re-layouts, to_dest(): shaped = rows.reshape((repeat, place_count // repeat) + rows.shape[1:])  1.62 us
  transfers between devices with their start and end apart: 2, of which 1 were waited for; matrix products, arithmetic and copies ran while one was open for 5% of the time, Pallas kernels for 0%

profile of v9, /device:TPU:0, one launch (start us, length us, event | category | flops | bytes accessed | tf_op | source)
XLA Modules:
  0.0 77.9 jit_solution(13360947396908995655)
XLA Ops:
  0.0 0.0 copy-start
  0.0 1.4 %reshape_reshape_squeeze.3 = bf16[1,64,8,4,128]{4,3,2,1,0:T(4,128)(2,1)S(1)} reshape(bf16[1,64,4096]{2,1,0:T(8,128)(2,1)} %param.3) | data formatting | bytes 1048576 | tf_op jit(solution)/shard_map/reshape;reshape;squeeze | solution.py:51
  1.4 0.2 copy.34
  1.6 0.9 %constant_dynamic-update-slice_fusion = bf16[8,646,128]{2,1,0:T(8,128)(2,1)} fusion(bf16[8,256,128]{2,1,0:T(8,128)(2,1)S(1)} %bitcast.55), kind=kLoop, calls=%fused_computation.66 | loop fusion | bytes 1048576
  2.6 0.0 copy-done
  2.6 2.1 %all_gather.3 = bf16[1,128,1024]{2,1,0:T(8,128)(2,1)S(1)} all-gather(bf16[1,64,1024]{2,1,0:T(8,128)(2,1)S(1)} %copy-done), channel_id=1, replica_groups=mesh['grp'=2,'ctx'=8,'head'=2] {'head'}, dimensions={1}, use_global_device_ids=true | all-gather | bytes 393216 | tf_op jit(solution)/shard_map/all_gather | solution.py:142
  4.6 0.2 copy.35
  4.8 0.0 copy-start.1
  4.8 0.4 fusion.47
  5.2 0.2 fusion.13
  5.4 0.3 copy-done.1
  5.7 1.2 %fusion.9 = bf16[8,646,128]{2,1,0:T(8,128)(2,1)} fusion(bf16[8,646,128]{2,1,0:T(8,128)(2,1)} %constant_dynamic-update-slice_fusion, bf16[128,8,128]{0,2,1:T(8,128)(2,1)S(1)} %bitcast.61, f32[8,256,128]{1,2,0:T(8,128)S(1)} %get-tuple-element.16, f32[8,256]{1,0:T(8,128)S(1)} %fusion.13, f32[8,256]{1,0:T(8,128)S(1)} %get-tuple-element.15), kind=kOutput, calls=%fused_computation.18 | convolution fusion | flops 68157440 | bytes 1851392 | tf_op jit(solution)/shard_map/jpi,ijd->jpd/dot_general | solution.py:80
  6.9 0.4 exponential_reduce_fusion.1
  7.4 0.7 bitcast_dynamic-update-slice_fusion.1
  8.1 0.7 bitcast_dynamic-update-slice_fusion
  8.8 0.6 copy_dynamic-update-slice_fusion
  9.4 7.2 %all-to-all-start = ((bf16[8,646,128]{2,1,0:T(8,128)(2,1)}), bf16[8,646,128]{2,1,0:T(8,128)(2,1)S(1)}, u32[]{:S(2)}, u32[]{:S(2)}) async-start(bf16[8,646,128]{2,1,0:T(8,128)(2,1)} %copy_dynamic-update-slice_fusion), calls=%async_computation | async-start | bytes 2654208 | tf_op jit(solution)/shard_map/all_to_all | solution.py:36
  16.5 32.0 %all-to-all-done = bf16[8,646,128]{2,1,0:T(8,128)(2,1)S(1)} async-done(((bf16[8,646,128]{2,1,0:T(8,128)(2,1)}), bf16[8,646,128]{2,1,0:T(8,128)(2,1)S(1)}, u32[]{:S(2)}, u32[]{:S(2)}) %all-to-all-start) | async-done | bytes 1323040 | tf_op jit(solution)/shard_map/all_to_all | solution.py:36
  48.6 0.1 collective-permute-start
  48.7 0.1 copy.44
  48.9 0.1 fusion.46
  49.0 2.7 %fusion.48 = (f32[256,8]{1,0:T(8,128)S(1)}, f32[256,8,8]{1,2,0:T(8,128)S(1)}) fusion(bf16[8,256,128]{2,1,0:T(8,128)(2,1)S(1)} %get-tuple-element.12, f32[256,8]{1,0:T(8,128)S(1)} %copy.44, bf16[8,256,128]{2,1,0:T(8,128)(2,1)S(1)} %get-tuple-element.11), kind=kOutput, calls=%fused_computation.80 | convolution fusion | flops 4259847 | bytes 1130496 | tf_op jit(solution)/shard_map/sub | solution.py:44
  51.7 0.4 fusion.30
  52.1 0.6 fusion.10
  52.7 0.0 collective-permute-done
  52.8 0.3 fusion.49
  53.1 0.2 fusion.15
  53.3 0.4 convolution_convert_fusion.1
  53.6 0.4 convolution_convert_fusion.2
  54.0 0.4 exponential_reduce_fusion
  54.4 0.1 copy.54
  54.6 2.7 %fusion.50 = (f32[256,8]{1,0:T(8,128)S(1)}, f32[256,8,8]{1,2,0:T(8,128)S(1)}) fusion(bf16[8,256,128]{2,1,0:T(8,128)(2,1)S(1)} %convolution_convert_fusion.1, f32[256,8]{1,0:T(8,128)S(1)} %copy.54, bf16[8,256,128]{2,1,0:T(8,128)(2,1)S(1)} %get-tuple-element.11), kind=kOutput, calls=%fused_computation.82 | convolution fusion | flops 4259847 | bytes 1130496 | tf_op jit(solution)/shard_map/sub | solution.py:44
  57.3 0.6 fusion.11
  57.9 0.1 copy.57
  57.9 18.6 %all_to_all.10 = bf16[8,256,128]{2,1,0:T(8,128)(2,1)S(1)} all-to-all(bf16[8,256,128]{2,1,0:T(8,128)(2,1)S(1)} %copy.57), channel_id=1, replica_groups=mesh['grp'=2,'ctx'=8,'head'=2] {'ctx'}, dimensions={0} | all-to-all | bytes 1048576 | tf_op jit(solution)/shard_map/all_to_all | solution.py:36
  76.5 0.2 copy.58
  76.7 1.2 %stack_reshape.3 = bf16[1,64,4096]{2,1,0:T(8,128)(2,1)} reshape(bf16[1,64,8,4,128]{4,3,2,1,0:T(4,128)(2,1)S(1)} %copy.58) | data formatting | bytes 1048576 | tf_op jit(solution)/shard_map/stack;reshape | solution.py:143
  (16 shorter events, 0.2 us)
Async XLA Ops:
  0.0 2.6 %copy-start = (bf16[1,64,1024]{2,1,0:T(8,128)(2,1)S(1)}, bf16[1,64,1024]{2,1,0:T(8,128)(2,1)}, u32[]{:S(2)}) copy-start(bf16[1,64,1024]{2,1,0:T(8,128)(2,1)} %param.4) | copy-start | bytes 393220
  4.8 0.9 %copy-start.1 = (bf16[1,64,1024]{2,1,0:T(8,128)(2,1)S(1)}, bf16[1,64,1024]{2,1,0:T(8,128)(2,1)}, u32[]{:S(2)}) copy-start(bf16[1,64,1024]{2,1,0:T(8,128)(2,1)} %param.5) | copy-start | bytes 393220
  9.4 39.2 %all-to-all-start = ((bf16[8,646,128]{2,1,0:T(8,128)(2,1)}), bf16[8,646,128]{2,1,0:T(8,128)(2,1)S(1)}, u32[]{:S(2)}, u32[]{:S(2)}) async-start(bf16[8,646,128]{2,1,0:T(8,128)(2,1)} %copy_dynamic-update-slice_fusion), calls=%async_computation | async-start | bytes 2654208 | tf_op jit(solution)/shard_map/all_to_all | solution.py:36
  48.6 4.1 %collective-permute-start = (bf16[8,2,64,128]{3,2,0,1:T(8,128)(2,1)S(1)}, bf16[8,2,64,128]{3,2,0,1:T(8,128)(2,1)S(1)}, u32[]{:S(2)}, u32[]{:S(2)}) collective-permute-start(bf16[8,2,64,128]{3,2,0,1:T(8,128)(2,1)S(1)} %copy.47), channel_id=1, source_target_pairs={{0,1},{1,0},{2,3},{3,2},{4,5},{5,4},{6,7},{7,6},{8,9},{9,8},{10,11... | collective-permute-start | bytes 786440 | tf_op jit(solution)/shard_map/ppermute | solution.py:107

commit v10 on v7

v10 whole, which is shorter than its diff:
```python
import math

import jax
import jax.numpy as jnp
from jax import lax
from jax.sharding import PartitionSpec as P

DH = 128


def softmax_terms(logits):
    weights = jax.nn.softmax(logits, axis=-1)
    entropy = jax.nn.logsumexp(logits, axis=-1) - jnp.sum(weights * logits, axis=-1)
    return weights, entropy


def exchange(grid):
    return lax.all_to_all(grid, "ctx", split_axis=0, concat_axis=0, tiled=True)


def left_step(query_grid, key_grid, entropy_grid):
    logits = jnp.einsum(
        "apd,lpd->pal", query_grid, key_grid, preferred_element_type=jnp.float32
    ) / math.sqrt(DH)
    logits = logits + jnp.transpose(entropy_grid, (1, 0))[:, None, :]
    weights = jax.nn.softmax(logits, axis=-1)
    return weights, weights.astype(jnp.bfloat16)


def to_dest(rows, ctx, heads_kv):
    place_count, group = rows.shape[0], rows.shape[2]
    repeat = ctx // heads_kv
    shaped = rows.reshape((repeat, place_count // repeat) + rows.shape[1:])
    shaped = jnp.moveaxis(shaped, 2, 0)
    return shaped.reshape((ctx, place_count // repeat * group) + rows.shape[3:])


def from_dest(grid, place_count, heads_kv):
    ctx = grid.shape[0]
    repeat = ctx // heads_kv
    shaped = grid.reshape(heads_kv, repeat, place_count // repeat, -1, DH)
    shaped = jnp.moveaxis(shaped, 0, 2)
    return shaped.reshape(place_count, -1)


def right_step(query_grid, block_keys):
    logits = jnp.einsum(
        "lpd,lid->lpi", query_grid, block_keys, preferred_element_type=jnp.float32
    ) / math.sqrt(DH)
    weights, entropy = softmax_terms(logits)
    rounded = weights.astype(jnp.bfloat16)
    key_mix = jnp.einsum(
        "lpi,lid->lpd", rounded, block_keys, preferred_element_type=jnp.float32
    ).astype(jnp.bfloat16)
    return rounded, entropy, key_mix


def one_sequence(queries, own_keys, own_values, ctx):
    place_count, feature_width = queries.shape
    own_len = own_keys.shape[0]
    heads_kv = own_keys.shape[1] // DH
    repeat = ctx // heads_kv
    query_rows = to_dest(queries.reshape(place_count, heads_kv, -1, DH), ctx, heads_kv)
    chunk = query_rows.shape[1]
    key_rows = jnp.repeat(
        jnp.swapaxes(own_keys.reshape(own_len, heads_kv, DH), 0, 1), repeat, axis=0
    )
    value_rows = jnp.repeat(
        jnp.swapaxes(own_values.reshape(own_len, heads_kv, DH), 0, 1), repeat, axis=0
    )
    rows = exchange(jnp.concatenate([query_rows, key_rows, value_rows], axis=1))
    query_grid = rows[:, :chunk]
    halves = lax.all_gather(
        rows[:, chunk:].reshape(ctx, 2, own_len, DH), "head", axis=2, tiled=True
    )
    block_keys, block_values = halves[:, 0], halves[:, 1]

    _, entropy_grid, key_grid = right_step(query_grid, block_keys)
    weights, left_rounded = left_step(query_grid, key_grid, entropy_grid)
    column_mass = jnp.transpose(jnp.sum(weights, axis=1), (1, 0))
    mixed = jnp.einsum(
        "pal,apd->lpd", left_rounded, query_grid, preferred_element_type=jnp.float32
    )
    query_mix = (mixed / jnp.maximum(column_mass, 1.0)[..., None]).astype(jnp.bfloat16)

    rounded, entropy, key_mix = right_step(query_mix, block_keys)
    value_mix = jnp.einsum(
        "lpi,lid->lpd", rounded, block_values, preferred_element_type=jnp.float32
    ).astype(jnp.bfloat16)

    _, final_left = left_step(query_grid, key_mix, entropy)
    attended = jnp.einsum(
        "pal,lpd->apd", final_left, value_mix, preferred_element_type=jnp.float32
    ).astype(jnp.bfloat16)
    return from_dest(exchange(attended), place_count, heads_kv)


def make_local(ctx):
    def local(queries, key_states, value_states):
        return jnp.stack(
            [
                one_sequence(queries[s], key_states[s], value_states[s], ctx)
                for s in range(queries.shape[0])
            ]
        )

    return local


def solution(mesh):
    placed = P("grp", ("ctx", "head"), None)
    return jax.shard_map(
        make_local(mesh.shape["ctx"]),
        mesh=mesh,
        in_specs=(placed, placed, placed),
        out_specs=placed,
        check_vma=False,
    )
```

time: 76.2 us -> 63.1 us (0.83)
  blocking collectives: 61.5 us -> 47.6 us
  local copies, waits for them, and re-layouts: 4.12 us -> 5.23 us
    all_to_all x2, blocking collectives: 57.3 us -> 45.4 us  [exchange(): return lax.all_to_all(grid, 'ctx', split_axis=0, concat_axis=0, tiled=True)]
    all_gather x2 -> x1, blocking collectives: 4.27 us -> 2.18 us  [one_sequence(): lax.all_gather(rows[:, chunk:].reshape(ctx, 2, own_len, DH), 'head', axis...]
    unnamed x10 -> x2, local copies, waits for them, and re-layouts: 0.5 us -> 1.85 us
where the time goes in v10:
time: 63.1 us; the launch traced here: 62.9 us
  blocking collectives  47.6 us (75%)
  matrix products  8.36 us (13%)
  local copies, waits for them, and re-layouts  5.23 us (8%)
  other arithmetic  1.52 us (2%)
    all_to_all x2, blocking collectives, exchange(): return lax.all_to_all(grid, 'ctx', split_axis=0, concat_axis=0, tiled=True)  45.4 us
    sub x2, matrix products, left_step(): weights = jax.nn.softmax(logits, axis=-1)  5.46 us
    all_gather x1, blocking collectives, one_sequence(): lax.all_gather(rows[:, chunk:].reshape(ctx, 2, own_len, DH), 'head', axis...  2.18 us
    unnamed x2, local copies, waits for them, and re-layouts  1.85 us
    another operation x2, local copies, waits for them, and re-layouts, to_dest(): shaped = rows.reshape((repeat, place_count // repeat) + rows.shape[1:])  1.59 us

profile of v10, /device:TPU:0, one launch (start us, length us, event | category | flops | bytes accessed | tf_op | source)
XLA Modules:
  0.0 62.9 jit_solution(3467234731037353927)
XLA Ops:
  0.0 0.9 %copy.44 = bf16[8,8,8,128]{3,2,1,0:T(8,128)(2,1)S(1)} copy(bf16[8,8,8,128]{3,1,2,0:T(8,128)(2,1)} %bitcast.57) | data formatting | bytes 262144
  0.9 0.9 %copy.45 = bf16[8,8,8,128]{3,2,1,0:T(8,128)(2,1)S(1)} copy(bf16[8,8,8,128]{3,1,2,0:T(8,128)(2,1)} %bitcast.58) | data formatting | bytes 262144
  1.9 1.4 %reshape_reshape_squeeze.3 = bf16[1,64,8,4,128]{4,3,2,1,0:T(4,128)(2,1)S(1)} reshape(bf16[1,64,4096]{2,1,0:T(8,128)(2,1)} %param.3) | data formatting | bytes 1048576 | tf_op jit(solution)/shard_map/reshape;reshape;squeeze | solution.py:33
  3.3 0.2 copy.21
  3.5 0.1 pad_maximum_fusion
  3.6 27.2 %all_to_all.10 = bf16[8,384,128]{2,1,0:T(8,128)(2,1)S(1)} all-to-all(bf16[8,384,128]{2,1,0:T(8,128)(2,1)S(1)} %pad_maximum_fusion), channel_id=1, replica_groups=mesh['grp'=2,'ctx'=8,'head'=2] {'ctx'}, dimensions={0} | all-to-all | bytes 1572864 | tf_op jit(solution)/shard_map/all_to_all | solution.py:18
  30.8 2.2 %all_gather.3 = bf16[8,2,128,128]{3,2,0,1:T(8,128)(2,1)S(1)} all-gather(bf16[8,2,64,128]{3,2,0,1:T(8,128)(2,1)S(1)} %copy.24), channel_id=1, replica_groups=mesh['grp'=2,'ctx'=8,'head'=2] {'head'}, dimensions={2}, use_global_device_ids=true | all-gather | bytes 786432 | tf_op jit(solution)/shard_map/all_gather | solution.py:73
  33.0 0.3 fusion.35
  33.3 0.2 fusion.12
  33.5 0.4 convolution_convert_fusion.3
  33.9 0.4 exponential_reduce_fusion.1
  34.3 0.1 copy.28
  34.4 2.7 %fusion.36 = (f32[256,8]{1,0:T(8,128)S(1)}, f32[256,8,8]{1,2,0:T(8,128)S(1)}) fusion(bf16[8,256,128]{2,1,0:T(8,128)(2,1)S(1)} %convolution_convert_fusion.3, f32[256,8]{1,0:T(8,128)S(1)} %copy.28, bf16[8,256,128]{2,1,0:T(8,128)(2,1)S(1)} %slice.16), kind=kOutput, calls=%fused_computation.60 | convolution fusion | flops 4259847 | bytes 1130496 | tf_op jit(solution)/shard_map/sub | solution.py:26
  37.2 0.4 fusion.27
  37.6 0.6 fusion.9
  38.2 0.3 fusion.37
  38.5 0.2 fusion.14
  38.7 0.4 convolution_convert_fusion.1
  39.0 0.4 convolution_convert_fusion.2
  39.4 0.4 exponential_reduce_fusion
  39.8 0.1 copy.35
  40.0 2.7 %fusion.38 = (f32[256,8]{1,0:T(8,128)S(1)}, f32[256,8,8]{1,2,0:T(8,128)S(1)}) fusion(bf16[8,256,128]{2,1,0:T(8,128)(2,1)S(1)} %convolution_convert_fusion.1, f32[256,8]{1,0:T(8,128)S(1)} %copy.35, bf16[8,256,128]{2,1,0:T(8,128)(2,1)S(1)} %slice.16), kind=kOutput, calls=%fused_computation.62 | convolution fusion | flops 4259847 | bytes 1130496 | tf_op jit(solution)/shard_map/sub | solution.py:26
  42.7 0.6 fusion.10
  43.3 0.1 copy.38
  43.3 18.2 %all_to_all.11 = bf16[8,256,128]{2,1,0:T(8,128)(2,1)S(1)} all-to-all(bf16[8,256,128]{2,1,0:T(8,128)(2,1)S(1)} %copy.38), channel_id=1, replica_groups=mesh['grp'=2,'ctx'=8,'head'=2] {'ctx'}, dimensions={0} | all-to-all | bytes 1048576 | tf_op jit(solution)/shard_map/all_to_all | solution.py:18
  61.5 0.2 copy.39
  61.7 1.2 %stack_reshape.3 = bf16[1,64,4096]{2,1,0:T(8,128)(2,1)} reshape(bf16[1,64,8,4,128]{4,3,2,1,0:T(4,128)(2,1)S(1)} %copy.39) | data formatting | bytes 1048576 | tf_op jit(solution)/shard_map/stack;reshape | solution.py:100
  (9 shorter events, 0.2 us)

commit v11 on v10

--- a/solution.py
+++ b/solution.py
@@ -3,6 +3,7 @@
 import jax
 import jax.numpy as jnp
 from jax import lax
+from jax.experimental import pallas as pl
 from jax.sharding import PartitionSpec as P
 
 DH = 128
@@ -31,16 +32,73 @@
     place_count, group = rows.shape[0], rows.shape[2]
     repeat = ctx // heads_kv
     shaped = rows.reshape((repeat, place_count // repeat) + rows.shape[1:])
-    shaped = jnp.moveaxis(shaped, 2, 0)
+    shaped = jnp.moveaxis(shaped, (2, 0, 3), (0, 1, 2))
     return shaped.reshape((ctx, place_count // repeat * group) + rows.shape[3:])
 
 
 def from_dest(grid, place_count, heads_kv):
     ctx = grid.shape[0]
     repeat = ctx // heads_kv
-    shaped = grid.reshape(heads_kv, repeat, place_count // repeat, -1, DH)
-    shaped = jnp.moveaxis(shaped, 0, 2)
+    shaped = grid.reshape(heads_kv, repeat, -1, place_count // repeat, DH)
+    shaped = jnp.moveaxis(shaped, (0, 1, 2), (2, 0, 3))
     return shaped.reshape(place_count, -1)
+
+
+def pack_kernel(query_ref, key_ref, value_ref, out_ref):
+    place_count = query_ref.shape[0]
+    ctx = out_ref.shape[0]
+    group = query_ref.shape[1] // key_ref.shape[1]
+    for dest in range(ctx):
+        for g in range(group):
+            head = dest * group + g
+            out_ref[dest, g * place_count : (g + 1) * place_count, :] = query_ref[
+                :, head * DH : (head + 1) * DH
+            ]
+        base = group * place_count
+        out_ref[dest, base : base + place_count, :] = key_ref[:, dest * DH : (dest + 1) * DH]
+        base += place_count
+        out_ref[dest, base : base + place_count, :] = value_ref[:, dest * DH : (dest + 1) * DH]
+
+
+def unpack_kernel(grid_ref, out_ref):
+    ctx, rows, _ = grid_ref.shape
+    place_count = out_ref.shape[0]
+    group = rows // place_count
+    for source in range(ctx):
+        for g in range(group):
+            head = source * group + g
+            out_ref[:, head * DH : (head + 1) * DH] = grid_ref[
+                source, g * place_count : (g + 1) * place_count, :
+            ]
+
+
+def pack(queries, own_keys, own_values, ctx):
+    place_count = queries.shape[0]
+    heads_kv = own_keys.shape[1] // DH
+    if ctx != heads_kv:
+        repeat = ctx // heads_kv
+        query_rows = to_dest(queries.reshape(place_count, heads_kv, -1, DH), ctx, heads_kv)
+        key_rows = jnp.repeat(
+            jnp.swapaxes(own_keys.reshape(place_count, heads_kv, DH), 0, 1), repeat, axis=0
+        )
+        value_rows = jnp.repeat(
+            jnp.swapaxes(own_values.reshape(place_count, heads_kv, DH), 0, 1), repeat, axis=0
+        )
+        return jnp.concatenate([query_rows, key_rows, value_rows], axis=1)
+    rows = queries.shape[1] // DH // heads_kv * place_count + 2 * place_count
+    return pl.pallas_call(
+        pack_kernel, out_shape=jax.ShapeDtypeStruct((ctx, rows, DH), queries.dtype)
+    )(queries, own_keys, own_values)
+
+
+def unpack(grid, place_count, heads_kv):
+    ctx, rows, _ = grid.shape
+    if ctx != heads_kv:
+        return from_dest(grid, place_count, heads_kv)
+    return pl.pallas_call(
+        unpack_kernel,
+        out_shape=jax.ShapeDtypeStruct((place_count, ctx * rows // place_count * DH), grid.dtype),
+    )(grid)
 
 
 def right_step(query_grid, block_keys):
@@ -59,16 +117,8 @@
     place_count, feature_width = queries.shape
     own_len = own_keys.shape[0]
     heads_kv = own_keys.shape[1] // DH
-    repeat = ctx // heads_kv
-    query_rows = to_dest(queries.reshape(place_count, heads_kv, -1, DH), ctx, heads_kv)
-    chunk = query_rows.shape[1]
-    key_rows = jnp.repeat(
-        jnp.swapaxes(own_keys.reshape(own_len, heads_kv, DH), 0, 1), repeat, axis=0
-    )
-    value_rows = jnp.repeat(
-        jnp.swapaxes(own_values.reshape(own_len, heads_kv, DH), 0, 1), repeat, axis=0
-    )
-    rows = exchange(jnp.concatenate([query_rows, key_rows, value_rows], axis=1))
+    chunk = feature_width // DH * place_count // ctx
+    rows = exchange(pack(queries, own_keys, own_values, ctx))
     query_grid = rows[:, :chunk]
     halves = lax.all_gather(
         rows[:, chunk:].reshape(ctx, 2, own_len, DH), "head", axis=2, tiled=True
@@ -92,7 +142,7 @@
     attended = jnp.einsum(
         "pal,lpd->apd", final_left, value_mix, preferred_element_type=jnp.float32
     ).astype(jnp.bfloat16)
-    return from_dest(exchange(attended), place_count, heads_kv)
+    return unpack(exchange(attended), place_count, heads_kv)
 
 
 def make_local(ctx):

time: 63.1 us -> 63.1 us (level)
  local copies, waits for them, and re-layouts: 5.23 us -> 0.44 us
  Pallas kernels: 0 us -> 4.07 us
    pallas_call x0 -> x2, Pallas kernels: none -> 4.07 us  [the longest x1 2.15 us: pack(): pl.pallas_call(pack_kernel, out_shape=jax.ShapeDtypeStruct((ctx, rows, DH...]
    another operation x3 -> x0, local copies, waits for them, and re-layouts: 2.77 us -> none  [the longest x2 1.59 us: to_dest(): shaped = rows.reshape((repeat, place_count // repeat) + rows.shape[1:])]
    unnamed x2 -> x0, local copies, waits for them, and re-layouts: 1.85 us -> none
where the time goes in v11:
time: 63.1 us; the launch traced here: 62.8 us
  blocking collectives  47.9 us (76%)
  matrix products  8.72 us (14%)
  Pallas kernels  4.07 us (6%)
  other arithmetic  1.5 us (2%)
    all_to_all x2, blocking collectives, exchange(): return lax.all_to_all(grid, 'ctx', split_axis=0, concat_axis=0, tiled=True)  45.7 us
    sub x2, matrix products, left_step(): weights = jax.nn.softmax(logits, axis=-1)  5.46 us
    all_gather x1, blocking collectives, one_sequence(): lax.all_gather(rows[:, chunk:].reshape(ctx, 2, own_len, DH), 'head', axis...  2.18 us
    pallas_call x1, Pallas kernels, pack(): pl.pallas_call(pack_kernel, out_shape=jax.ShapeDtypeStruct((ctx, rows, DH...  2.15 us
    pallas_call x1, Pallas kernels, unpack(): pl.pallas_call(unpack_kernel, out_shape=jax.ShapeDtypeStruct((place_count...  1.93 us

profile of v11, /device:TPU:0, one launch (start us, length us, event | category | flops | bytes accessed | tf_op | source)
XLA Modules:
  0.0 62.8 jit_solution(1548722426692487398)
XLA Ops:
  0.0 2.1 %shard_map.37 = bf16[8,384,128]{2,1,0:T(8,128)(2,1)} custom-call(bf16[64,4096]{1,0:T(8,128)(2,1)} %bitcast.46, bf16[64,1024]{1,0:T(8,128)(2,1)} %bitcast.47, bf16[64,1024]{1,0:T(8,128)(2,1)} %bitcast.48), custom_call_target="tpu_custom_call" | custom-call | tf_op jit(solution)/shard_map/pallas_call | solution.py:89
  2.1 27.4 %all_to_all.10 = bf16[8,384,128]{2,1,0:T(8,128)(2,1)S(1)} all-to-all(bf16[8,384,128]{2,1,0:T(8,128)(2,1)} %shard_map.37), channel_id=1, replica_groups=mesh['grp'=2,'ctx'=8,'head'=2] {'ctx'}, dimensions={0} | all-to-all | bytes 1572864 | tf_op jit(solution)/shard_map/all_to_all | solution.py:19
  29.6 2.2 %all_gather.3 = bf16[8,2,128,128]{3,2,0,1:T(8,128)(2,1)S(1)} all-gather(bf16[8,2,64,128]{3,2,0,1:T(8,128)(2,1)S(1)} %copy.11), channel_id=1, replica_groups=mesh['grp'=2,'ctx'=8,'head'=2] {'head'}, dimensions={2}, use_global_device_ids=true | all-gather | bytes 786432 | tf_op jit(solution)/shard_map/all_gather | solution.py:123
  31.8 0.3 fusion.35
  32.1 0.2 fusion.10
  32.3 0.4 fusion.22
  32.6 0.4 exponential_reduce_fusion.1
  33.0 0.1 copy.13
  33.2 2.7 %fusion.36 = (f32[256,8]{1,0:T(8,128)S(1)}, f32[256,8,8]{1,2,0:T(8,128)S(1)}) fusion(bf16[8,256,128]{2,1,0:T(8,128)(2,1)S(1)} %fusion.22, f32[256,8]{1,0:T(8,128)S(1)} %copy.13, bf16[8,256,128]{2,1,0:T(8,128)(2,1)S(1)} %slice.16), kind=kOutput, calls=%fused_computation.58 | convolution fusion | flops 4259847 | bytes 1130496 | tf_op jit(solution)/shard_map/sub | solution.py:27
  36.0 0.4 fusion.27
  36.3 0.5 fusion.20
  36.9 0.1 copy.14
  36.9 0.8 %fusion.37 = (f32[8,256]{1,0:T(8,128)S(1)}, f32[8,256,128]{1,2,0:T(8,128)S(1)}) fusion(bf16[8,2,128,128]{3,2,0,1:T(8,128)(2,1)S(1)} %all_gather.3, f32[256,128,8]{1,2,0:T(8,128)S(1)} %fusion.20, f32[8,256]{1,0:T(8,128)S(1)} %copy.14), kind=kOutput, calls=%fused_computation.59 | convolution fusion | flops 68155392 | bytes 2375680 | tf_op jit(solution)/shard_map/lpd,lid->lpi/dot_general | solution.py:105
  37.7 0.2 fusion.12
  37.9 0.4 exponential_reduce_fusion
  38.3 0.3 fusion.28
  38.7 0.3 fusion.29
  39.0 0.1 copy.16
  39.2 2.7 %fusion.38 = (f32[256,8]{1,0:T(8,128)S(1)}, f32[256,8,8]{1,2,0:T(8,128)S(1)}) fusion(bf16[8,256,128]{2,1,0:T(8,128)(2,1)S(1)} %fusion.29, f32[256,8]{1,0:T(8,128)S(1)} %copy.16, bf16[8,256,128]{2,1,0:T(8,128)(2,1)S(1)} %slice.16), kind=kOutput, calls=%fused_computation.60 | convolution fusion | flops 4259847 | bytes 1130496 | tf_op jit(solution)/shard_map/sub | solution.py:27
  41.9 0.6 fusion.15
  42.5 0.1 copy.51
  42.5 18.3 %all_to_all.11.grid_ref = bf16[8,256,128]{2,1,0:T(8,128)(2,1)} all-to-all(bf16[8,256,128]{2,1,0:T(8,128)(2,1)S(1)} %bitcast.44), channel_id=1, replica_groups=mesh['grp'=2,'ctx'=8,'head'=2] {'ctx'}, dimensions={0} | all-to-all | bytes 1048576 | tf_op jit(solution)/shard_map/all_to_all | solution.py:19
  60.8 1.9 %shard_map.38 = bf16[64,4096]{1,0:T(8,128)(2,1)} custom-call(bf16[8,256,128]{2,1,0:T(8,128)(2,1)} %all_to_all.11.grid_ref), custom_call_target="tpu_custom_call" | custom-call | tf_op jit(solution)/shard_map/pallas_call | solution.py:98
  (8 shorter events, 0.1 us)

commit v12 on v11

--- a/solution.py
+++ b/solution.py
@@ -60,18 +60,6 @@
         out_ref[dest, base : base + place_count, :] = value_ref[:, dest * DH : (dest + 1) * DH]
 
 
-def unpack_kernel(grid_ref, out_ref):
-    ctx, rows, _ = grid_ref.shape
-    place_count = out_ref.shape[0]
-    group = rows // place_count
-    for source in range(ctx):
-        for g in range(group):
-            head = source * group + g
-            out_ref[:, head * DH : (head + 1) * DH] = grid_ref[
-                source, g * place_count : (g + 1) * place_count, :
-            ]
-
-
 def pack(queries, own_keys, own_values, ctx):
     place_count = queries.shape[0]
     heads_kv = own_keys.shape[1] // DH
@@ -89,16 +77,6 @@
     return pl.pallas_call(
         pack_kernel, out_shape=jax.ShapeDtypeStruct((ctx, rows, DH), queries.dtype)
     )(queries, own_keys, own_values)
-
-
-def unpack(grid, place_count, heads_kv):
-    ctx, rows, _ = grid.shape
-    if ctx != heads_kv:
-        return from_dest(grid, place_count, heads_kv)
-    return pl.pallas_call(
-        unpack_kernel,
-        out_shape=jax.ShapeDtypeStruct((place_count, ctx * rows // place_count * DH), grid.dtype),
-    )(grid)
 
 
 def right_step(query_grid, block_keys):
@@ -142,7 +120,7 @@
     attended = jnp.einsum(
         "pal,lpd->apd", final_left, value_mix, preferred_element_type=jnp.float32
     ).astype(jnp.bfloat16)
-    return unpack(exchange(attended), place_count, heads_kv)
+    return from_dest(exchange(attended), place_count, heads_kv)
 
 
 def make_local(ctx):

time: 63.1 us -> 62.6 us (level)
  Pallas kernels: 4.07 us -> 2.15 us
  local copies, waits for them, and re-layouts: 0.44 us -> 2.03 us
    pallas_call x1 -> x0, Pallas kernels: 1.93 us -> none  [unpack(): pl.pallas_call(unpack_kernel, out_shape=jax.ShapeDtypeStruct((place_count...]
    another operation x0 -> x1, local copies, waits for them, and re-layouts: none -> 1.18 us  [local(): jnp.stack([one_sequence(queries[s], key_states[s], value_states[s], ctx)...]
where the time goes in v12:
time: 62.6 us; the launch traced here: 62.3 us
  blocking collectives  47.8 us (76%)
  matrix products  8.72 us (14%)
  Pallas kernels  2.15 us (3%)
  local copies, waits for them, and re-layouts  2.03 us (3%)
  other arithmetic  1.5 us (2%)
    all_to_all x2, blocking collectives, exchange(): return lax.all_to_all(grid, 'ctx', split_axis=0, concat_axis=0, tiled=True)  45.6 us
    sub x2, matrix products, left_step(): weights = jax.nn.softmax(logits, axis=-1)  5.46 us
    all_gather x1, blocking collectives, one_sequence(): lax.all_gather(rows[:, chunk:].reshape(ctx, 2, own_len, DH), 'head', axis...  2.18 us
    pallas_call x1, Pallas kernels, pack(): pl.pallas_call(pack_kernel, out_shape=jax.ShapeDtypeStruct((ctx, rows, DH...  2.15 us

profile of v12, /device:TPU:0, one launch (start us, length us, event | category | flops | bytes accessed | tf_op | source)
XLA Modules:
  0.0 62.3 jit_solution(5011161252880114616)
XLA Ops:
  0.0 2.1 %shard_map.37 = bf16[8,384,128]{2,1,0:T(8,128)(2,1)} custom-call(bf16[64,4096]{1,0:T(8,128)(2,1)} %bitcast.47, bf16[64,1024]{1,0:T(8,128)(2,1)} %bitcast.48, bf16[64,1024]{1,0:T(8,128)(2,1)} %bitcast.49), custom_call_target="tpu_custom_call" | custom-call | tf_op jit(solution)/shard_map/pallas_call | solution.py:77
  2.1 27.4 %all_to_all.10 = bf16[8,384,128]{2,1,0:T(8,128)(2,1)S(1)} all-to-all(bf16[8,384,128]{2,1,0:T(8,128)(2,1)} %shard_map.37), channel_id=1, replica_groups=mesh['grp'=2,'ctx'=8,'head'=2] {'ctx'}, dimensions={0} | all-to-all | bytes 1572864 | tf_op jit(solution)/shard_map/all_to_all | solution.py:19
  29.6 2.2 %all_gather.3 = bf16[8,2,128,128]{3,2,0,1:T(8,128)(2,1)S(1)} all-gather(bf16[8,2,64,128]{3,2,0,1:T(8,128)(2,1)S(1)} %copy.11), channel_id=1, replica_groups=mesh['grp'=2,'ctx'=8,'head'=2] {'head'}, dimensions={2}, use_global_device_ids=true | all-gather | bytes 786432 | tf_op jit(solution)/shard_map/all_gather | solution.py:101
  31.8 0.3 fusion.34
  32.1 0.2 fusion.11
  32.3 0.4 fusion.21
  32.6 0.4 exponential_reduce_fusion.1
  33.0 0.1 copy.13
  33.2 2.7 %fusion.35 = (f32[256,8]{1,0:T(8,128)S(1)}, f32[256,8,8]{1,2,0:T(8,128)S(1)}) fusion(bf16[8,256,128]{2,1,0:T(8,128)(2,1)S(1)} %fusion.21, f32[256,8]{1,0:T(8,128)S(1)} %copy.13, bf16[8,256,128]{2,1,0:T(8,128)(2,1)S(1)} %slice.16), kind=kOutput, calls=%fused_computation.57 | convolution fusion | flops 4259847 | bytes 1130496 | tf_op jit(solution)/shard_map/sub | solution.py:27
  36.0 0.4 fusion.26
  36.3 0.5 fusion.19
  36.9 0.1 copy.14
  36.9 0.8 %fusion.36 = (f32[8,256]{1,0:T(8,128)S(1)}, f32[8,256,128]{1,2,0:T(8,128)S(1)}) fusion(bf16[8,2,128,128]{3,2,0,1:T(8,128)(2,1)S(1)} %all_gather.3, f32[256,128,8]{1,2,0:T(8,128)S(1)} %fusion.19, f32[8,256]{1,0:T(8,128)S(1)} %copy.14), kind=kOutput, calls=%fused_computation.58 | convolution fusion | flops 68155392 | bytes 2375680 | tf_op jit(solution)/shard_map/lpd,lid->lpi/dot_general | solution.py:83
  37.7 0.2 fusion.13
  37.9 0.4 exponential_reduce_fusion
  38.3 0.3 fusion.27
  38.7 0.3 fusion.28
  39.0 0.1 copy.16
  39.2 2.7 %fusion.37 = (f32[256,8]{1,0:T(8,128)S(1)}, f32[256,8,8]{1,2,0:T(8,128)S(1)}) fusion(bf16[8,256,128]{2,1,0:T(8,128)(2,1)S(1)} %fusion.28, f32[256,8]{1,0:T(8,128)S(1)} %copy.16, bf16[8,256,128]{2,1,0:T(8,128)(2,1)S(1)} %slice.16), kind=kOutput, calls=%fused_computation.59 | convolution fusion | flops 4259847 | bytes 1130496 | tf_op jit(solution)/shard_map/sub | solution.py:27
  41.9 0.6 fusion.8
  42.5 0.1 copy.18
  42.5 18.2 %all_to_all.11 = bf16[8,256,128]{2,1,0:T(8,128)(2,1)S(1)} all-to-all(bf16[8,256,128]{2,1,0:T(8,128)(2,1)S(1)} %copy.18), channel_id=1, replica_groups=mesh['grp'=2,'ctx'=8,'head'=2] {'ctx'}, dimensions={0} | all-to-all | bytes 1048576 | tf_op jit(solution)/shard_map/all_to_all | solution.py:19
  60.7 0.4 copy.19
  61.1 1.2 %stack_reshape.3 = bf16[1,64,4096]{2,1,0:T(8,128)(2,1)} reshape(bf16[1,64,8,4,128]{4,3,2,1,0:T(4,128)(2,1)S(1)} %copy.19) | data formatting | bytes 1048576 | tf_op jit(solution)/shard_map/stack;reshape | solution.py:128
  (8 shorter events, 0.1 us)

commit v13 on v12

--- a/solution.py
+++ b/solution.py
@@ -19,10 +19,31 @@
     return lax.all_to_all(grid, "ctx", split_axis=0, concat_axis=0, tiled=True)
 
 
+def pair_logits(query_grid, key_grid):
+    blocks, pairs, _ = query_grid.shape
+    tile = 16 if pairs % 16 == 0 else pairs
+    groups = pairs // tile
+
+    def grouped(grid):
+        shaped = grid.reshape(blocks, groups, tile, DH)
+        return jnp.transpose(shaped, (1, 2, 0, 3)).reshape(groups, tile * blocks, DH)
+
+    products = jnp.einsum(
+        "gxd,gyd->gxy", grouped(query_grid), grouped(key_grid),
+        preferred_element_type=jnp.float32,
+    )
+    index = jnp.arange(tile * blocks)
+    same_pair = (index[:, None] // blocks) == (index[None, :] // blocks)
+    select = (index[:, None] % blocks == jnp.arange(blocks)[None, :]).astype(jnp.float32)
+    folded = jnp.einsum(
+        "gxy,yl->gxl", jnp.where(same_pair, products, 0.0), select,
+        precision=lax.Precision.HIGHEST,
+    )
+    return folded.reshape(pairs, blocks, blocks)
+
+
 def left_step(query_grid, key_grid, entropy_grid):
-    logits = jnp.einsum(
-        "apd,lpd->pal", query_grid, key_grid, preferred_element_type=jnp.float32
-    ) / math.sqrt(DH)
+    logits = pair_logits(query_grid, key_grid) / math.sqrt(DH)
     logits = logits + jnp.transpose(entropy_grid, (1, 0))[:, None, :]
     weights = jax.nn.softmax(logits, axis=-1)
     return weights, weights.astype(jnp.bfloat16)

time: 62.6 us -> 63.8 us (1.019)
  blocking collectives: 47.8 us -> 20.3 us
  waiting for transfers between devices: 0 us -> 20.1 us
  starting transfers between devices: 0 us -> 7.25 us
  local copies, waits for them, and re-layouts: 2.03 us -> 5.82 us
  matrix products: 8.72 us -> 5.66 us
    all_to_all x2 -> x1, blocking collectives: 45.6 us -> 18.1 us  [exchange(): return lax.all_to_all(grid, 'ctx', split_axis=0, concat_axis=0, tiled=True)]
    all_to_all x0 -> x1, waiting for transfers between devices: none -> 20.1 us  [exchange(): return lax.all_to_all(grid, 'ctx', split_axis=0, concat_axis=0, tiled=True)]
    all_to_all x0 -> x1, starting transfers between devices: none -> 7.25 us  [exchange(): return lax.all_to_all(grid, 'ctx', split_axis=0, concat_axis=0, tiled=True)]
    sub x2 -> x0, matrix products: 5.46 us -> none  [left_step(): weights = jax.nn.softmax(logits, axis=-1)]
    dot_general x0 -> x4, matrix products: none -> 2.64 us  [the longest x2 1.42 us: pair_logits(): jnp.einsum('gxd,gyd->gxy', grouped(query_grid), grouped(key_grid), prefer...]
    div x0 -> x8, local copies, waits for them, and re-layouts: none -> 1.74 us  [the longest x5 1.47 us: left_step(): logits = pair_logits(query_grid, key_grid) / math.sqrt(DH)]
    add x0 -> x4, local copies, waits for them, and re-layouts: none -> 1.65 us  [left_step(): logits = logits + jnp.transpose(entropy_grid, (1, 0))[:, None, :]]
  transfers between devices with their start and end apart: 0 -> 1, of which waited for: 0 -> 1; matrix products, arithmetic and copies ran while one was open for 0% -> 0% of each run, Pallas kernels for 0% -> 0%
where the time goes in v13:
time: 63.8 us; the launch traced here: 63.6 us
  blocking collectives  20.3 us (32%)
  waiting for transfers between devices  20.1 us (32%)
  starting transfers between devices  7.25 us (11%)
  local copies, waits for them, and re-layouts  5.82 us (9%)
  matrix products  5.66 us (9%)
  Pallas kernels  2.15 us (3%)
  other arithmetic  2 us (3%)
    all_to_all x1, waiting for transfers between devices, exchange(): return lax.all_to_all(grid, 'ctx', split_axis=0, concat_axis=0, tiled=True)  20.1 us
    all_to_all x1, blocking collectives, exchange(): return lax.all_to_all(grid, 'ctx', split_axis=0, concat_axis=0, tiled=True)  18.1 us
    all_to_all x1, starting transfers between devices, exchange(): return lax.all_to_all(grid, 'ctx', split_axis=0, concat_axis=0, tiled=True)  7.25 us
    all_gather x1, blocking collectives, one_sequence(): lax.all_gather(rows[:, chunk:].reshape(ctx, 2, own_len, DH), 'head', axis...  2.18 us
    pallas_call x1, Pallas kernels, pack(): pl.pallas_call(pack_kernel, out_shape=jax.ShapeDtypeStruct((ctx, rows, DH...  2.15 us
    add x4, local copies, waits for them, and re-layouts, left_step(): logits = logits + jnp.transpose(entropy_grid, (1, 0))[:, None, :]  1.65 us
    div x5, local copies, waits for them, and re-layouts, left_step(): logits = pair_logits(query_grid, key_grid) / math.sqrt(DH)  1.47 us
    dot_general x2, matrix products, pair_logits(): jnp.einsum('gxd,gyd->gxy', grouped(query_grid), grouped(key_grid), prefer...  1.42 us
  transfers between devices with their start and end apart: 1, of which 1 were waited for; matrix products, arithmetic and copies ran while one was open for 0% of the time, Pallas kernels for 0%

profile of v13, /device:TPU:0, one launch (start us, length us, event | category | flops | bytes accessed | tf_op | source)
XLA Modules:
  0.0 63.6 jit_solution(1269111443183122849)
XLA Ops:
  0.0 2.1 %shard_map.37 = bf16[8,384,128]{2,1,0:T(8,128)(2,1)} custom-call(bf16[64,4096]{1,0:T(8,128)(2,1)} %bitcast.85, bf16[64,1024]{1,0:T(8,128)(2,1)} %bitcast.88, bf16[64,1024]{1,0:T(8,128)(2,1)} %bitcast.89), custom_call_target="tpu_custom_call" | custom-call | tf_op jit(solution)/shard_map/pallas_call | solution.py:98
  2.1 7.3 %all-to-all-start = ((bf16[8,384,128]{2,1,0:T(8,128)(2,1)}), bf16[8,384,128]{2,1,0:T(8,128)(2,1)S(1)}, u32[]{:S(2)}, u32[]{:S(2)}) async-start(bf16[8,384,128]{2,1,0:T(8,128)(2,1)} %shard_map.37), calls=%async_computation | async-start | bytes 1572864 | tf_op jit(solution)/shard_map/all_to_all | solution.py:19
  9.4 0.1 broadcast_compare_fusion
  9.5 20.1 %all-to-all-done = bf16[8,384,128]{2,1,0:T(8,128)(2,1)S(1)} async-done(((bf16[8,384,128]{2,1,0:T(8,128)(2,1)}), bf16[8,384,128]{2,1,0:T(8,128)(2,1)S(1)}, u32[]{:S(2)}, u32[]{:S(2)}) %all-to-all-start) | async-done | bytes 786464 | tf_op jit(solution)/shard_map/all_to_all | solution.py:19
  29.6 2.2 %all_gather.3 = bf16[8,2,128,128]{3,2,0,1:T(8,128)(2,1)S(1)} all-gather(bf16[8,2,64,128]{3,2,0,1:T(8,128)(2,1)S(1)} %copy.60), channel_id=1, replica_groups=mesh['grp'=2,'ctx'=8,'head'=2] {'head'}, dimensions={2}, use_global_device_ids=true | all-gather | bytes 786432 | tf_op jit(solution)/shard_map/all_gather | solution.py:122
  31.8 0.3 fusion.38
  32.1 0.2 fusion.4
  32.3 0.4 convolution_convert_fusion.3
  32.7 0.4 exponential_reduce_fusion.1
  33.1 0.3 add.65
  33.4 0.5 add.67
  34.0 0.7 %convolution_select_fusion.1 = f32[16,128,128]{2,1,0:T(8,128)S(1)} fusion(bf16[8,16,16,128]{3,2,1,0:T(8,128)(2,1)S(1)} %bitcast.86, pred[128,128]{1,0:T(8,128)(4,1)S(1)} %broadcast_compare_fusion, bf16[8,16,16,128]{3,2,1,0:T(8,128)(2,1)S(1)} %bitcast.81), kind=kOutput, calls=%fused_computation.1 | convolution fusion | flops 67371008 | bytes 2113536 | tf_op jit(solution)/shard_map/gxd,gyd->gxy/dot_general | solution.py:31
  34.7 0.6 fusion.24
  35.3 0.1 exponential_reduce_fusion.3
  35.4 0.1 sub.92
  35.5 0.1 div.85
  35.6 0.6 div.84
  36.1 0.7 %fusion.22 = (f32[256,8]{0,1:T(8,128)S(1)}, bf16[256,8,8]{1,0,2:T(8,128)(2,1)S(1)}) fusion(f32[256,8]{1,0:T(8,128)S(1)} %div.85, f32[256,8]{1,0:T(8,128)S(1)} %sub.92, f32[256,8,8]{1,0,2:T(8,128)S(1)} %div.84, f32[256,8]{0,1:T(8,128)S(1)} %fusion.27), kind=kLoop, calls=%fused_computation.41 | loop fusion | flops 79872 | bytes 131072 | tf_op jit(solution)/shard_map/reduce_sum | solution.py:129
  36.8 0.1 copy.67
  36.9 0.8 %fusion.1 = bf16[8,256,128]{2,0,1:T(8,128)(2,1)S(1)} fusion(bf16[256,8,8]{1,0,2:T(8,128)(2,1)S(1)} %get-tuple-element.10, bf16[8,256,128]{2,1,0:T(8,128)(2,1)S(1)} %slice.16, f32[8,256]{0,1:T(8,128)S(1)} %copy.67), kind=kOutput, calls=%fused_computation.10 | convolution fusion | flops 4718592 | bytes 1089536 | tf_op jit(solution)/shard_map/pal,apd->lpd/dot_general | solution.py:130
  37.7 0.3 fusion.39
  38.1 0.2 fusion.6
  38.3 0.4 convolution_convert_fusion.1
  38.6 0.4 convolution_convert_fusion.2
  39.0 0.4 exponential_reduce_fusion
  39.4 0.7 %convolution_select_fusion = f32[16,128,128]{2,1,0:T(8,128)S(1)} fusion(bf16[8,16,16,128]{3,2,1,0:T(8,128)(2,1)S(1)} %bitcast.87, pred[128,128]{1,0:T(8,128)(4,1)S(1)} %broadcast_compare_fusion, bf16[8,16,16,128]{3,2,1,0:T(8,128)(2,1)S(1)} %bitcast.82), kind=kOutput, calls=%fused_computation | convolution fusion | flops 67371008 | bytes 2113536 | tf_op jit(solution)/shard_map/gxd,gyd->gxy/dot_general | solution.py:31
  40.1 0.3 add.70.clone
  40.4 0.5 add.72
  40.9 0.6 fusion.25
  41.6 0.1 sub.102
  41.7 0.1 copy.76
  41.8 0.1 div.95
  41.9 0.1 copy.77
  42.0 0.6 div.94
  42.6 0.3 copy.73
  42.9 0.1 divide_convert_fusion
  42.9 0.3 copy.79
  43.3 0.5 fusion.2
  43.7 0.1 copy.80
  43.8 18.1 %all_to_all.10 = bf16[8,256,128]{2,1,0:T(8,128)(2,1)S(1)} all-to-all(bf16[8,256,128]{2,1,0:T(8,128)(2,1)S(1)} %copy.80), channel_id=1, replica_groups=mesh['grp'=2,'ctx'=8,'head'=2] {'ctx'}, dimensions={0} | all-to-all | bytes 1048576 | tf_op jit(solution)/shard_map/all_to_all | solution.py:19
  62.0 0.4 copy.81
  62.4 1.2 %stack_reshape.3 = bf16[1,64,4096]{2,1,0:T(8,128)(2,1)} reshape(bf16[1,64,8,4,128]{4,3,2,1,0:T(4,128)(2,1)S(1)} %copy.81) | data formatting | bytes 1048576 | tf_op jit(solution)/shard_map/stack;reshape | solution.py:149
  (13 shorter events, 0.2 us)
Async XLA Ops:
  2.1 27.4 %all-to-all-start = ((bf16[8,384,128]{2,1,0:T(8,128)(2,1)}), bf16[8,384,128]{2,1,0:T(8,128)(2,1)S(1)}, u32[]{:S(2)}, u32[]{:S(2)}) async-start(bf16[8,384,128]{2,1,0:T(8,128)(2,1)} %shard_map.37), calls=%async_computation | async-start | bytes 1572864 | tf_op jit(solution)/shard_map/all_to_all | solution.py:19

commit v14 on v11

--- a/solution.py
+++ b/solution.py
@@ -4,6 +4,7 @@
 import jax.numpy as jnp
 from jax import lax
 from jax.experimental import pallas as pl
+from jax.experimental.pallas import tpu as pltpu
 from jax.sharding import PartitionSpec as P
 
 DH = 128
@@ -44,32 +45,50 @@
     return shaped.reshape(place_count, -1)
 
 
-def pack_kernel(query_ref, key_ref, value_ref, out_ref):
+def pack_kernel(query_ref, key_ref, value_ref, out_ref, sems):
     place_count = query_ref.shape[0]
     ctx = out_ref.shape[0]
     group = query_ref.shape[1] // key_ref.shape[1]
+    moves = []
     for dest in range(ctx):
         for g in range(group):
             head = dest * group + g
-            out_ref[dest, g * place_count : (g + 1) * place_count, :] = query_ref[
-                :, head * DH : (head + 1) * DH
-            ]
+            moves.append(
+                (query_ref.at[:, pl.ds(head * DH, DH)], out_ref.at[dest, pl.ds(g * place_count, place_count)])
+            )
         base = group * place_count
-        out_ref[dest, base : base + place_count, :] = key_ref[:, dest * DH : (dest + 1) * DH]
+        moves.append((key_ref.at[:, pl.ds(dest * DH, DH)], out_ref.at[dest, pl.ds(base, place_count)]))
         base += place_count
-        out_ref[dest, base : base + place_count, :] = value_ref[:, dest * DH : (dest + 1) * DH]
+        moves.append((value_ref.at[:, pl.ds(dest * DH, DH)], out_ref.at[dest, pl.ds(base, place_count)]))
+    copies = [
+        pltpu.make_async_copy(source, target, sems.at[index])
+        for index, (source, target) in enumerate(moves)
+    ]
+    for copy in copies:
+        copy.start()
+    for copy in copies:
+        copy.wait()
 
 
-def unpack_kernel(grid_ref, out_ref):
+def unpack_kernel(grid_ref, out_ref, sems):
     ctx, rows, _ = grid_ref.shape
     place_count = out_ref.shape[0]
     group = rows // place_count
+    copies = []
     for source in range(ctx):
         for g in range(group):
             head = source * group + g
-            out_ref[:, head * DH : (head + 1) * DH] = grid_ref[
-                source, g * place_count : (g + 1) * place_count, :
-            ]
+            copies.append(
+                pltpu.make_async_copy(
+                    grid_ref.at[source, pl.ds(g * place_count, place_count)],
+                    out_ref.at[:, pl.ds(head * DH, DH)],
+                    sems.at[len(copies)],
+                )
+            )
+    for copy in copies:
+        copy.start()
+    for copy in copies:
+        copy.wait()
 
 
 def pack(queries, own_keys, own_values, ctx):
@@ -86,8 +105,13 @@
         )
         return jnp.concatenate([query_rows, key_rows, value_rows], axis=1)
     rows = queries.shape[1] // DH // heads_kv * place_count + 2 * place_count
+    anywhere = pl.BlockSpec(memory_space=pl.ANY)
     return pl.pallas_call(
-        pack_kernel, out_shape=jax.ShapeDtypeStruct((ctx, rows, DH), queries.dtype)
+        pack_kernel,
+        out_shape=jax.ShapeDtypeStruct((ctx, rows, DH), queries.dtype),
+        in_specs=[anywhere, anywhere, anywhere],
+        out_specs=anywhere,
+        scratch_shapes=[pltpu.SemaphoreType.DMA((ctx * (queries.shape[1] // DH // heads_kv + 2),))],
     )(queries, own_keys, own_values)
 
 
@@ -95,9 +119,14 @@
     ctx, rows, _ = grid.shape
     if ctx != heads_kv:
         return from_dest(grid, place_count, heads_kv)
+    anywhere = pl.BlockSpec(memory_space=pl.ANY)
+    heads = ctx * rows // place_count
     return pl.pallas_call(
         unpack_kernel,
-        out_shape=jax.ShapeDtypeStruct((place_count, ctx * rows // place_count * DH), grid.dtype),
+        out_shape=jax.ShapeDtypeStruct((place_count, heads * DH), grid.dtype),
+        in_specs=[anywhere],
+        out_specs=anywhere,
+        scratch_shapes=[pltpu.SemaphoreType.DMA((heads,))],
     )(grid)
 
 

time: 63.1 us -> 102 us (1.62)
  Pallas kernels: 4.07 us -> 42.6 us
    pallas_call x1, Pallas kernels: 2.15 us -> 25.4 us  [pack(): pl.pallas_call(pack_kernel, out_shape=jax.ShapeDtypeStruct((ctx, rows, DH...]
    pallas_call x1, Pallas kernels: 1.93 us -> 17.3 us  [unpack(): pl.pallas_call(unpack_kernel, out_shape=jax.ShapeDtypeStruct((place_count...]
where the time goes in v14:
time: 102 us; the launch traced here: 101 us
  blocking collectives  47.9 us (47%)
  Pallas kernels  42.6 us (42%)
  matrix products  8.72 us (9%)
  other arithmetic  1.5 us (1%)
    all_to_all x2, blocking collectives, exchange(): return lax.all_to_all(grid, 'ctx', split_axis=0, concat_axis=0, tiled=True)  45.7 us
    pallas_call x1, Pallas kernels, pack(): pl.pallas_call(pack_kernel, out_shape=jax.ShapeDtypeStruct((ctx, rows, DH...  25.4 us
    pallas_call x1, Pallas kernels, unpack(): pl.pallas_call(unpack_kernel, out_shape=jax.ShapeDtypeStruct((place_count...  17.3 us
    sub x2, matrix products, left_step(): weights = jax.nn.softmax(logits, axis=-1)  5.46 us
    all_gather x1, blocking collectives, one_sequence(): lax.all_gather(rows[:, chunk:].reshape(ctx, 2, own_len, DH), 'head', axis...  2.18 us

profile of v14, /device:TPU:0, one launch (start us, length us, event | category | flops | bytes accessed | tf_op | source)
XLA Modules:
  0.0 101.3 jit_solution(923105089089305185)
XLA Ops:
  0.0 25.4 %shard_map.37 = bf16[8,384,128]{2,1,0:T(8,128)(2,1)} custom-call(bf16[64,4096]{1,0:T(8,128)(2,1)} %bitcast.46, bf16[64,1024]{1,0:T(8,128)(2,1)} %bitcast.47, bf16[64,1024]{1,0:T(8,128)(2,1)} %bitcast.48), custom_call_target="tpu_custom_call" | custom-call | tf_op jit(solution)/shard_map/pallas_call | solution.py:109
  25.4 27.4 %all_to_all.10 = bf16[8,384,128]{2,1,0:T(8,128)(2,1)S(1)} all-to-all(bf16[8,384,128]{2,1,0:T(8,128)(2,1)} %shard_map.37), channel_id=1, replica_groups=mesh['grp'=2,'ctx'=8,'head'=2] {'ctx'}, dimensions={0} | all-to-all | bytes 1572864 | tf_op jit(solution)/shard_map/all_to_all | solution.py:20
  52.8 2.2 %all_gather.3 = bf16[8,2,128,128]{3,2,0,1:T(8,128)(2,1)S(1)} all-gather(bf16[8,2,64,128]{3,2,0,1:T(8,128)(2,1)S(1)} %copy.11), channel_id=1, replica_groups=mesh['grp'=2,'ctx'=8,'head'=2] {'head'}, dimensions={2}, use_global_device_ids=true | all-gather | bytes 786432 | tf_op jit(solution)/shard_map/all_gather | solution.py:152
  55.0 0.3 fusion.35
  55.3 0.2 fusion.10
  55.5 0.4 fusion.22
  55.9 0.4 exponential_reduce_fusion.1
  56.3 0.1 copy.13
  56.4 2.7 %fusion.36 = (f32[256,8]{1,0:T(8,128)S(1)}, f32[256,8,8]{1,2,0:T(8,128)S(1)}) fusion(bf16[8,256,128]{2,1,0:T(8,128)(2,1)S(1)} %fusion.22, f32[256,8]{1,0:T(8,128)S(1)} %copy.13, bf16[8,256,128]{2,1,0:T(8,128)(2,1)S(1)} %slice.16), kind=kOutput, calls=%fused_computation.58 | convolution fusion | flops 4259847 | bytes 1130496 | tf_op jit(solution)/shard_map/sub | solution.py:28
  59.2 0.4 fusion.27
  59.5 0.5 fusion.20
  60.1 0.1 copy.14
  60.1 0.8 fusion.37
  61.0 0.2 fusion.12
  61.1 0.4 exponential_reduce_fusion
  61.5 0.4 fusion.28
  61.9 0.4 fusion.29
  62.3 0.1 copy.16
  62.4 2.7 %fusion.38 = (f32[256,8]{1,0:T(8,128)S(1)}, f32[256,8,8]{1,2,0:T(8,128)S(1)}) fusion(bf16[8,256,128]{2,1,0:T(8,128)(2,1)S(1)} %fusion.29, f32[256,8]{1,0:T(8,128)S(1)} %copy.16, bf16[8,256,128]{2,1,0:T(8,128)(2,1)S(1)} %slice.16), kind=kOutput, calls=%fused_computation.60 | convolution fusion | flops 4259847 | bytes 1130496 | tf_op jit(solution)/shard_map/sub | solution.py:28
  65.1 0.6 fusion.15
  65.7 0.1 copy.51
  65.8 18.3 %all_to_all.11.grid_ref = bf16[8,256,128]{2,1,0:T(8,128)(2,1)} all-to-all(bf16[8,256,128]{2,1,0:T(8,128)(2,1)S(1)} %bitcast.44), channel_id=1, replica_groups=mesh['grp'=2,'ctx'=8,'head'=2] {'ctx'}, dimensions={0} | all-to-all | bytes 1048576 | tf_op jit(solution)/shard_map/all_to_all | solution.py:20
  84.1 17.3 %shard_map.38 = bf16[64,4096]{1,0:T(8,128)(2,1)} custom-call(bf16[8,256,128]{2,1,0:T(8,128)(2,1)} %all_to_all.11.grid_ref), custom_call_target="tpu_custom_call" | custom-call | tf_op jit(solution)/shard_map/pallas_call | solution.py:124
  (8 shorter events, 0.1 us)

commit v15 on v12

--- a/solution.py
+++ b/solution.py
@@ -21,10 +21,10 @@
 
 def left_step(query_grid, key_grid, entropy_grid):
     logits = jnp.einsum(
-        "apd,lpd->pal", query_grid, key_grid, preferred_element_type=jnp.float32
+        "apd,lpd->alp", query_grid, key_grid, preferred_element_type=jnp.float32
     ) / math.sqrt(DH)
-    logits = logits + jnp.transpose(entropy_grid, (1, 0))[:, None, :]
-    weights = jax.nn.softmax(logits, axis=-1)
+    logits = logits + entropy_grid[None]
+    weights = jax.nn.softmax(logits, axis=1)
     return weights, weights.astype(jnp.bfloat16)
 
 
@@ -105,9 +105,9 @@
 
     _, entropy_grid, key_grid = right_step(query_grid, block_keys)
     weights, left_rounded = left_step(query_grid, key_grid, entropy_grid)
-    column_mass = jnp.transpose(jnp.sum(weights, axis=1), (1, 0))
+    column_mass = jnp.sum(weights, axis=0)
     mixed = jnp.einsum(
-        "pal,apd->lpd", left_rounded, query_grid, preferred_element_type=jnp.float32
+        "alp,apd->lpd", left_rounded, query_grid, preferred_element_type=jnp.float32
     )
     query_mix = (mixed / jnp.maximum(column_mass, 1.0)[..., None]).astype(jnp.bfloat16)
 
@@ -118,7 +118,7 @@
 
     _, final_left = left_step(query_grid, key_mix, entropy)
     attended = jnp.einsum(
-        "pal,lpd->apd", final_left, value_mix, preferred_element_type=jnp.float32
+        "alp,lpd->apd", final_left, value_mix, preferred_element_type=jnp.float32
     ).astype(jnp.bfloat16)
     return from_dest(exchange(attended), place_count, heads_kv)
 

time: 62.6 us -> 62.3 us (level)
  no operation moved by 1% of the time
where the time goes in v15:
time: 62.3 us; the launch traced here: 62.1 us
  blocking collectives  47.8 us (77%)
  matrix products  8.36 us (13%)
  local copies, waits for them, and re-layouts  2.17 us (3%)
  Pallas kernels  2.15 us (3%)
  other arithmetic  1.46 us (2%)
    all_to_all x2, blocking collectives, exchange(): return lax.all_to_all(grid, 'ctx', split_axis=0, concat_axis=0, tiled=True)  45.6 us
    sub x2, matrix products, left_step(): weights = jax.nn.softmax(logits, axis=1)  5.46 us
    all_gather x1, blocking collectives, one_sequence(): lax.all_gather(rows[:, chunk:].reshape(ctx, 2, own_len, DH), 'head', axis...  2.18 us
    pallas_call x1, Pallas kernels, pack(): pl.pallas_call(pack_kernel, out_shape=jax.ShapeDtypeStruct((ctx, rows, DH...  2.15 us

profile of v15, /device:TPU:0, one launch (start us, length us, event | category | flops | bytes accessed | tf_op | source)
XLA Modules:
  0.0 62.1 jit_solution(3870028104694689961)
XLA Ops:
  0.0 2.1 %shard_map.37 = bf16[8,384,128]{2,1,0:T(8,128)(2,1)} custom-call(bf16[64,4096]{1,0:T(8,128)(2,1)} %bitcast.42, bf16[64,1024]{1,0:T(8,128)(2,1)} %bitcast.43, bf16[64,1024]{1,0:T(8,128)(2,1)} %bitcast.44), custom_call_target="tpu_custom_call" | custom-call | tf_op jit(solution)/shard_map/pallas_call | solution.py:77
  2.1 27.4 %all_to_all.10 = bf16[8,384,128]{2,1,0:T(8,128)(2,1)S(1)} all-to-all(bf16[8,384,128]{2,1,0:T(8,128)(2,1)} %shard_map.37), channel_id=1, replica_groups=mesh['grp'=2,'ctx'=8,'head'=2] {'ctx'}, dimensions={0} | all-to-all | bytes 1572864 | tf_op jit(solution)/shard_map/all_to_all | solution.py:19
  29.6 2.2 %all_gather.3 = bf16[8,2,128,128]{3,2,0,1:T(8,128)(2,1)S(1)} all-gather(bf16[8,2,64,128]{3,2,0,1:T(8,128)(2,1)S(1)} %copy.20), channel_id=1, replica_groups=mesh['grp'=2,'ctx'=8,'head'=2] {'head'}, dimensions={2}, use_global_device_ids=true | all-gather | bytes 786432 | tf_op jit(solution)/shard_map/all_gather | solution.py:101
  31.8 0.3 fusion.33
  32.1 0.2 fusion.14
  32.3 0.4 convolution_convert_fusion.3
  32.6 0.4 exponential_reduce_fusion.1
  33.0 0.1 copy.24
  33.2 2.7 %fusion.34 = (f32[8,256]{0,1:T(8,128)S(1)}, f32[8,8,256]{0,1,2:T(8,128)S(1)}) fusion(bf16[8,256,128]{2,1,0:T(8,128)(2,1)S(1)} %convolution_convert_fusion.3, f32[8,256]{0,1:T(8,128)S(1)} %copy.24, bf16[8,256,128]{2,1,0:T(8,128)(2,1)S(1)} %slice.16), kind=kOutput, calls=%fused_computation.55 | convolution fusion | flops 4259847 | bytes 1130496 | tf_op jit(solution)/shard_map/sub | solution.py:27
  36.0 0.4 fusion.29
  36.3 0.1 copy.26
  36.4 0.1 copy.27
  36.5 0.6 fusion.11
  37.1 0.3 fusion.35
  37.5 0.2 fusion.16
  37.6 0.4 convolution_convert_fusion.1
  38.0 0.4 convolution_convert_fusion.2
  38.4 0.4 exponential_reduce_fusion
  38.8 0.1 copy.33
  38.9 2.7 %fusion.36 = (f32[8,256]{0,1:T(8,128)S(1)}, f32[8,8,256]{0,1,2:T(8,128)S(1)}) fusion(bf16[8,256,128]{2,1,0:T(8,128)(2,1)S(1)} %convolution_convert_fusion.1, f32[8,256]{0,1:T(8,128)S(1)} %copy.33, bf16[8,256,128]{2,1,0:T(8,128)(2,1)S(1)} %slice.16), kind=kOutput, calls=%fused_computation.57 | convolution fusion | flops 4259847 | bytes 1130496 | tf_op jit(solution)/shard_map/sub | solution.py:27
  41.7 0.6 fusion.12
  42.2 0.1 copy.36
  42.3 18.2 %all_to_all.11 = bf16[8,256,128]{2,1,0:T(8,128)(2,1)S(1)} all-to-all(bf16[8,256,128]{2,1,0:T(8,128)(2,1)S(1)} %copy.36), channel_id=1, replica_groups=mesh['grp'=2,'ctx'=8,'head'=2] {'ctx'}, dimensions={0} | all-to-all | bytes 1048576 | tf_op jit(solution)/shard_map/all_to_all | solution.py:19
  60.5 0.4 copy.37
  60.9 1.2 %stack_reshape.3 = bf16[1,64,4096]{2,1,0:T(8,128)(2,1)} reshape(bf16[1,64,8,4,128]{4,3,2,1,0:T(4,128)(2,1)S(1)} %copy.37) | data formatting | bytes 1048576 | tf_op jit(solution)/shard_map/stack;reshape | solution.py:128
  (8 shorter events, 0.1 us)

commit v16 on v15

--- a/solution.py
+++ b/solution.py
@@ -46,18 +46,12 @@
 
 def pack_kernel(query_ref, key_ref, value_ref, out_ref):
     place_count = query_ref.shape[0]
-    ctx = out_ref.shape[0]
-    group = query_ref.shape[1] // key_ref.shape[1]
-    for dest in range(ctx):
-        for g in range(group):
-            head = dest * group + g
-            out_ref[dest, g * place_count : (g + 1) * place_count, :] = query_ref[
-                :, head * DH : (head + 1) * DH
-            ]
-        base = group * place_count
-        out_ref[dest, base : base + place_count, :] = key_ref[:, dest * DH : (dest + 1) * DH]
-        base += place_count
-        out_ref[dest, base : base + place_count, :] = value_ref[:, dest * DH : (dest + 1) * DH]
+    group = query_ref.shape[1] // DH
+    for g in range(group):
+        out_ref[0, g * place_count : (g + 1) * place_count, :] = query_ref[:, g * DH : (g + 1) * DH]
+    base = group * place_count
+    out_ref[0, base : base + place_count, :] = key_ref[...]
+    out_ref[0, base + place_count : base + 2 * place_count, :] = value_ref[...]
 
 
 def pack(queries, own_keys, own_values, ctx):
@@ -73,9 +67,18 @@
             jnp.swapaxes(own_values.reshape(place_count, heads_kv, DH), 0, 1), repeat, axis=0
         )
         return jnp.concatenate([query_rows, key_rows, value_rows], axis=1)
-    rows = queries.shape[1] // DH // heads_kv * place_count + 2 * place_count
+    group = queries.shape[1] // DH // heads_kv
+    rows = group * place_count + 2 * place_count
     return pl.pallas_call(
-        pack_kernel, out_shape=jax.ShapeDtypeStruct((ctx, rows, DH), queries.dtype)
+        pack_kernel,
+        grid=(ctx,),
+        in_specs=[
+            pl.BlockSpec((place_count, group * DH), lambda i: (0, i)),
+            pl.BlockSpec((place_count, DH), lambda i: (0, i)),
+            pl.BlockSpec((place_count, DH), lambda i: (0, i)),
+        ],
+        out_specs=pl.BlockSpec((1, rows, DH), lambda i: (i, 0, 0)),
+        out_shape=jax.ShapeDtypeStruct((ctx, rows, DH), queries.dtype),
     )(queries, own_keys, own_values)
 
 

time: 62.3 us -> 65.3 us (1.048)
  Pallas kernels: 2.15 us -> 4.91 us
    pallas_call x1, Pallas kernels: 2.15 us -> 4.91 us  [pack(): pl.pallas_call(pack_kernel, grid=(ctx,), in_specs=[pl.BlockSpec((place_co...]
where the time goes in v16:
time: 65.3 us; the launch traced here: 64.8 us
  blocking collectives  47.8 us (73%)
  matrix products  8.36 us (13%)
  Pallas kernels  4.91 us (8%)
  local copies, waits for them, and re-layouts  2.17 us (3%)
  other arithmetic  1.46 us (2%)
    all_to_all x2, blocking collectives, exchange(): return lax.all_to_all(grid, 'ctx', split_axis=0, concat_axis=0, tiled=True)  45.6 us
    sub x2, matrix products, left_step(): weights = jax.nn.softmax(logits, axis=1)  5.46 us
    pallas_call x1, Pallas kernels, pack(): pl.pallas_call(pack_kernel, grid=(ctx,), in_specs=[pl.BlockSpec((place_co...  4.91 us
    all_gather x1, blocking collectives, one_sequence(): lax.all_gather(rows[:, chunk:].reshape(ctx, 2, own_len, DH), 'head', axis...  2.18 us

profile of v16, /device:TPU:0, one launch (start us, length us, event | category | flops | bytes accessed | tf_op | source)
XLA Modules:
  0.0 64.8 jit_solution(12533728519241857876)
XLA Ops:
  0.0 4.9 %shard_map.37 = bf16[8,384,128]{2,1,0:T(8,128)(2,1)} custom-call(bf16[64,4096]{1,0:T(8,128)(2,1)} %bitcast.42, bf16[64,1024]{1,0:T(8,128)(2,1)} %bitcast.43, bf16[64,1024]{1,0:T(8,128)(2,1)} %bitcast.44), custom_call_target="tpu_custom_call" | custom-call | tf_op jit(solution)/shard_map/pallas_call | solution.py:72
  4.9 27.4 %all_to_all.10 = bf16[8,384,128]{2,1,0:T(8,128)(2,1)S(1)} all-to-all(bf16[8,384,128]{2,1,0:T(8,128)(2,1)} %shard_map.37), channel_id=1, replica_groups=mesh['grp'=2,'ctx'=8,'head'=2] {'ctx'}, dimensions={0} | all-to-all | bytes 1572864 | tf_op jit(solution)/shard_map/all_to_all | solution.py:19
  32.4 2.2 %all_gather.3 = bf16[8,2,128,128]{3,2,0,1:T(8,128)(2,1)S(1)} all-gather(bf16[8,2,64,128]{3,2,0,1:T(8,128)(2,1)S(1)} %copy.20), channel_id=1, replica_groups=mesh['grp'=2,'ctx'=8,'head'=2] {'head'}, dimensions={2}, use_global_device_ids=true | all-gather | bytes 786432 | tf_op jit(solution)/shard_map/all_gather | solution.py:104
  34.5 0.3 fusion.33
  34.9 0.2 fusion.14
  35.0 0.4 convolution_convert_fusion.3
  35.4 0.4 exponential_reduce_fusion.1
  35.8 0.1 copy.24
  36.0 2.7 %fusion.34 = (f32[8,256]{0,1:T(8,128)S(1)}, f32[8,8,256]{0,1,2:T(8,128)S(1)}) fusion(bf16[8,256,128]{2,1,0:T(8,128)(2,1)S(1)} %convolution_convert_fusion.3, f32[8,256]{0,1:T(8,128)S(1)} %copy.24, bf16[8,256,128]{2,1,0:T(8,128)(2,1)S(1)} %slice.16), kind=kOutput, calls=%fused_computation.55 | convolution fusion | flops 4259847 | bytes 1130496 | tf_op jit(solution)/shard_map/sub | solution.py:27
  38.7 0.4 fusion.29
  39.1 0.1 copy.26
  39.1 0.1 copy.27
  39.3 0.6 fusion.11
  39.9 0.3 fusion.35
  40.2 0.2 fusion.16
  40.4 0.4 convolution_convert_fusion.1
  40.8 0.4 convolution_convert_fusion.2
  41.2 0.4 exponential_reduce_fusion
  41.6 0.1 copy.33
  41.7 2.7 %fusion.36 = (f32[8,256]{0,1:T(8,128)S(1)}, f32[8,8,256]{0,1,2:T(8,128)S(1)}) fusion(bf16[8,256,128]{2,1,0:T(8,128)(2,1)S(1)} %convolution_convert_fusion.1, f32[8,256]{0,1:T(8,128)S(1)} %copy.33, bf16[8,256,128]{2,1,0:T(8,128)(2,1)S(1)} %slice.16), kind=kOutput, calls=%fused_computation.57 | convolution fusion | flops 4259847 | bytes 1130496 | tf_op jit(solution)/shard_map/sub | solution.py:27
  44.4 0.6 fusion.12
  45.0 0.1 copy.36
  45.1 18.2 %all_to_all.11 = bf16[8,256,128]{2,1,0:T(8,128)(2,1)S(1)} all-to-all(bf16[8,256,128]{2,1,0:T(8,128)(2,1)S(1)} %copy.36), channel_id=1, replica_groups=mesh['grp'=2,'ctx'=8,'head'=2] {'ctx'}, dimensions={0} | all-to-all | bytes 1048576 | tf_op jit(solution)/shard_map/all_to_all | solution.py:19
  63.2 0.4 copy.37
  63.7 1.2 %stack_reshape.3 = bf16[1,64,4096]{2,1,0:T(8,128)(2,1)} reshape(bf16[1,64,8,4,128]{4,3,2,1,0:T(4,128)(2,1)S(1)} %copy.37) | data formatting | bytes 1048576 | tf_op jit(solution)/shard_map/stack;reshape | solution.py:131
  (8 shorter events, 0.1 us)

commit v17 on v15

--- a/solution.py
+++ b/solution.py
@@ -117,10 +117,21 @@
     ).astype(jnp.bfloat16)
 
     _, final_left = left_step(query_grid, key_mix, entropy)
+    if ctx != heads_kv:
+        attended = jnp.einsum(
+            "alp,lpd->apd", final_left, value_mix, preferred_element_type=jnp.float32
+        ).astype(jnp.bfloat16)
+        return from_dest(exchange(attended), place_count, heads_kv)
+    blocks, groups = final_left.shape[0], chunk // place_count
+    tiles = place_count // 8
     attended = jnp.einsum(
-        "alp,lpd->apd", final_left, value_mix, preferred_element_type=jnp.float32
+        "algbc,lgbcd->bagcd",
+        final_left.reshape(blocks, blocks, groups, tiles, 8),
+        value_mix.reshape(blocks, groups, tiles, 8, DH),
+        preferred_element_type=jnp.float32,
     ).astype(jnp.bfloat16)
-    return from_dest(exchange(attended), place_count, heads_kv)
+    back = lax.all_to_all(attended, "ctx", split_axis=1, concat_axis=1, tiled=True)
+    return jnp.transpose(back, (0, 3, 1, 2, 4)).reshape(place_count, feature_width)
 
 
 def make_local(ctx):

time: 62.3 us -> 60.4 us (0.970)
  matrix products: 8.36 us -> 6.81 us
    all_to_all x2 -> x1, blocking collectives: 45.6 us -> 27.4 us  [exchange(): return lax.all_to_all(grid, 'ctx', split_axis=0, concat_axis=0, tiled=True)]
    all_to_all x0 -> x1, blocking collectives: none -> 18.2 us  [one_sequence(): lax.all_to_all(attended, 'ctx', split_axis=1, concat_axis=1, tiled=True)]
    sub x2 -> x1, matrix products: 5.46 us -> 2.73 us  [left_step(): weights = jax.nn.softmax(logits, axis=1)]
    div x0 -> x1, matrix products: none -> 1.21 us  [left_step(): weights = jax.nn.softmax(logits, axis=1)]
where the time goes in v17:
time: 60.4 us; the launch traced here: 60.2 us
  blocking collectives  47.8 us (79%)
  matrix products  6.81 us (11%)
  Pallas kernels  2.15 us (4%)
  local copies, waits for them, and re-layouts  1.82 us (3%)
  other arithmetic  1.47 us (2%)
    all_to_all x1, blocking collectives, exchange(): return lax.all_to_all(grid, 'ctx', split_axis=0, concat_axis=0, tiled=True)  27.4 us
    all_to_all x1, blocking collectives, one_sequence(): lax.all_to_all(attended, 'ctx', split_axis=1, concat_axis=1, tiled=True)  18.2 us
    sub x1, matrix products, left_step(): weights = jax.nn.softmax(logits, axis=1)  2.73 us
    all_gather x1, blocking collectives, one_sequence(): lax.all_gather(rows[:, chunk:].reshape(ctx, 2, own_len, DH), 'head', axis...  2.18 us
    pallas_call x1, Pallas kernels, pack(): pl.pallas_call(pack_kernel, out_shape=jax.ShapeDtypeStruct((ctx, rows, DH...  2.15 us
    div x1, matrix products, left_step(): weights = jax.nn.softmax(logits, axis=1)  1.21 us

profile of v17, /device:TPU:0, one launch (start us, length us, event | category | flops | bytes accessed | tf_op | source)
XLA Modules:
  0.0 60.2 jit_solution(4677079214005551099)
XLA Ops:
  0.0 2.1 %shard_map.37 = bf16[8,384,128]{2,1,0:T(8,128)(2,1)} custom-call(bf16[64,4096]{1,0:T(8,128)(2,1)} %bitcast.44, bf16[64,1024]{1,0:T(8,128)(2,1)} %bitcast.47, bf16[64,1024]{1,0:T(8,128)(2,1)} %bitcast.48), custom_call_target="tpu_custom_call" | custom-call | tf_op jit(solution)/shard_map/pallas_call | solution.py:77
  2.1 27.4 %all_to_all.10 = bf16[8,384,128]{2,1,0:T(8,128)(2,1)S(1)} all-to-all(bf16[8,384,128]{2,1,0:T(8,128)(2,1)} %shard_map.37), channel_id=1, replica_groups=mesh['grp'=2,'ctx'=8,'head'=2] {'ctx'}, dimensions={0} | all-to-all | bytes 1572864 | tf_op jit(solution)/shard_map/all_to_all | solution.py:19
  29.6 2.2 %all_gather.3 = bf16[8,2,128,128]{3,2,0,1:T(8,128)(2,1)S(1)} all-gather(bf16[8,2,64,128]{3,2,0,1:T(8,128)(2,1)S(1)} %copy.21), channel_id=1, replica_groups=mesh['grp'=2,'ctx'=8,'head'=2] {'head'}, dimensions={2}, use_global_device_ids=true | all-gather | bytes 786432 | tf_op jit(solution)/shard_map/all_gather | solution.py:101
  31.8 0.3 fusion.36
  32.1 0.2 fusion.17
  32.3 0.4 convolution_convert_fusion.3
  32.6 0.4 exponential_reduce_fusion.1
  33.0 0.1 copy.25
  33.2 2.7 %fusion.37 = (f32[8,256]{0,1:T(8,128)S(1)}, f32[8,8,256]{0,1,2:T(8,128)S(1)}) fusion(bf16[8,256,128]{2,1,0:T(8,128)(2,1)S(1)} %convolution_convert_fusion.3, f32[8,256]{0,1:T(8,128)S(1)} %copy.25, bf16[8,256,128]{2,1,0:T(8,128)(2,1)S(1)} %slice.16), kind=kOutput, calls=%fused_computation.57 | convolution fusion | flops 4259847 | bytes 1130496 | tf_op jit(solution)/shard_map/sub | solution.py:27
  36.0 0.4 fusion.32
  36.3 0.6 fusion.14
  36.9 0.3 fusion.38
  37.3 0.2 fusion.19
  37.4 0.4 convolution_convert_fusion.1
  37.8 0.4 convolution_convert_fusion.2
  38.2 0.4 exponential_reduce_fusion
  38.6 0.1 copy.32
  38.7 1.2 %fusion.13 = bf16[8,8,256]{0,1,2:T(8,128)(2,1)S(1)} fusion(bf16[8,256,128]{2,1,0:T(8,128)(2,1)S(1)} %convolution_convert_fusion.1, f32[8,256]{0,1:T(8,128)S(1)} %copy.32, bf16[8,256,128]{2,1,0:T(8,128)(2,1)S(1)} %slice.16), kind=kOutput, calls=%fused_computation.18 | convolution fusion | flops 4280334 | bytes 1089536 | tf_op jit(solution)/shard_map/div | solution.py:27
  39.9 0.5 fusion.15
  40.5 0.1 copy.35
  40.6 18.2 %all_to_all.11 = bf16[8,8,4,8,128]{4,3,2,0,1:T(8,128)(2,1)S(1)} all-to-all(bf16[8,8,4,8,128]{4,3,2,0,1:T(8,128)(2,1)S(1)} %copy.35), channel_id=1, replica_groups=mesh['grp'=2,'ctx'=8,'head'=2] {'ctx'}, dimensions={1} | all-to-all | bytes 1048576 | tf_op jit(solution)/shard_map/all_to_all | solution.py:133
  58.7 0.2 copy.36
  59.0 1.2 %stack_reshape.3 = bf16[1,64,4096]{2,1,0:T(8,128)(2,1)} reshape(bf16[8,8,8,4,128]{4,3,2,1,0:T(4,128)(2,1)S(1)} %copy.36) | data formatting | bytes 1048576 | tf_op jit(solution)/shard_map/stack;reshape | solution.py:139
  (8 shorter events, 0.1 us)

commit v18 on v17

--- a/solution.py
+++ b/solution.py
@@ -125,13 +125,13 @@
     blocks, groups = final_left.shape[0], chunk // place_count
     tiles = place_count // 8
     attended = jnp.einsum(
-        "algbc,lgbcd->bagcd",
+        "algbc,lgbcd->bcagd",
         final_left.reshape(blocks, blocks, groups, tiles, 8),
         value_mix.reshape(blocks, groups, tiles, 8, DH),
         preferred_element_type=jnp.float32,
     ).astype(jnp.bfloat16)
-    back = lax.all_to_all(attended, "ctx", split_axis=1, concat_axis=1, tiled=True)
-    return jnp.transpose(back, (0, 3, 1, 2, 4)).reshape(place_count, feature_width)
+    back = lax.all_to_all(attended, "ctx", split_axis=2, concat_axis=2, tiled=True)
+    return back.reshape(place_count, feature_width)
 
 
 def make_local(ctx):

time: 60.4 us -> 60.5 us (level)
  no operation moved by 1% of the time
where the time goes in v18:
time: 60.5 us; the launch traced here: 60.3 us
  blocking collectives  47.8 us (79%)
  matrix products  6.82 us (11%)
  Pallas kernels  2.15 us (4%)
  local copies, waits for them, and re-layouts  1.9 us (3%)
  other arithmetic  1.47 us (2%)
    all_to_all x1, blocking collectives, exchange(): return lax.all_to_all(grid, 'ctx', split_axis=0, concat_axis=0, tiled=True)  27.4 us
    all_to_all x1, blocking collectives, one_sequence(): lax.all_to_all(attended, 'ctx', split_axis=2, concat_axis=2, tiled=True)  18.2 us
    sub x1, matrix products, left_step(): weights = jax.nn.softmax(logits, axis=1)  2.73 us
    all_gather x1, blocking collectives, one_sequence(): lax.all_gather(rows[:, chunk:].reshape(ctx, 2, own_len, DH), 'head', axis...  2.18 us
    pallas_call x1, Pallas kernels, pack(): pl.pallas_call(pack_kernel, out_shape=jax.ShapeDtypeStruct((ctx, rows, DH...  2.15 us
    div x1, matrix products, left_step(): weights = jax.nn.softmax(logits, axis=1)  1.21 us

profile of v18, /device:TPU:0, one launch (start us, length us, event | category | flops | bytes accessed | tf_op | source)
XLA Modules:
  0.0 60.3 jit_solution(11369618848026905448)
XLA Ops:
  0.0 2.1 %shard_map.37 = bf16[8,384,128]{2,1,0:T(8,128)(2,1)} custom-call(bf16[64,4096]{1,0:T(8,128)(2,1)} %bitcast.42, bf16[64,1024]{1,0:T(8,128)(2,1)} %bitcast.45, bf16[64,1024]{1,0:T(8,128)(2,1)} %bitcast.46), custom_call_target="tpu_custom_call" | custom-call | tf_op jit(solution)/shard_map/pallas_call | solution.py:77
  2.1 27.4 %all_to_all.10 = bf16[8,384,128]{2,1,0:T(8,128)(2,1)S(1)} all-to-all(bf16[8,384,128]{2,1,0:T(8,128)(2,1)} %shard_map.37), channel_id=1, replica_groups=mesh['grp'=2,'ctx'=8,'head'=2] {'ctx'}, dimensions={0} | all-to-all | bytes 1572864 | tf_op jit(solution)/shard_map/all_to_all | solution.py:19
  29.6 2.2 %all_gather.3 = bf16[8,2,128,128]{3,2,0,1:T(8,128)(2,1)S(1)} all-gather(bf16[8,2,64,128]{3,2,0,1:T(8,128)(2,1)S(1)} %copy.21), channel_id=1, replica_groups=mesh['grp'=2,'ctx'=8,'head'=2] {'head'}, dimensions={2}, use_global_device_ids=true | all-gather | bytes 786432 | tf_op jit(solution)/shard_map/all_gather | solution.py:101
  31.8 0.3 fusion.36
  32.1 0.2 fusion.17
  32.3 0.4 convolution_convert_fusion.3
  32.6 0.4 exponential_reduce_fusion.1
  33.0 0.1 copy.25
  33.2 2.7 %fusion.37 = (f32[8,256]{0,1:T(8,128)S(1)}, f32[8,8,256]{0,1,2:T(8,128)S(1)}) fusion(bf16[8,256,128]{2,1,0:T(8,128)(2,1)S(1)} %convolution_convert_fusion.3, f32[8,256]{0,1:T(8,128)S(1)} %copy.25, bf16[8,256,128]{2,1,0:T(8,128)(2,1)S(1)} %slice.16), kind=kOutput, calls=%fused_computation.57 | convolution fusion | flops 4259847 | bytes 1130496 | tf_op jit(solution)/shard_map/sub | solution.py:27
  36.0 0.4 fusion.32
  36.3 0.6 fusion.14
  36.9 0.3 fusion.38
  37.3 0.2 fusion.19
  37.4 0.4 convolution_convert_fusion.1
  37.8 0.4 convolution_convert_fusion.2
  38.2 0.4 exponential_reduce_fusion
  38.6 0.1 copy.32
  38.7 1.2 %fusion.13 = bf16[8,8,256]{0,1,2:T(8,128)(2,1)S(1)} fusion(bf16[8,256,128]{2,1,0:T(8,128)(2,1)S(1)} %convolution_convert_fusion.1, f32[8,256]{0,1:T(8,128)S(1)} %copy.32, bf16[8,256,128]{2,1,0:T(8,128)(2,1)S(1)} %slice.16), kind=kOutput, calls=%fused_computation.18 | convolution fusion | flops 4280334 | bytes 1089536 | tf_op jit(solution)/shard_map/div | solution.py:27
  39.9 0.5 fusion.15
  40.5 0.2 copy.35
  40.7 18.2 %all_to_all.11 = bf16[8,8,8,4,128]{4,3,1,0,2:T(4,128)(2,1)S(1)} all-to-all(bf16[8,8,8,4,128]{4,3,1,0,2:T(4,128)(2,1)S(1)} %copy.35), channel_id=1, replica_groups=mesh['grp'=2,'ctx'=8,'head'=2] {'ctx'}, dimensions={2} | all-to-all | bytes 1048576 | tf_op jit(solution)/shard_map/all_to_all | solution.py:133
  58.9 0.2 copy.36
  59.1 1.2 %stack_reshape.3 = bf16[1,64,4096]{2,1,0:T(8,128)(2,1)} reshape(bf16[8,8,8,4,128]{4,3,2,1,0:T(4,128)(2,1)S(1)} %copy.36) | data formatting | bytes 1048576 | tf_op jit(solution)/shard_map/stack;reshape | solution.py:139
  (8 shorter events, 0.1 us)

commit v19 on v17

--- a/solution.py
+++ b/solution.py
@@ -106,9 +106,18 @@
     _, entropy_grid, key_grid = right_step(query_grid, block_keys)
     weights, left_rounded = left_step(query_grid, key_grid, entropy_grid)
     column_mass = jnp.sum(weights, axis=0)
-    mixed = jnp.einsum(
-        "alp,apd->lpd", left_rounded, query_grid, preferred_element_type=jnp.float32
-    )
+    if ctx != heads_kv:
+        mixed = jnp.einsum(
+            "alp,apd->lpd", left_rounded, query_grid, preferred_element_type=jnp.float32
+        )
+    else:
+        blocks, groups = left_rounded.shape[0], chunk // place_count
+        mixed = jnp.einsum(
+            "algbc,agbcd->lgbcd",
+            left_rounded.reshape(blocks, blocks, groups, place_count // 8, 8),
+            query_grid.reshape(blocks, groups, place_count // 8, 8, DH),
+            preferred_element_type=jnp.float32,
+        ).reshape(blocks, chunk, DH)
     query_mix = (mixed / jnp.maximum(column_mass, 1.0)[..., None]).astype(jnp.bfloat16)
 
     rounded, entropy, key_mix = right_step(query_mix, block_keys)

time: 60.4 us -> 60.8 us (level)
  no operation moved by 1% of the time
where the time goes in v19:
time: 60.8 us; the launch traced here: 60.6 us
  blocking collectives  47.8 us (79%)
  matrix products  7.17 us (12%)
  Pallas kernels  2.15 us (4%)
  local copies, waits for them, and re-layouts  1.88 us (3%)
  other arithmetic  1.46 us (2%)
    all_to_all x1, blocking collectives, exchange(): return lax.all_to_all(grid, 'ctx', split_axis=0, concat_axis=0, tiled=True)  27.4 us
    all_to_all x1, blocking collectives, one_sequence(): lax.all_to_all(attended, 'ctx', split_axis=1, concat_axis=1, tiled=True)  18.2 us
    sub x1, matrix products, left_step(): weights = jax.nn.softmax(logits, axis=1)  2.73 us
    all_gather x1, blocking collectives, one_sequence(): lax.all_gather(rows[:, chunk:].reshape(ctx, 2, own_len, DH), 'head', axis...  2.18 us
    pallas_call x1, Pallas kernels, pack(): pl.pallas_call(pack_kernel, out_shape=jax.ShapeDtypeStruct((ctx, rows, DH...  2.15 us

profile of v19, /device:TPU:0, one launch (start us, length us, event | category | flops | bytes accessed | tf_op | source)
XLA Modules:
  0.0 60.6 jit_solution(11644370287243488577)
XLA Ops:
  0.0 2.1 %shard_map.37 = bf16[8,384,128]{2,1,0:T(8,128)(2,1)} custom-call(bf16[64,4096]{1,0:T(8,128)(2,1)} %bitcast.47, bf16[64,1024]{1,0:T(8,128)(2,1)} %bitcast.50, bf16[64,1024]{1,0:T(8,128)(2,1)} %bitcast.51), custom_call_target="tpu_custom_call" | custom-call | tf_op jit(solution)/shard_map/pallas_call | solution.py:77
  2.1 27.4 %all_to_all.10 = bf16[8,384,128]{2,1,0:T(8,128)(2,1)S(1)} all-to-all(bf16[8,384,128]{2,1,0:T(8,128)(2,1)} %shard_map.37), channel_id=1, replica_groups=mesh['grp'=2,'ctx'=8,'head'=2] {'ctx'}, dimensions={0} | all-to-all | bytes 1572864 | tf_op jit(solution)/shard_map/all_to_all | solution.py:19
  29.6 2.2 %all_gather.3 = bf16[8,2,128,128]{3,2,0,1:T(8,128)(2,1)S(1)} all-gather(bf16[8,2,64,128]{3,2,0,1:T(8,128)(2,1)S(1)} %copy.42), channel_id=1, replica_groups=mesh['grp'=2,'ctx'=8,'head'=2] {'head'}, dimensions={2}, use_global_device_ids=true | all-gather | bytes 786432 | tf_op jit(solution)/shard_map/all_gather | solution.py:101
  31.8 0.3 fusion.37
  32.1 0.2 fusion.16
  32.3 0.4 convolution_convert_fusion.3
  32.6 0.4 exponential_reduce_fusion.1
  33.0 0.1 copy.46
  33.2 2.7 %fusion.38 = (f32[8,256]{0,1:T(8,128)S(1)}, f32[8,8,256]{0,1,2:T(8,128)S(1)}) fusion(bf16[8,256,128]{2,1,0:T(8,128)(2,1)S(1)} %convolution_convert_fusion.3, f32[8,256]{0,1:T(8,128)S(1)} %copy.46, bf16[8,256,128]{2,1,0:T(8,128)(2,1)S(1)} %slice.16), kind=kOutput, calls=%fused_computation.57 | convolution fusion | flops 4259847 | bytes 1130496 | tf_op jit(solution)/shard_map/sub | solution.py:27
  36.0 0.4 fusion.32
  36.3 0.1 copy.48
  36.4 0.5 fusion.25
  36.9 0.8 %fusion.39 = (f32[8,256]{1,0:T(8,128)S(1)}, f32[8,256,128]{1,2,0:T(8,128)S(1)}) fusion(bf16[8,2,128,128]{3,2,0,1:T(8,128)(2,1)S(1)} %all_gather.3, f32[8,256,128]{2,0,1:T(8,128)S(1)} %bitcast.45, f32[8,256]{1,0:T(8,128)S(1)} %broadcast_maximum_fusion), kind=kOutput, calls=%fused_computation.58 | convolution fusion | flops 68155392 | bytes 2375680 | tf_op jit(solution)/shard_map/lpd,lid->lpi/dot_general | solution.py:83
  37.7 0.2 fusion.18
  37.9 0.4 convolution_convert_fusion.1
  38.2 0.4 convolution_convert_fusion.2
  38.6 0.4 exponential_reduce_fusion
  39.0 0.1 copy.54
  39.1 1.2 %fusion.12 = bf16[8,8,256]{0,1,2:T(8,128)(2,1)S(1)} fusion(bf16[8,256,128]{2,1,0:T(8,128)(2,1)S(1)} %convolution_convert_fusion.1, f32[8,256]{0,1:T(8,128)S(1)} %copy.54, bf16[8,256,128]{2,1,0:T(8,128)(2,1)S(1)} %slice.16), kind=kOutput, calls=%fused_computation.16 | convolution fusion | flops 4280334 | bytes 1089536 | tf_op jit(solution)/shard_map/div | solution.py:27
  40.4 0.5 fusion.13
  40.9 0.1 copy.57
  41.0 18.2 %all_to_all.11 = bf16[8,8,4,8,128]{4,3,2,0,1:T(8,128)(2,1)S(1)} all-to-all(bf16[8,8,4,8,128]{4,3,2,0,1:T(8,128)(2,1)S(1)} %copy.57), channel_id=1, replica_groups=mesh['grp'=2,'ctx'=8,'head'=2] {'ctx'}, dimensions={1} | all-to-all | bytes 1048576 | tf_op jit(solution)/shard_map/all_to_all | solution.py:142
  59.2 0.2 copy.58
  59.4 1.2 %stack_reshape.3 = bf16[1,64,4096]{2,1,0:T(8,128)(2,1)} reshape(bf16[8,8,8,4,128]{4,3,2,1,0:T(4,128)(2,1)S(1)} %copy.58) | data formatting | bytes 1048576 | tf_op jit(solution)/shard_map/stack;reshape | solution.py:148
  (8 shorter events, 0.1 us)

commit v20 on v17

--- a/solution.py
+++ b/solution.py
@@ -20,10 +20,19 @@
 
 
 def left_step(query_grid, key_grid, entropy_grid):
-    logits = jnp.einsum(
-        "apd,lpd->alp", query_grid, key_grid, preferred_element_type=jnp.float32
-    ) / math.sqrt(DH)
-    logits = logits + entropy_grid[None]
+    blocks, pairs, _ = query_grid.shape
+    if pairs % 32:
+        logits = jnp.einsum(
+            "apd,lpd->alp", query_grid, key_grid, preferred_element_type=jnp.float32
+        )
+    else:
+        logits = jnp.einsum(
+            "agbcd,lgbcd->algbc",
+            query_grid.reshape(blocks, 4, -1, 8, DH),
+            key_grid.reshape(blocks, 4, -1, 8, DH),
+            preferred_element_type=jnp.float32,
+        ).reshape(blocks, blocks, pairs)
+    logits = logits / math.sqrt(DH) + entropy_grid[None]
     weights = jax.nn.softmax(logits, axis=1)
     return weights, weights.astype(jnp.bfloat16)
 

time: 60.4 us -> 62.2 us (1.030)
  local copies, waits for them, and re-layouts: 1.82 us -> 3.16 us
  other arithmetic: 1.47 us -> 2.77 us
  matrix products: 6.81 us -> 5.86 us
    sub x1, matrix products: 2.73 us -> 1.25 us  [left_step(): weights = jax.nn.softmax(logits, axis=1)]
    div x1 -> x0, matrix products: 1.21 us -> none  [left_step(): weights = jax.nn.softmax(logits, axis=1)]
    dot_general x0 -> x1, matrix products: none -> 0.95 us  [left_step(): jnp.einsum('agbcd,lgbcd->algbc', query_grid.reshape(blocks, 4, -1, 8, DH)...]
    dot_general x2, matrix products: 0.75 us -> 1.54 us  [right_step(): jnp.einsum('lpi,lid->lpd', rounded, block_keys, preferred_element_type=jn...]
    unnamed x0 -> x2, local copies, waits for them, and re-layouts: none -> 0.73 us
where the time goes in v20:
time: 62.2 us; the launch traced here: 61.9 us
  blocking collectives  47.8 us (77%)
  matrix products  5.86 us (9%)
  local copies, waits for them, and re-layouts  3.16 us (5%)
  other arithmetic  2.77 us (4%)
  Pallas kernels  2.15 us (3%)
    all_to_all x1, blocking collectives, exchange(): return lax.all_to_all(grid, 'ctx', split_axis=0, concat_axis=0, tiled=True)  27.4 us
    all_to_all x1, blocking collectives, one_sequence(): lax.all_to_all(attended, 'ctx', split_axis=1, concat_axis=1, tiled=True)  18.2 us
    all_gather x1, blocking collectives, one_sequence(): lax.all_gather(rows[:, chunk:].reshape(ctx, 2, own_len, DH), 'head', axis...  2.18 us
    pallas_call x1, Pallas kernels, pack(): pl.pallas_call(pack_kernel, out_shape=jax.ShapeDtypeStruct((ctx, rows, DH...  2.15 us
    dot_general x2, matrix products, right_step(): jnp.einsum('lpi,lid->lpd', rounded, block_keys, preferred_element_type=jn...  1.54 us
    sub x1, matrix products, left_step(): weights = jax.nn.softmax(logits, axis=1)  1.25 us

profile of v20, /device:TPU:0, one launch (start us, length us, event | category | flops | bytes accessed | tf_op | source)
XLA Modules:
  0.0 61.9 jit_solution(11174954457112527142)
XLA Ops:
  0.0 2.1 %shard_map.37 = bf16[8,384,128]{2,1,0:T(8,128)(2,1)} custom-call(bf16[64,4096]{1,0:T(8,128)(2,1)} %bitcast.71, bf16[64,1024]{1,0:T(8,128)(2,1)} %bitcast.80, bf16[64,1024]{1,0:T(8,128)(2,1)} %bitcast.81), custom_call_target="tpu_custom_call" | custom-call | tf_op jit(solution)/shard_map/pallas_call | solution.py:86
  2.1 27.4 %all_to_all.10 = bf16[8,384,128]{2,1,0:T(8,128)(2,1)S(1)} all-to-all(bf16[8,384,128]{2,1,0:T(8,128)(2,1)} %shard_map.37), channel_id=1, replica_groups=mesh['grp'=2,'ctx'=8,'head'=2] {'ctx'}, dimensions={0} | all-to-all | bytes 1572864 | tf_op jit(solution)/shard_map/all_to_all | solution.py:19
  29.6 2.2 %all_gather.3 = bf16[8,2,128,128]{3,2,0,1:T(8,128)(2,1)S(1)} all-gather(bf16[8,2,64,128]{3,2,0,1:T(8,128)(2,1)S(1)} %copy.39), channel_id=1, replica_groups=mesh['grp'=2,'ctx'=8,'head'=2] {'head'}, dimensions={2}, use_global_device_ids=true | all-gather | bytes 786432 | tf_op jit(solution)/shard_map/all_gather | solution.py:110
  31.8 0.3 fusion.36
  32.1 0.1 copy.71
  32.2 0.2 fusion.14
  32.4 0.4 convolution_convert_fusion.3
  32.8 0.4 exponential_reduce_fusion.1
  33.2 0.1 copy.67
  33.3 0.1 copy.66
  33.4 0.1 copy.43
  33.6 1.0 %fusion.12 = (f32[8,4,8,8]{0,3,2,1:T(8,128)S(1)}, f32[4,8,8,8,8]{4,3,2,1,0:T(8,128)S(1)}) fusion(f32[8,4,8,8]{0,3,2,1:T(8,128)S(1)} %fusion.30, bf16[8,4,8,8,128]{4,3,2,1,0:T(8,128)(2,1)S(1)} %bitcast.72, bf16[8,4,8,8,128]{4,3,2,1,0:T(8,128)(2,1)S(1)} %bitcast.84), kind=kOutput, calls=%fused_computation.32 | convolution fusion | flops 4241408 | bytes 1130496 | tf_op jit(solution)/shard_map/agbcd,lgbcd->algbc/dot_general | solution.py:29
  34.6 0.5 fusion.17
  35.1 0.7 %divide_reduce_fusion = f32[8,4,8,8]{0,3,2,1:T(8,128)S(1)} fusion(f32[4,8,8,8,8]{4,3,2,1,0:T(8,128)S(1)} %get-tuple-element.14, f32[8,4,8,8]{0,3,2,1:T(8,128)S(1)} %fusion.17, f32[8,4,8,8]{0,3,2,1:T(8,128)S(1)} %get-tuple-element.13, f32[8,4,8,8]{0,3,2,1:T(8,128)S(1)} %fusion.30), kind=kLoop, calls=%fused_computation.31 | loop fusion | flops 63488 | bytes 98304 | tf_op jit(solution)/shard_map/reduce_sum | solution.py:117
  35.9 0.4 fusion.11
  36.2 0.6 fusion.6
  36.8 0.3 fusion.37
  37.1 0.2 fusion.16
  37.3 0.4 convolution_convert_fusion.2
  37.7 1.2 %convolution_convert_fusion.1 = bf16[8,256,128]{2,1,0:T(8,128)(2,1)} fusion(bf16[8,2,128,128]{3,2,0,1:T(8,128)(2,1)S(1)} %all_gather.3, f32[8,256,128]{1,2,0:T(8,128)S(1)} %get-tuple-element.16, f32[8,256]{1,0:T(8,128)S(1)} %fusion.16, f32[8,256]{1,0:T(8,128)S(1)} %get-tuple-element.15), kind=kOutput, calls=%fused_computation.12 | convolution fusion | flops 68157440 | bytes 1851392 | tf_op jit(solution)/shard_map/lpi,lid->lpd/dot_general | solution.py:97
  38.9 0.1 copy.72
  39.0 0.4 exponential_reduce_fusion
  39.4 0.0 copy-start
  39.4 0.1 copy.69
  39.5 0.1 copy.68
  39.7 0.7 %copy-done = bf16[8,256,128]{2,1,0:T(8,128)(2,1)S(1)} copy-done((bf16[8,256,128]{2,1,0:T(8,128)(2,1)S(1)}, bf16[8,256,128]{2,1,0:T(8,128)(2,1)}, u32[]{:S(2)}) %copy-start) | copy-done | bytes 524312
  40.4 1.3 %fusion.38 = (f32[8,4,8,8]{0,3,2,1:T(8,128)S(1)}, f32[8,8,4,8,8]{0,1,4,3,2:T(8,128)S(1)}) fusion(bf16[8,4,8,8,128]{4,3,2,1,0:T(8,128)(2,1)S(1)} %bitcast.85, f32[8,4,8,8]{0,3,2,1:T(8,128)S(1)} %fusion.32, bf16[8,4,8,8,128]{4,3,2,1,0:T(8,128)(2,1)S(1)} %bitcast.73), kind=kOutput, calls=%fused_computation.65 | convolution fusion | flops 4259847 | bytes 1130496 | tf_op jit(solution)/shard_map/sub | solution.py:36
  41.7 0.6 fusion.7
  42.2 0.1 copy.60
  42.3 18.2 %all_to_all.11 = bf16[8,8,4,8,128]{4,3,2,0,1:T(8,128)(2,1)S(1)} all-to-all(bf16[8,8,4,8,128]{4,3,2,0,1:T(8,128)(2,1)S(1)} %copy.60), channel_id=1, replica_groups=mesh['grp'=2,'ctx'=8,'head'=2] {'ctx'}, dimensions={1} | all-to-all | bytes 1048576 | tf_op jit(solution)/shard_map/all_to_all | solution.py:142
  60.5 0.2 copy.61
  60.8 1.2 %stack_reshape.3 = bf16[1,64,4096]{2,1,0:T(8,128)(2,1)} reshape(bf16[8,8,8,4,128]{4,3,2,1,0:T(4,128)(2,1)S(1)} %copy.61) | data formatting | bytes 1048576 | tf_op jit(solution)/shard_map/stack;reshape | solution.py:148
  (10 shorter events, 0.2 us)
Async XLA Ops:
  39.4 1.0 %copy-start = (bf16[8,256,128]{2,1,0:T(8,128)(2,1)S(1)}, bf16[8,256,128]{2,1,0:T(8,128)(2,1)}, u32[]{:S(2)}) copy-start(bf16[8,256,128]{2,1,0:T(8,128)(2,1)} %convolution_convert_fusion.1) | copy-start | bytes 1572868

commit v21 on v17

--- a/solution.py
+++ b/solution.py
@@ -111,10 +111,15 @@
     )
     query_mix = (mixed / jnp.maximum(column_mass, 1.0)[..., None]).astype(jnp.bfloat16)
 
-    rounded, entropy, key_mix = right_step(query_mix, block_keys)
-    value_mix = jnp.einsum(
-        "lpi,lid->lpd", rounded, block_values, preferred_element_type=jnp.float32
+    logits = jnp.einsum(
+        "lpd,lid->lpi", query_mix, block_keys, preferred_element_type=jnp.float32
+    ) / math.sqrt(DH)
+    weights, entropy = softmax_terms(logits)
+    both = jnp.concatenate([block_keys, block_values], axis=2)
+    mixes = jnp.einsum(
+        "lpi,lid->lpd", weights.astype(jnp.bfloat16), both, preferred_element_type=jnp.float32
     ).astype(jnp.bfloat16)
+    key_mix, value_mix = mixes[:, :, :DH], mixes[:, :, DH:]
 
     _, final_left = left_step(query_grid, key_mix, entropy)
     if ctx != heads_kv:

time: 60.4 us -> 60.5 us (level)
  no operation moved by 1% of the time
where the time goes in v21:
time: 60.5 us; the launch traced here: 60.2 us
  blocking collectives  47.8 us (79%)
  matrix products  6.57 us (11%)
  Pallas kernels  2.15 us (4%)
  local copies, waits for them, and re-layouts  2.12 us (4%)
  other arithmetic  1.47 us (2%)
    all_to_all x1, blocking collectives, exchange(): return lax.all_to_all(grid, 'ctx', split_axis=0, concat_axis=0, tiled=True)  27.4 us
    all_to_all x1, blocking collectives, one_sequence(): lax.all_to_all(attended, 'ctx', split_axis=1, concat_axis=1, tiled=True)  18.2 us
    sub x1, matrix products, left_step(): weights = jax.nn.softmax(logits, axis=1)  2.73 us
    all_gather x1, blocking collectives, one_sequence(): lax.all_gather(rows[:, chunk:].reshape(ctx, 2, own_len, DH), 'head', axis...  2.18 us
    pallas_call x1, Pallas kernels, pack(): pl.pallas_call(pack_kernel, out_shape=jax.ShapeDtypeStruct((ctx, rows, DH...  2.15 us
    div x1, matrix products, left_step(): weights = jax.nn.softmax(logits, axis=1)  1.21 us

profile of v21, /device:TPU:0, one launch (start us, length us, event | category | flops | bytes accessed | tf_op | source)
XLA Modules:
  0.0 60.2 jit_solution(17341347151674776663)
XLA Ops:
  0.0 2.1 %shard_map.37 = bf16[8,384,128]{2,1,0:T(8,128)(2,1)} custom-call(bf16[64,4096]{1,0:T(8,128)(2,1)} %bitcast.43, bf16[64,1024]{1,0:T(8,128)(2,1)} %bitcast.45, bf16[64,1024]{1,0:T(8,128)(2,1)} %bitcast.46), custom_call_target="tpu_custom_call" | custom-call | tf_op jit(solution)/shard_map/pallas_call | solution.py:77
  2.1 27.4 %all_to_all.10 = bf16[8,384,128]{2,1,0:T(8,128)(2,1)S(1)} all-to-all(bf16[8,384,128]{2,1,0:T(8,128)(2,1)} %shard_map.37), channel_id=1, replica_groups=mesh['grp'=2,'ctx'=8,'head'=2] {'ctx'}, dimensions={0} | all-to-all | bytes 1572864 | tf_op jit(solution)/shard_map/all_to_all | solution.py:19
  29.6 2.2 %all_gather.3 = bf16[8,2,128,128]{3,2,0,1:T(8,128)(2,1)S(1)} all-gather(bf16[8,2,64,128]{3,2,0,1:T(8,128)(2,1)S(1)} %copy.23), channel_id=1, replica_groups=mesh['grp'=2,'ctx'=8,'head'=2] {'head'}, dimensions={2}, use_global_device_ids=true | all-gather | bytes 786432 | tf_op jit(solution)/shard_map/all_gather | solution.py:101
  31.8 0.3 fusion.42
  32.1 0.2 fusion.17
  32.3 0.4 convolution_convert_fusion.2
  32.7 0.4 exponential_reduce_fusion.1
  33.1 0.1 copy.27
  33.3 2.7 %fusion.43 = (f32[8,256]{0,1:T(8,128)S(1)}, f32[8,8,256]{0,1,2:T(8,128)S(1)}) fusion(bf16[8,256,128]{2,1,0:T(8,128)(2,1)S(1)} %convolution_convert_fusion.2, f32[8,256]{0,1:T(8,128)S(1)} %copy.27, bf16[8,256,128]{2,1,0:T(8,128)(2,1)S(1)} %slice.24), kind=kOutput, calls=%fused_computation.63 | convolution fusion | flops 4259847 | bytes 1130496 | tf_op jit(solution)/shard_map/sub | solution.py:27
  36.0 0.4 fusion.38
  36.4 0.6 %fusion.14 = bf16[8,256,128]{2,0,1:T(8,128)(2,1)S(1)} fusion(f32[8,256]{0,1:T(8,128)S(1)} %broadcast_maximum_fusion, bf16[8,256,128]{2,1,0:T(8,128)(2,1)S(1)} %slice.24, f32[8,8,256]{0,1,2:T(8,128)S(1)} %get-tuple-element.16, f32[8,256]{0,1:T(8,128)S(1)} %get-tuple-element.15), kind=kOutput, calls=%fused_computation.22 | convolution fusion | flops 4751360 | bytes 1130496 | tf_op jit(solution)/shard_map/alp,apd->lpd/dot_general | solution.py:109
  37.0 0.3 fusion.44
  37.3 0.2 fusion.19
  37.5 0.4 exponential_reduce_fusion
  37.9 0.5 convolution_convert_fusion
  38.4 0.3 fusion.41
  38.7 0.1 copy.33
  38.8 1.2 %fusion.13 = bf16[8,8,256]{0,1,2:T(8,128)(2,1)S(1)} fusion(bf16[8,256,128]{2,1,0:T(8,128)(2,1)S(1)} %get-tuple-element.10, f32[8,256]{0,1:T(8,128)S(1)} %copy.33, bf16[8,256,128]{2,1,0:T(8,128)(2,1)S(1)} %slice.24), kind=kOutput, calls=%fused_computation.19 | convolution fusion | flops 4280334 | bytes 1089536 | tf_op jit(solution)/shard_map/div | solution.py:27
  40.0 0.5 fusion.15
  40.5 0.1 copy.36
  40.6 18.2 %all_to_all.11 = bf16[8,8,4,8,128]{4,3,2,0,1:T(8,128)(2,1)S(1)} all-to-all(bf16[8,8,4,8,128]{4,3,2,0,1:T(8,128)(2,1)S(1)} %copy.36), channel_id=1, replica_groups=mesh['grp'=2,'ctx'=8,'head'=2] {'ctx'}, dimensions={1} | all-to-all | bytes 1048576 | tf_op jit(solution)/shard_map/all_to_all | solution.py:138
  58.8 0.2 copy.37
  59.1 1.2 %stack_reshape.3 = bf16[1,64,4096]{2,1,0:T(8,128)(2,1)} reshape(bf16[8,8,8,4,128]{4,3,2,1,0:T(4,128)(2,1)S(1)} %copy.37) | data formatting | bytes 1048576 | tf_op jit(solution)/shard_map/stack;reshape | solution.py:144
  (9 shorter events, 0.2 us)
